TPU v7x, 32 devices: a whole 2x2x4 slice. The times are simulated.
32 devices in a mesh: fsdp: 8 (over z, y), dp: 4 (over x, core).
Axes of the slice: x: 2, y: 2, z: 4, core: 2. Of those that a mesh axis runs over, the one named last changes fastest.
Arguments:
- tokens: bfloat16 [32768, 768], P(('fsdp', 'dp')), may hold values from -6 to 6
- image_table: int32 [160, 3], P(('fsdp', 'dp')), may hold values from 0 to 996, as said below
- ln1_gain: bfloat16 [768], P('fsdp'), may hold values from 0.5 to 1.5
- ln1_bias: bfloat16 [768], P('fsdp'), may hold values from -3 to 3
- qkv_weight: bfloat16 [768, 2304], P('fsdp'), may hold values from -0.21875 to 0.21875
- qkv_bias: bfloat16 [2304], P('fsdp'), may hold values from -2 to 2
- out_weight: bfloat16 [768, 768], P('fsdp'), may hold values from -0.875 to 0.875
- out_bias: bfloat16 [768], P('fsdp'), may hold values from -2 to 2
- ln2_gain: bfloat16 [768], P('fsdp'), may hold values from 0.5 to 1.5
- ln2_bias: bfloat16 [768], P('fsdp'), may hold values from -3 to 3
- fc1_weight: bfloat16 [768, 3072], P('fsdp'), may hold values from -0.21875 to 0.21875
- fc1_bias: bfloat16 [3072], P('fsdp'), may hold values from -3 to 3
- fc2_weight: bfloat16 [3072, 768], P('fsdp'), may hold values from -0.109375 to 0.109375
- fc2_bias: bfloat16 [768], P('fsdp'), may hold values from -2 to 2
- frequencies: bfloat16 [768], P('fsdp'), may hold values from -0.796875 to 0.796875
- cotangent: bfloat16 [32768, 768], P(('fsdp', 'dp')), may hold values from -6 to 6
Outputs:
- block_out: bfloat16 [32768, 768], P(('fsdp', 'dp'))
- tokens_grad: bfloat16 [32768, 768], P(('fsdp', 'dp'))
- first_norm_gain_gradient: float32 [768], P('fsdp')
- ln1_bias_grad: float32 [768], P('fsdp')
- qkv_weight_grad: float32 [768, 2304], P('fsdp')
- qkv_bias_grad: float32 [2304], P('fsdp')
- out_weight_grad: float32 [768, 768], P('fsdp')
- out_bias_grad: float32 [768], P('fsdp')
- second_norm_gain_gradient: float32 [768], P('fsdp')
- ln2_bias_grad: float32 [768], P('fsdp')
- fc1_weight_grad: float32 [768, 3072], P('fsdp')
- fc1_bias_grad: float32 [3072], P('fsdp')
- fc2_weight_grad: float32 [3072, 768], P('fsdp')
- fc2_bias_grad: float32 [768], P('fsdp')
- frequencies_grad: float32 [768], P('fsdp')
- freq_grad_norm: float32 [], replicated
- other_grad_norm: float32 [], replicated
Inputs may be any that keep to these rules, and one draw needn't show every extreme that they name: `image_table`: rows 5b to 5b+4 describe bin b: either a 24x24 and a 20x20 image, or 24x24 and two 14x14, or two 20x20 and one 14x14, or one 20x20 and three 14x14, or five 14x14, laid end to end from offset 0 in the listed order; unused rows have height and width 0 and the offset where the used rows end. Grids are square.
All inputs are finite; a program needn't handle non-finite values.
Results may differ from a plain program's by a relative error of at most 0.015.
Values may be sent and summed in bfloat16 or wider, within the bound.
No kernel may reach another device: no remote copies, remote signals or barrier semaphores. Data moves between devices by JAX's collectives and lax.ppermute only.
A program may use at most 192 MiB of HBM per device.

v0:
```python
import jax
import jax.numpy as jnp
from jax import lax
from jax.sharding import PartitionSpec as P

H = 12
HD = 64
BIN = 1024


norm_eps = 1e-06
masked_score = -1e30
inv_sqrt_two_pi = 0.3989422804014327


def matmul(left, right):
    return jnp.dot(left, right, preferred_element_type=jnp.float32)


def matmul_left_t(left, right):
    return lax.dot_general(
        left, right, (((0,), (0,)), ((), ())), preferred_element_type=jnp.float32
    )


def matmul_right_t(left, right):
    return lax.dot_general(
        left, right, (((1,), (1,)), ((), ())), preferred_element_type=jnp.float32
    )


def image_layout(image_table, bin_count, bin_rows):
    slot_count = image_table.shape[0] // bin_count
    table = image_table.reshape(bin_count, slot_count, 3)
    offset = table[:, :, 0:1]
    height = table[:, :, 1:2]
    width = table[:, :, 2:3]
    place = jnp.arange(bin_rows, dtype=jnp.int32)[None, None, :]
    inside = ((place >= offset) & (place < offset + height * width)).astype(jnp.int32)
    live = jnp.sum(inside, axis=1)
    slot_ids = jnp.arange(slot_count, dtype=jnp.int32)[None, :, None]
    segment = jnp.sum(inside * slot_ids, axis=1) + slot_count * (1 - live)
    local_place = place[:, 0, :] - jnp.sum(inside * offset, axis=1)
    grid_width = jnp.maximum(jnp.sum(inside * width, axis=1), 1)
    grid_row = local_place // grid_width * live
    grid_col = local_place % grid_width * live
    return (
        segment,
        grid_row.reshape(-1).astype(jnp.float32),
        grid_col.reshape(-1).astype(jnp.float32),
    )


def rotary_tables(frequencies, grid_row, grid_col):
    half_width = frequencies.shape[0] // 2
    freq_float = frequencies.astype(jnp.float32)
    freq_row = freq_float[:half_width].reshape(H, HD // 2)
    freq_col = freq_float[half_width:].reshape(H, HD // 2)
    theta = grid_row[:, None, None] * freq_row[None] + grid_col[:, None, None] * freq_col[None]
    return (jnp.cos(theta), jnp.sin(theta))


def rotate(heads, cosine, sine):
    half_width = heads.shape[-1] // 2
    first = heads[..., :half_width]
    second = heads[..., half_width:]
    return jnp.concatenate(
        [first * cosine - second * sine, first * sine + second * cosine], axis=-1
    )


def layer_norm_forward(values):
    center = values - jnp.mean(values, axis=-1, keepdims=True)
    inverse_deviation = lax.rsqrt(jnp.mean(center * center, axis=-1, keepdims=True) + norm_eps)
    return (center * inverse_deviation, inverse_deviation)


def layer_norm_backward(
    gradient_norm_total, centered_normalized, inverse_deviation, norm_gain_vector
):
    gain_scaled_output = gradient_norm_total * norm_gain_vector
    return inverse_deviation * (
        gain_scaled_output
        - jnp.mean(gain_scaled_output, axis=-1, keepdims=True)
        - centered_normalized
        * jnp.mean(gain_scaled_output * centered_normalized, axis=-1, keepdims=True)
    )


def gelu_slope(values):
    return (
        0.5 * (1.0 + lax.erf(values * 0.7071067811865476))
        + values * jnp.exp(-0.5 * values * values) * inv_sqrt_two_pi
    )


def join_heads(stacked):
    return jnp.transpose(stacked, (1, 0, 2)).reshape(stacked.shape[1], H * HD)


def head_slice(matrix, head_index):
    return lax.dynamic_slice_in_dim(matrix, head_index * HD, HD, 1)


def attend_bin(packed):
    query, key_rows, value, segment = packed
    mask = segment[:, None] == segment[None, :]
    scale = HD ** (-0.5)

    def one_head(head_index):
        q_head = head_slice(query, head_index)
        k_head = head_slice(key_rows, head_index)
        v_head = head_slice(value, head_index)
        scores = jnp.where(mask, matmul_right_t(q_head, k_head) * scale, masked_score)
        top = jnp.max(scores, axis=-1, keepdims=True)
        log_total = top + jnp.log(jnp.sum(jnp.exp(scores - top), axis=-1, keepdims=True))
        probs = jnp.exp(scores - log_total).astype(jnp.bfloat16)
        return (matmul(probs, v_head).astype(jnp.bfloat16), log_total[:, 0])

    mixed, log_total = lax.map(one_head, jnp.arange(H, dtype=jnp.int32))
    return (join_heads(mixed), log_total)


def attend_bin_back(packed):
    query, key_rows, value, d_mixed, log_total, segment = packed
    mask = segment[:, None] == segment[None, :]
    scale = HD ** (-0.5)

    def one_head(head_index):
        q_head = head_slice(query, head_index)
        k_head = head_slice(key_rows, head_index)
        v_head = head_slice(value, head_index)
        d_head = head_slice(d_mixed, head_index)
        total_head = lax.dynamic_index_in_dim(log_total, head_index, 0, keepdims=False)
        scores = jnp.where(mask, matmul_right_t(q_head, k_head) * scale, masked_score)
        probs = jnp.exp(scores - total_head[:, None])
        d_probs = matmul_right_t(d_head, v_head)
        d_value = matmul_left_t(probs.astype(jnp.bfloat16), d_head)
        inner = jnp.sum(probs * d_probs, axis=-1, keepdims=True)
        d_scores = (probs * (d_probs - inner)).astype(jnp.bfloat16)
        d_query = matmul(d_scores, k_head) * scale
        d_key = matmul_left_t(d_scores, q_head) * scale
        return (d_query, d_key, d_value)

    d_query, d_key, d_value = lax.map(one_head, jnp.arange(H, dtype=jnp.int32))
    return (join_heads(d_query), join_heads(d_key), join_heads(d_value))


def square_sums(pieces):
    freq_sq = jnp.sum(pieces[12] * pieces[12])
    other_sq = jnp.float32(0.0)
    for member in pieces[:12]:
        other_sq = other_sq + jnp.sum(member * member)
    return (freq_sq, other_sq)


def shards(
    tokens,
    image_table,
    ln1_gain,
    ln1_bias,
    qkv_weight,
    qkv_bias,
    out_weight,
    out_bias,
    ln2_gain,
    ln2_bias,
    fc1_weight,
    fc1_bias,
    fc2_weight,
    fc2_bias,
    frequencies,
    cotangent,
):
    block_parameters = (
        lax.all_gather(ln1_gain, "fsdp", axis=0, tiled=True),
        lax.all_gather(ln1_bias, "fsdp", axis=0, tiled=True),
        lax.all_gather(qkv_weight, "fsdp", axis=0, tiled=True),
        lax.all_gather(qkv_bias, "fsdp", axis=0, tiled=True),
        lax.all_gather(out_weight, "fsdp", axis=0, tiled=True),
        lax.all_gather(out_bias, "fsdp", axis=0, tiled=True),
        lax.all_gather(ln2_gain, "fsdp", axis=0, tiled=True),
        lax.all_gather(ln2_bias, "fsdp", axis=0, tiled=True),
        lax.all_gather(fc1_weight, "fsdp", axis=0, tiled=True),
        lax.all_gather(fc1_bias, "fsdp", axis=0, tiled=True),
        lax.all_gather(fc2_weight, "fsdp", axis=0, tiled=True),
        lax.all_gather(fc2_bias, "fsdp", axis=0, tiled=True),
        lax.all_gather(frequencies, "fsdp", axis=0, tiled=True),
    )
    row_count, width = tokens.shape
    bin_count = row_count // BIN
    half_head = HD // 2
    segment, grid_row, grid_col = image_layout(image_table, bin_count, BIN)
    cosine, sine = rotary_tables(block_parameters[12], grid_row, grid_col)
    input_single_precision = tokens.astype(jnp.float32)
    first_centered_normalized, first_inverse_deviation = layer_norm_forward(input_single_precision)
    first_activation = (
        first_centered_normalized * block_parameters[0].astype(jnp.float32)
        + block_parameters[1].astype(jnp.float32)
    ).astype(jnp.bfloat16)
    qkv_full = matmul(first_activation, block_parameters[2]) + block_parameters[3].astype(
        jnp.float32
    )
    q_rot = rotate(qkv_full[:, :width].reshape(row_count, H, HD), cosine, sine)
    k_rot = rotate(qkv_full[:, width : 2 * width].reshape(row_count, H, HD), cosine, sine)
    q_low = q_rot.reshape(row_count, width).astype(jnp.bfloat16)
    k_low = k_rot.reshape(row_count, width).astype(jnp.bfloat16)
    v_low = qkv_full[:, 2 * width :].astype(jnp.bfloat16)
    q_bins = q_low.reshape(bin_count, BIN, width)
    k_bins = k_low.reshape(bin_count, BIN, width)
    v_bins = v_low.reshape(bin_count, BIN, width)
    mixed, log_total = lax.map(attend_bin, (q_bins, k_bins, v_bins, segment))
    mixed = mixed.reshape(row_count, width)
    residual_stream = (
        input_single_precision
        + matmul(mixed, block_parameters[4])
        + block_parameters[5].astype(jnp.float32)
    )
    second_centered_normalized, second_inverse_deviation = layer_norm_forward(residual_stream)
    second_activation = (
        second_centered_normalized * block_parameters[6].astype(jnp.float32)
        + block_parameters[7].astype(jnp.float32)
    ).astype(jnp.bfloat16)
    up_proj = matmul(second_activation, block_parameters[8]) + block_parameters[9].astype(
        jnp.float32
    )
    gelu_low = jax.nn.gelu(up_proj, approximate=False).astype(jnp.bfloat16)
    block_out = (
        residual_stream
        + matmul(gelu_low, block_parameters[10])
        + block_parameters[11].astype(jnp.float32)
    ).astype(jnp.bfloat16)
    block_parameters = (
        lax.all_gather(ln1_gain, "fsdp", axis=0, tiled=True),
        lax.all_gather(ln1_bias, "fsdp", axis=0, tiled=True),
        lax.all_gather(qkv_weight, "fsdp", axis=0, tiled=True),
        lax.all_gather(qkv_bias, "fsdp", axis=0, tiled=True),
        lax.all_gather(out_weight, "fsdp", axis=0, tiled=True),
        lax.all_gather(out_bias, "fsdp", axis=0, tiled=True),
        lax.all_gather(ln2_gain, "fsdp", axis=0, tiled=True),
        lax.all_gather(ln2_bias, "fsdp", axis=0, tiled=True),
        lax.all_gather(fc1_weight, "fsdp", axis=0, tiled=True),
        lax.all_gather(fc1_bias, "fsdp", axis=0, tiled=True),
        lax.all_gather(fc2_weight, "fsdp", axis=0, tiled=True),
        lax.all_gather(fc2_bias, "fsdp", axis=0, tiled=True),
        lax.all_gather(frequencies, "fsdp", axis=0, tiled=True),
    )
    output_gradient = cotangent.astype(jnp.float32)
    fc2_bias_grad = jnp.sum(output_gradient, axis=0)
    fc2_weight_grad = matmul_left_t(gelu_low, cotangent)
    d_up = (matmul_right_t(cotangent, block_parameters[10]) * gelu_slope(up_proj)).astype(
        jnp.bfloat16
    )
    fc1_bias_grad = jnp.sum(d_up.astype(jnp.float32), axis=0)
    fc1_weight_grad = matmul_left_t(second_activation, d_up)
    second_activation_gradient = matmul_right_t(d_up, block_parameters[8])
    second_norm_gain_gradient = jnp.sum(
        second_activation_gradient * second_centered_normalized, axis=0
    )
    ln2_bias_grad = jnp.sum(second_activation_gradient, axis=0)
    residual_gradient = output_gradient + layer_norm_backward(
        second_activation_gradient,
        second_centered_normalized,
        second_inverse_deviation,
        block_parameters[6].astype(jnp.float32),
    )
    d_att = residual_gradient.astype(jnp.bfloat16)
    out_bias_grad = jnp.sum(d_att.astype(jnp.float32), axis=0)
    out_weight_grad = matmul_left_t(mixed, d_att)
    d_mixed = matmul_right_t(d_att, block_parameters[4]).astype(jnp.bfloat16)
    d_qrot, d_krot, d_value = lax.map(
        attend_bin_back,
        (q_bins, k_bins, v_bins, d_mixed.reshape(bin_count, BIN, width), log_total, segment),
    )
    d_qrot = d_qrot.reshape(row_count, H, HD)
    d_krot = d_krot.reshape(row_count, H, HD)
    d_theta = (
        d_qrot[..., half_head:] * q_rot[..., :half_head]
        - d_qrot[..., :half_head] * q_rot[..., half_head:]
    )
    d_theta = (
        d_theta
        + d_krot[..., half_head:] * k_rot[..., :half_head]
        - d_krot[..., :half_head] * k_rot[..., half_head:]
    )
    frequencies_grad = jnp.concatenate(
        [
            jnp.sum(grid_row[:, None, None] * d_theta, axis=0).reshape(-1),
            jnp.sum(grid_col[:, None, None] * d_theta, axis=0).reshape(-1),
        ]
    )
    d_query = rotate(d_qrot, cosine, -sine).reshape(row_count, width)
    d_key = rotate(d_krot, cosine, -sine).reshape(row_count, width)
    d_qkv = jnp.concatenate([d_query, d_key, d_value.reshape(row_count, width)], axis=1).astype(
        jnp.bfloat16
    )
    qkv_bias_grad = jnp.sum(d_qkv.astype(jnp.float32), axis=0)
    qkv_weight_grad = matmul_left_t(first_activation, d_qkv)
    first_activation_gradient = matmul_right_t(d_qkv, block_parameters[2])
    first_norm_gain_gradient = jnp.sum(
        first_activation_gradient * first_centered_normalized, axis=0
    )
    ln1_bias_grad = jnp.sum(first_activation_gradient, axis=0)
    tokens_grad = (
        residual_gradient
        + layer_norm_backward(
            first_activation_gradient,
            first_centered_normalized,
            first_inverse_deviation,
            block_parameters[0].astype(jnp.float32),
        )
    ).astype(jnp.bfloat16)
    pieces = (
        lax.psum_scatter(first_norm_gain_gradient, "fsdp", scatter_dimension=0, tiled=True),
        lax.psum_scatter(ln1_bias_grad, "fsdp", scatter_dimension=0, tiled=True),
        lax.psum_scatter(qkv_weight_grad, "fsdp", scatter_dimension=0, tiled=True),
        lax.psum_scatter(qkv_bias_grad, "fsdp", scatter_dimension=0, tiled=True),
        lax.psum_scatter(out_weight_grad, "fsdp", scatter_dimension=0, tiled=True),
        lax.psum_scatter(out_bias_grad, "fsdp", scatter_dimension=0, tiled=True),
        lax.psum_scatter(second_norm_gain_gradient, "fsdp", scatter_dimension=0, tiled=True),
        lax.psum_scatter(ln2_bias_grad, "fsdp", scatter_dimension=0, tiled=True),
        lax.psum_scatter(fc1_weight_grad, "fsdp", scatter_dimension=0, tiled=True),
        lax.psum_scatter(fc1_bias_grad, "fsdp", scatter_dimension=0, tiled=True),
        lax.psum_scatter(fc2_weight_grad, "fsdp", scatter_dimension=0, tiled=True),
        lax.psum_scatter(fc2_bias_grad, "fsdp", scatter_dimension=0, tiled=True),
        lax.psum_scatter(frequencies_grad, "fsdp", scatter_dimension=0, tiled=True),
    )
    pieces = (
        lax.psum(pieces[0].astype(jnp.bfloat16), "dp").astype(jnp.float32),
        lax.psum(pieces[1].astype(jnp.bfloat16), "dp").astype(jnp.float32),
        lax.psum(pieces[2].astype(jnp.bfloat16), "dp").astype(jnp.float32),
        lax.psum(pieces[3].astype(jnp.bfloat16), "dp").astype(jnp.float32),
        lax.psum(pieces[4].astype(jnp.bfloat16), "dp").astype(jnp.float32),
        lax.psum(pieces[5].astype(jnp.bfloat16), "dp").astype(jnp.float32),
        lax.psum(pieces[6].astype(jnp.bfloat16), "dp").astype(jnp.float32),
        lax.psum(pieces[7].astype(jnp.bfloat16), "dp").astype(jnp.float32),
        lax.psum(pieces[8].astype(jnp.bfloat16), "dp").astype(jnp.float32),
        lax.psum(pieces[9].astype(jnp.bfloat16), "dp").astype(jnp.float32),
        lax.psum(pieces[10].astype(jnp.bfloat16), "dp").astype(jnp.float32),
        lax.psum(pieces[11].astype(jnp.bfloat16), "dp").astype(jnp.float32),
        lax.psum(pieces[12].astype(jnp.bfloat16), "dp").astype(jnp.float32),
    )
    freq_sq, other_sq = square_sums(pieces)
    freq_sq, other_sq = lax.psum((freq_sq, other_sq), "fsdp")
    return (
        block_out,
        tokens_grad,
        pieces[0],
        pieces[1],
        pieces[2],
        pieces[3],
        pieces[4],
        pieces[5],
        pieces[6],
        pieces[7],
        pieces[8],
        pieces[9],
        pieces[10],
        pieces[11],
        pieces[12],
        jnp.sqrt(freq_sq),
        jnp.sqrt(other_sq),
    )


def solution(mesh):
    placed = (
        P(("fsdp", "dp"), None),
        P(("fsdp", "dp"), None),
        P("fsdp"),
        P("fsdp"),
        P("fsdp", None),
        P("fsdp"),
        P("fsdp", None),
        P("fsdp"),
        P("fsdp"),
        P("fsdp"),
        P("fsdp", None),
        P("fsdp"),
        P("fsdp", None),
        P("fsdp"),
        P("fsdp"),
        P(("fsdp", "dp"), None),
    )
    return jax.shard_map(
        shards,
        mesh=mesh,
        in_specs=placed,
        out_specs=(
            P(("fsdp", "dp"), None),
            P(("fsdp", "dp"), None),
            P("fsdp"),
            P("fsdp"),
            P("fsdp", None),
            P("fsdp"),
            P("fsdp", None),
            P("fsdp"),
            P("fsdp"),
            P("fsdp"),
            P("fsdp", None),
            P("fsdp"),
            P("fsdp", None),
            P("fsdp"),
            P("fsdp"),
            P(),
            P(),
        ),
        check_vma=False,
    )
```

profile of v0, /device:TPU:0, one launch (start us, length us, event | category | flops | bytes accessed | tf_op | source)
XLA Modules:
  0.0 1132.8 jit_solution(17472799987714436141)
XLA Ops:
  19.5 40.6 %all-reduce.19 = (bf16[768]{0:T(1024)(128)(2,1)S(1)}, bf16[2304]{0:T(1024)(128)(2,1)S(1)}, bf16[768]{0:T(1024)(128)(2,1)S(1)}, bf16[768]{0:T(1024)(128)(2,1)S(1)...) all-reduce(bf16[768]{0:T(1024)(128)(2,1)S(1)} %dynamic-update-slice, ...), channel_id=1, replica_groups=mesh['fsdp'=8,'dp'=4] {'fsdp'}, use_global_device_ids=true, to_apply=%add.3 | all-reduce | flops 7680 | bytes 30720
  62.9 26.6 %all-gather = bf16[8,1,384]{2,1,0:T(2,128)(2,1)S(1)} all-gather(bf16[1,1,384]{2,1,0:T(2,128)(2,1)S(1)} %reshape.697), channel_id=1, replica_groups=mesh['fsdp'=8,'dp'=4] {'fsdp'}, dimensions={0}, use_global_device_ids=true | all-gather | bytes 6912 | tf_op jit(solution)/shard_map/all_gather | solution.py:185
  91.6 6.3 convolution_add_fusion
  109.4 10.8 fusion.87
  126.7 83.8 %while.48 = (s32[]{:T(128)}, bf16[12,1024,64]{1,2,0:T(8,128)(2,1)}, f32[12,1024]{1,0:T(8,128)S(1)}, s32[12]{0:T(128)S(1)}, bf16[1024,768]{1,0:T(8,128)(2,1)S(1)}...) while((s32[]{:T(128)}, bf16[12,1024,64]{1,2,0:T(8,128)(2,1)}, ...), condition=%wide.region_9.10_spmd.clone, body=%wide.region_6.9_spmd.clone.sunk | while | flops 283180032 | bytes 13558979 | solution.py:120
  216.5 39.0 %fusion.44 = (bf16[1024,3072]{1,0:T(8,128)(2,1)}, f32[1024,3072]{1,0:T(8,128)}) fusion(f32[3072]{0:T(1024)S(1)} %bitcast.103, bf16[768,3072]{1,0:T(8,128)(2,1)} %all-gather.10.cloned.1.call-done, f32[1024,768]{0,1:T(8,128)} %copy-done.4, f32[768]{0:T(1024)S(1)} %convert_element_type.206, f32[768]{0:T(1024)S(1)} %convert_element_type.205, ...), kind=kOutput, calls=%fused_computation.50 | convolution fusion | flops 5043388416 | bytes 26765312 | tf_op jit(solution)/shard_map/dot_general | solution.py:17
  255.6 24.8 %all-gather.12.cloned.1.call-done = bf16[3072,768]{1,0:T(8,128)(2,1)} async-done(((bf16[384,768]{1,0:T(8,128)(2,1)}), bf16[3072,768]{1,0:T(8,128)(2,1)}) %all-gather.12.cloned.1.call-update) | async-done | bytes 4718608 | tf_op jit(solution)/shard_map/all_gather | solution.py:186
  280.4 11.9 %convert_reduce_fusion = (f32[3072]{0:T(1024)S(1)}, bf16[1024,3072]{1,0:T(8,128)(2,1)S(1)}) fusion(f32[1024,3072]{1,0:T(8,128)} %get-tuple-element.504, f32[3072]{0:T(1024)S(1)} %bitcast.104, bf16[1024,768]{1,0:T(8,128)(2,1)S(1)} %copy-done.15, bf16[3072,768]{1,0:T(8,128)(2,1)} %all-gather.12.cloned.1.call-done), kind=kOutput, calls=%fused_computation.57 | convolution fusion | flops 4872729600 | bytes 25190400 | tf_op jit(solution)/shard_map/dot_general | solution.py:27
  292.3 6.7 fusion.100
  317.3 230.9 %while.49 = (s32[]{:T(128)}, f32[12,1024,64]{1,2,0:T(8,128)}, f32[12,1024,64]{1,2,0:T(8,128)}, bf16[12,1024,64]{1,2,0:T(8,128)(2,1)}, s32[12]{0:T(128)S(1)}, /*i...) while((s32[]{:T(128)}, f32[12,1024,64]{1,2,0:T(8,128)}, ...), condition=%wide.region_16.17_spmd.clone, body=%wide.region_14.16_spmd.clone.sunk | while | flops 681704448 | bytes 50886960 | solution.py:145
  548.3 12.2 %multiply_subtract_fusion = (f32[1024,12,32]{0,2,1:T(8,128)S(1)}, bf16[1024,12,32]{0,2,1:T(8,128)(2,1)S(1)}, bf16[1024,12,32]{0,2,1:T(8,128)(2,1)S(1)}, bf16[1024,12,32]{0,2,1:T(8,128)(2,1)S(1)}) fusion(f32[1024,12,64]{0,2,1:T(8,128)} %bitcast.87, f32[1024,12,64]{0,2,1:T(8,128)} %bitcast.97, f32[1024,12,64]{0,2,1:T(8,128)} %bitcast.86, ...), kind=kLoop, calls=%fused_computation.114 | loop fusion | flops 13762560 | bytes 16526336 | tf_op jit(solution)/shard_map/sub | solution.py:282
  560.5 6.4 multiply_reduce_fusion.7
  569.4 7.0 fusion.89
  576.5 10.6 fusion.93
  587.1 9.9 fusion.101
  599.6 10.1 add_convert_fusion
  612.4 8.6 fusion.99
  636.5 35.2 %all-reduce.18 = (bf16[768]{0:T(1024)(128)(2,1)S(1)}, bf16[768]{0:T(1024)(128)(2,1)S(1)}, bf16[2304]{0:T(1024)(128)(2,1)S(1)}, bf16[768]{0:T(1024)(128)(2,1)S(1)...) all-reduce(f32[768]{0:T(1024)S(1)} %get-tuple-element.365, ...), channel_id=2, replica_groups=mesh['fsdp'=8,'dp'=4] {'fsdp'}, use_global_device_ids=true, to_apply=%region_20.21.clone | all-reduce | flops 10752 | bytes 64512
  672.4 6.1 all-reduce.20
  687.0 18.8 %reduce-scatter.5.cloned.1.call-done = f32[96,2304]{1,0:T(8,128)} async-done(((f32[768,2304]{1,0:T(8,128)}), f32[96,2304]{1,0:T(8,128)}) %reduce-scatter.5.cloned.1.call-update) | async-done | bytes 884752 | tf_op jit(solution)/shard_map/reduce_scatter | solution.py:316
  707.8 162.9 %reduce-scatter.9.cloned.1.call-done = f32[96,3072]{1,0:T(8,128)} async-done(((f32[768,3072]{1,0:T(8,128)}), f32[96,3072]{1,0:T(8,128)}) %reduce-scatter.9.cloned.1.call-update) | async-done | bytes 1179664 | tf_op jit(solution)/shard_map/reduce_scatter | solution.py:322
  872.8 162.6 %reduce-scatter.11.cloned.1.call-done = f32[384,768]{1,0:T(8,128)} async-done(((f32[3072,768]{1,0:T(8,128)}), f32[384,768]{1,0:T(8,128)}) %reduce-scatter.11.cloned.1.call-update) | async-done | bytes 1179664 | tf_op jit(solution)/shard_map/reduce_scatter | solution.py:324
  1042.3 42.1 %all-reduce.24.cloned.1.call-done = (bf16[96,2304]{1,0:T(8,128)(2,1)}, bf16[96,768]{1,0:T(8,128)(2,1)}, bf16[96,3072]{1,0:T(8,128)(2,1)}, bf16[384,768]{1,0:T(8,128)(2,1)}) async-done(((bf16[96,2304]{1,0:T(8,128)(2,1)}, bf16[96,768]{1,0:T(8,128)(2,1)}, bf16[96,3072]{1,0:T(8,128)(2,1)}, bf16[384,768]{1,0:T(8,128)(2,1)}), (bf16[96,2304]{1,0:T(8,128)(2,1)}, bf16[96,768]{1,0:T(8,128)(2,1)}, ...) | async-done | bytes 1769488 | tf_op jit(solution)/shard_map/psum | solution.py:331
  1100.5 22.0 %all-reduce.17 = (f32[]{:T(128)}, f32[]{:T(128)}) all-reduce(f32[]{:T(128)} %get-tuple-element.469, f32[]{:T(128)S(6)} %add.305), channel_id=1, replica_groups=mesh['fsdp'=8,'dp'=4] {'fsdp'}, use_global_device_ids=true, to_apply=%region_56.57 | all-reduce | flops 2 | bytes 16 | tf_op jit(solution)/shard_map/psum | solution.py:344
  (396 shorter events, 381.8 us)
Async XLA Ops:
  7.2 84.4 %all-gather.6.cloned.1.call-start = ((), (), s32[]{:S(2)}) async-start(), calls=%async_computation.4 | async-start | bytes 3981312 | tf_op jit(solution)/shard_map/all_gather | solution.py:178
  7.9 202.5 %all-gather.8.cloned.1.call-start = ((), (), s32[]{:S(2)}) async-start(), calls=%async_computation.5 | async-start | bytes 1327104 | tf_op jit(solution)/shard_map/all_gather | solution.py:180
  8.7 207.8 %all-gather.10.cloned.1.call-start = ((), (), s32[]{:S(2)}) async-start(), calls=%async_computation.6 | async-start | bytes 5308416 | tf_op jit(solution)/shard_map/all_gather | solution.py:184
  9.4 271.0 %all-gather.12.cloned.1.call-start = ((), (), s32[]{:S(2)}) async-start(), calls=%async_computation.7 | async-start | bytes 5308416 | tf_op jit(solution)/shard_map/all_gather | solution.py:186
  10.0 675.4 %reduce-scatter.7.cloned.1.call-start = ((), (), s32[]{:S(2)}) async-start(), calls=%async_computation.9 | async-start | bytes 2654208 | tf_op jit(solution)/shard_map/reduce_scatter | solution.py:318
  60.1 29.5 %copy-start.14 = (bf16[1024,768]{1,0:T(8,128)(2,1)S(1)}, bf16[1024,768]{1,0:T(8,128)(2,1)}, u32[]{:S(2)}) copy-start(bf16[1024,768]{1,0:T(8,128)(2,1)} %param.35) | copy-start | bytes 4718596
  61.9 148.6 %copy-start.1 = (bf16[1024,768]{0,1:T(8,128)(2,1)}, bf16[1024,768]{0,1:T(8,128)(2,1)S(1)}, u32[]{:S(2)}) copy-start(bf16[1024,768]{0,1:T(8,128)(2,1)S(1)} %copy.80) | copy-start | bytes 4718596
  61.9 29.7 %copy-start.32 = (f32[768]{0:T(1024)}, f32[768]{0:T(1024)S(1)}, u32[]{:S(2)}) copy-start(f32[768]{0:T(1024)S(1)} %convert_element_type.195) | copy-start | bytes 9220
  62.0 29.7 %copy-start.28 = (f32[768]{0:T(1024)}, f32[768]{0:T(1024)S(1)}, u32[]{:S(2)}) copy-start(f32[768]{0:T(1024)S(1)} %convert_element_type.194) | copy-start | bytes 9220
  62.2 35.7 %copy-start.22 = (f32[1024]{0:T(1024)}, f32[1024]{0:T(1024)S(1)}, u32[]{:S(2)}) copy-start(f32[1024]{0:T(1024)S(1)} %broadcast_multiply_fusion.5) | copy-start | bytes 12292
  62.7 35.3 %copy-start.30 = (f32[1024]{0:T(1024)}, f32[1024]{0:T(1024)S(1)}, u32[]{:S(2)}) copy-start(f32[1024]{0:T(1024)S(1)} %add_rsqrt_fusion.1) | copy-start | bytes 12292
  62.8 46.6 %copy-start.18 = (f32[12,32]{1,0:T(8,128)}, f32[12,32]{1,0:T(8,128)S(1)}, u32[]{:S(2)}) copy-start(f32[12,32]{1,0:T(8,128)S(1)} %slice.81) | copy-start | bytes 4612
  62.9 46.5 %copy-start.20 = (f32[12,32]{1,0:T(8,128)}, f32[12,32]{1,0:T(8,128)S(1)}, u32[]{:S(2)}) copy-start(f32[12,32]{1,0:T(8,128)S(1)} %slice.79) | copy-start | bytes 4612
  91.6 17.8 %copy-start.24 = (f32[1024]{0:T(1024)}, f32[1024]{0:T(1024)S(1)}, u32[]{:S(2)}) copy-start(f32[1024]{0:T(1024)S(1)} %get-tuple-element.490) | copy-start | bytes 12292
  216.5 63.9 %copy-start.15 = (bf16[1024,768]{1,0:T(8,128)(2,1)S(1)}, bf16[1024,768]{1,0:T(8,128)(2,1)}, u32[]{:S(2)}) copy-start(bf16[1024,768]{1,0:T(8,128)(2,1)} %param.35) | copy-start | bytes 4718596
  312.3 393.5 %reduce-scatter.5.cloned.1.call-start = ((), (), s32[]{:S(2)}) async-start(), calls=%async_computation.8 | async-start | bytes 7962624 | tf_op jit(solution)/shard_map/reduce_scatter | solution.py:316
  317.3 230.9 %copy-start.3 = (f32[1024,768]{0,1:T(8,128)S(1)}, f32[1024,768]{0,1:T(8,128)}, u32[]{:S(2)}) copy-start(f32[1024,768]{0,1:T(8,128)} %copy.82) | copy-start | bytes 9437188
  317.3 230.9 %copy-start.19 = (f32[12,32]{1,0:T(8,128)S(1)}, f32[12,32]{1,0:T(8,128)}, u32[]{:S(2)}) copy-start(f32[12,32]{1,0:T(8,128)} %copy-done.18) | copy-start | bytes 4612
  317.3 230.9 %copy-start.21 = (f32[12,32]{1,0:T(8,128)S(1)}, f32[12,32]{1,0:T(8,128)}, u32[]{:S(2)}) copy-start(f32[12,32]{1,0:T(8,128)} %copy-done.20) | copy-start | bytes 4612
  317.3 231.0 %copy-start.25 = (f32[1024]{0:T(1024)S(1)}, f32[1024]{0:T(1024)}, u32[]{:S(2)}) copy-start(f32[1024]{0:T(1024)} %copy-done.24) | copy-start | bytes 12292
  317.3 230.9 %copy-start.27 = (f32[1024]{0:T(1024)S(1)}, f32[1024]{0:T(1024)}, u32[]{:S(2)}) copy-start(f32[1024]{0:T(1024)} %copy-done.26) | copy-start | bytes 12292
  576.4 294.2 %reduce-scatter.9.cloned.1.call-start = ((), (), s32[]{:S(2)}) async-start(), calls=%async_computation.10 | async-start | bytes 10616832 | tf_op jit(solution)/shard_map/reduce_scatter | solution.py:322
  587.1 448.3 %reduce-scatter.11.cloned.1.call-start = ((), (), s32[]{:S(2)}) async-start(), calls=%async_computation.11 | async-start | bytes 10616832 | tf_op jit(solution)/shard_map/reduce_scatter | solution.py:324
  597.0 487.4 %all-reduce.24.cloned.1.call-start = ((), (), s32[]{:S(2)}) async-start(), calls=%async_computation.12 | async-start | bytes 3538944 | tf_op jit(solution)/shard_map/psum | solution.py:331
  (37 other events, 155.2 us)
Sparse Core Ops, SparseCore 0:
  10.2 67.9 all-gather.5
  80.4 39.9 all-gather.7
  122.6 77.9 all-gather.9
  202.6 77.6 all-gather.11
  312.5 67.9 reduce-scatter.6
  576.6 129.1 reduce-scatter.4
  709.4 161.1 reduce-scatter.8
  874.2 161.1 reduce-scatter.10
  1039.2 45.2 all-reduce.23
where the time goes:
time: 1140 us; the launch traced here: 1130 us
  waiting for transfers between devices  414 us (36%)
  matrix products  354 us (31%)
  blocking collectives  130 us (11%)
  other arithmetic  101 us (9%)
  local copies, waits for them, and re-layouts  62 us (5%)
  loops' own time  40.6 us (4%)
  between operations  29.2 us (3%)
    reduce_scatter x1, waiting for transfers between devices, shards(): lax.psum_scatter(fc1_weight_grad, 'fsdp', scatter_dimension=0, tiled=True)  163 us
    reduce_scatter x1, waiting for transfers between devices, shards(): lax.psum_scatter(fc2_weight_grad, 'fsdp', scatter_dimension=0, tiled=True)  163 us
    dot_general x40, matrix products, matmul_right_t(): lax.dot_general(left, right, (((1,), (1,)), ((), ())), preferred_element_...  145 us
    dot_general x28, matrix products, matmul(): return jnp.dot(left, right, preferred_element_type=jnp.float32)  120 us
    dot_general x28, matrix products, matmul_left_t(): lax.dot_general(left, right, (((0,), (0,)), ((), ())), preferred_element_...  89.3 us
    unnamed x2, blocking collectives  75.7 us
    psum x1, waiting for transfers between devices, shards(): lax.psum(pieces[2].astype(jnp.bfloat16), 'dp').astype(jnp.float32)  42.1 us
    another operation x1, loops' own time, attend_bin_back(): d_query, d_key, d_value = lax.map(one_head, jnp.arange(H, dtype=jnp.int32))  32.1 us
  transfers between devices with their start and end apart: 9, of which 5 were waited for; matrix products, arithmetic and copies ran while one was open for 41% of the time, Pallas kernels for 0%

commit v1 on v0

--- a/solution.py
+++ b/solution.py
@@ -3,9 +3,11 @@
 from jax import lax
 from jax.sharding import PartitionSpec as P
 
+
 H = 12
 HD = 64
 BIN = 1024
+PACK_ROWS = 16
 
 
 norm_eps = 1e-06
@@ -154,6 +156,46 @@
     return (freq_sq, other_sq)
 
 
+def gather_weight(shard):
+    pieces = lax.psum(1, "dp")
+    part = shard.shape[0] // pieces
+    mine = lax.dynamic_slice_in_dim(shard, lax.axis_index("dp") * part, part, 0)
+    return lax.all_gather(mine, ("fsdp", "dp"), axis=0, tiled=True)
+
+
+def gather_small(vectors):
+    sizes = [v.shape[0] for v in vectors]
+    packed = lax.all_gather(jnp.concatenate(vectors), "fsdp", axis=0, tiled=False)
+    out, at = [], 0
+    for n in sizes:
+        out.append(packed[:, at : at + n].reshape(-1))
+        at += n
+    return out
+
+
+def reduce_grads(grads):
+    blocks = lax.psum(1, ("fsdp", "dp"))
+    flats = [g.reshape(blocks, -1).astype(jnp.bfloat16) for g in grads]
+    sizes = [f.shape[1] for f in flats]
+    total = sum(sizes)
+    padded = -(-total // (PACK_ROWS * 128)) * PACK_ROWS * 128
+    if padded > total:
+        flats.append(jnp.zeros((blocks, padded - total), jnp.bfloat16))
+    packed = jnp.concatenate(flats, axis=1).reshape(blocks * PACK_ROWS, padded // PACK_ROWS)
+    return packed, sizes
+
+
+def finish_grads(packed, sizes, shapes):
+    mine = lax.psum_scatter(packed, ("fsdp", "dp"), scatter_dimension=0, tiled=True)
+    owned = lax.all_gather(mine, "dp", axis=0, tiled=True)
+    owned = owned.reshape(lax.psum(1, "dp"), -1)
+    out, at = [], 0
+    for n, shape in zip(sizes, shapes):
+        out.append(owned[:, at : at + n].reshape(shape).astype(jnp.float32))
+        at += n
+    return out
+
+
 def shards(
     tokens,
     image_table,
@@ -172,20 +214,23 @@
     frequencies,
     cotangent,
 ):
+    small_local = (ln1_gain, ln1_bias, qkv_bias, out_bias, ln2_gain, ln2_bias, fc1_bias, fc2_bias, frequencies)
+    (g_ln1_gain, g_ln1_bias, g_qkv_bias, g_out_bias, g_ln2_gain, g_ln2_bias, g_fc1_bias, g_fc2_bias,
+     g_frequencies) = gather_small(small_local)
     block_parameters = (
-        lax.all_gather(ln1_gain, "fsdp", axis=0, tiled=True),
-        lax.all_gather(ln1_bias, "fsdp", axis=0, tiled=True),
-        lax.all_gather(qkv_weight, "fsdp", axis=0, tiled=True),
-        lax.all_gather(qkv_bias, "fsdp", axis=0, tiled=True),
-        lax.all_gather(out_weight, "fsdp", axis=0, tiled=True),
-        lax.all_gather(out_bias, "fsdp", axis=0, tiled=True),
-        lax.all_gather(ln2_gain, "fsdp", axis=0, tiled=True),
-        lax.all_gather(ln2_bias, "fsdp", axis=0, tiled=True),
-        lax.all_gather(fc1_weight, "fsdp", axis=0, tiled=True),
-        lax.all_gather(fc1_bias, "fsdp", axis=0, tiled=True),
-        lax.all_gather(fc2_weight, "fsdp", axis=0, tiled=True),
-        lax.all_gather(fc2_bias, "fsdp", axis=0, tiled=True),
-        lax.all_gather(frequencies, "fsdp", axis=0, tiled=True),
+        g_ln1_gain,
+        g_ln1_bias,
+        gather_weight(qkv_weight),
+        g_qkv_bias,
+        gather_weight(out_weight),
+        g_out_bias,
+        g_ln2_gain,
+        g_ln2_bias,
+        gather_weight(fc1_weight),
+        g_fc1_bias,
+        gather_weight(fc2_weight),
+        g_fc2_bias,
+        g_frequencies,
     )
     row_count, width = tokens.shape
     bin_count = row_count // BIN
@@ -230,21 +275,6 @@
         + matmul(gelu_low, block_parameters[10])
         + block_parameters[11].astype(jnp.float32)
     ).astype(jnp.bfloat16)
-    block_parameters = (
-        lax.all_gather(ln1_gain, "fsdp", axis=0, tiled=True),
-        lax.all_gather(ln1_bias, "fsdp", axis=0, tiled=True),
-        lax.all_gather(qkv_weight, "fsdp", axis=0, tiled=True),
-        lax.all_gather(qkv_bias, "fsdp", axis=0, tiled=True),
-        lax.all_gather(out_weight, "fsdp", axis=0, tiled=True),
-        lax.all_gather(out_bias, "fsdp", axis=0, tiled=True),
-        lax.all_gather(ln2_gain, "fsdp", axis=0, tiled=True),
-        lax.all_gather(ln2_bias, "fsdp", axis=0, tiled=True),
-        lax.all_gather(fc1_weight, "fsdp", axis=0, tiled=True),
-        lax.all_gather(fc1_bias, "fsdp", axis=0, tiled=True),
-        lax.all_gather(fc2_weight, "fsdp", axis=0, tiled=True),
-        lax.all_gather(fc2_bias, "fsdp", axis=0, tiled=True),
-        lax.all_gather(frequencies, "fsdp", axis=0, tiled=True),
-    )
     output_gradient = cotangent.astype(jnp.float32)
     fc2_bias_grad = jnp.sum(output_gradient, axis=0)
     fc2_weight_grad = matmul_left_t(gelu_low, cotangent)
@@ -268,6 +298,17 @@
     out_bias_grad = jnp.sum(d_att.astype(jnp.float32), axis=0)
     out_weight_grad = matmul_left_t(mixed, d_att)
     d_mixed = matmul_right_t(d_att, block_parameters[4]).astype(jnp.bfloat16)
+    early_packed, early_sizes = reduce_grads(
+        (fc2_weight_grad, fc1_weight_grad, out_weight_grad, fc2_bias_grad, fc1_bias_grad,
+         out_bias_grad, second_norm_gain_gradient, ln2_bias_grad)
+    )
+    early_packed, d_mixed = lax.optimization_barrier((early_packed, d_mixed))
+    early_owned = finish_grads(
+        early_packed,
+        early_sizes,
+        (fc2_weight.shape, fc1_weight.shape, out_weight.shape, fc2_bias.shape, fc1_bias.shape,
+         out_bias.shape, ln2_gain.shape, ln2_bias.shape),
+    )
     d_qrot, d_krot, d_value = lax.map(
         attend_bin_back,
         (q_bins, k_bins, v_bins, d_mixed.reshape(bin_count, BIN, width), log_total, segment),
@@ -310,54 +351,38 @@
             block_parameters[0].astype(jnp.float32),
         )
     ).astype(jnp.bfloat16)
+    late_packed, late_sizes = reduce_grads(
+        (qkv_weight_grad, qkv_bias_grad, first_norm_gain_gradient, ln1_bias_grad, frequencies_grad)
+    )
+    late_owned = finish_grads(
+        late_packed,
+        late_sizes,
+        (qkv_weight.shape, qkv_bias.shape, ln1_gain.shape, ln1_bias.shape, frequencies.shape),
+    )
+    (fc2_weight_g, fc1_weight_g, out_weight_g, fc2_bias_g, fc1_bias_g, out_bias_g, ln2_gain_g,
+     ln2_bias_g) = early_owned
+    qkv_weight_g, qkv_bias_g, ln1_gain_g, ln1_bias_g, frequencies_g = late_owned
     pieces = (
-        lax.psum_scatter(first_norm_gain_gradient, "fsdp", scatter_dimension=0, tiled=True),
-        lax.psum_scatter(ln1_bias_grad, "fsdp", scatter_dimension=0, tiled=True),
-        lax.psum_scatter(qkv_weight_grad, "fsdp", scatter_dimension=0, tiled=True),
-        lax.psum_scatter(qkv_bias_grad, "fsdp", scatter_dimension=0, tiled=True),
-        lax.psum_scatter(out_weight_grad, "fsdp", scatter_dimension=0, tiled=True),
-        lax.psum_scatter(out_bias_grad, "fsdp", scatter_dimension=0, tiled=True),
-        lax.psum_scatter(second_norm_gain_gradient, "fsdp", scatter_dimension=0, tiled=True),
-        lax.psum_scatter(ln2_bias_grad, "fsdp", scatter_dimension=0, tiled=True),
-        lax.psum_scatter(fc1_weight_grad, "fsdp", scatter_dimension=0, tiled=True),
-        lax.psum_scatter(fc1_bias_grad, "fsdp", scatter_dimension=0, tiled=True),
-        lax.psum_scatter(fc2_weight_grad, "fsdp", scatter_dimension=0, tiled=True),
-        lax.psum_scatter(fc2_bias_grad, "fsdp", scatter_dimension=0, tiled=True),
-        lax.psum_scatter(frequencies_grad, "fsdp", scatter_dimension=0, tiled=True),
-    )
-    pieces = (
-        lax.psum(pieces[0].astype(jnp.bfloat16), "dp").astype(jnp.float32),
-        lax.psum(pieces[1].astype(jnp.bfloat16), "dp").astype(jnp.float32),
-        lax.psum(pieces[2].astype(jnp.bfloat16), "dp").astype(jnp.float32),
-        lax.psum(pieces[3].astype(jnp.bfloat16), "dp").astype(jnp.float32),
-        lax.psum(pieces[4].astype(jnp.bfloat16), "dp").astype(jnp.float32),
-        lax.psum(pieces[5].astype(jnp.bfloat16), "dp").astype(jnp.float32),
-        lax.psum(pieces[6].astype(jnp.bfloat16), "dp").astype(jnp.float32),
-        lax.psum(pieces[7].astype(jnp.bfloat16), "dp").astype(jnp.float32),
-        lax.psum(pieces[8].astype(jnp.bfloat16), "dp").astype(jnp.float32),
-        lax.psum(pieces[9].astype(jnp.bfloat16), "dp").astype(jnp.float32),
-        lax.psum(pieces[10].astype(jnp.bfloat16), "dp").astype(jnp.float32),
-        lax.psum(pieces[11].astype(jnp.bfloat16), "dp").astype(jnp.float32),
-        lax.psum(pieces[12].astype(jnp.bfloat16), "dp").astype(jnp.float32),
+        ln1_gain_g,
+        ln1_bias_g,
+        qkv_weight_g,
+        qkv_bias_g,
+        out_weight_g,
+        out_bias_g,
+        ln2_gain_g,
+        ln2_bias_g,
+        fc1_weight_g,
+        fc1_bias_g,
+        fc2_weight_g,
+        fc2_bias_g,
+        frequencies_g,
     )
     freq_sq, other_sq = square_sums(pieces)
     freq_sq, other_sq = lax.psum((freq_sq, other_sq), "fsdp")
     return (
         block_out,
         tokens_grad,
-        pieces[0],
-        pieces[1],
-        pieces[2],
-        pieces[3],
-        pieces[4],
-        pieces[5],
-        pieces[6],
-        pieces[7],
-        pieces[8],
-        pieces[9],
-        pieces[10],
-        pieces[11],
-        pieces[12],
+        *pieces,
         jnp.sqrt(freq_sq),
         jnp.sqrt(other_sq),
     )

time: 1140 us -> 1040 us (0.912)
  waiting for transfers between devices: 414 us -> 279 us
  local copies, waits for them, and re-layouts: 62 us -> 175 us
  blocking collectives: 130 us -> 67.8 us
  matrix products: 354 us -> 333 us
  other arithmetic: 101 us -> 85.5 us
  loops' own time: 40.6 us -> 54.5 us
    reduce_scatter x4 -> x2, waiting for transfers between devices: 344 us -> 264 us  [finish_grads(): lax.psum_scatter(packed, ('fsdp', 'dp'), scatter_dimension=0, tiled=True)]
    psum x1 -> x0, waiting for transfers between devices: 42.1 us -> none  [shards(): lax.psum(pieces[2].astype(jnp.bfloat16), 'dp').astype(jnp.float32)]
    unnamed x2 -> x1, blocking collectives: 75.7 us -> 39 us
    convert_element_type x0 -> x33, local copies, waits for them, and re-layouts: none -> 32.7 us  [the longest x12 19.6 us: reduce_grads(): flats = [g.reshape(blocks, -1).astype(jnp.bfloat16) for g in grads]]
    unnamed x113 -> x96, local copies, waits for them, and re-layouts: 28.1 us -> 49.9 us
    all_gather x1, blocking collectives: 26.6 us -> 6.69 us  [finish_grads(): owned = lax.all_gather(mine, 'dp', axis=0, tiled=True)]
    reshape x2 -> x4, local copies, waits for them, and re-layouts: 0.15 us -> 18.8 us  [the longest x2 16 us: reduce_grads(): jnp.concatenate(flats, axis=1)]
    dot_general x28, matrix products: 89.3 us -> 71.9 us  [matmul_left_t(): lax.dot_general(left, right, (((0,), (0,)), ((), ())), preferred_element_...]
  transfers between devices with their start and end apart: 9 -> 7, of which waited for: 5 -> 4; matrix products, arithmetic and copies ran while one was open for 41% -> 21% of each run, Pallas kernels for 0% -> 0%
where the time goes in v1:
time: 1040 us; the launch traced here: 1020 us
  matrix products  333 us (32%)
  waiting for transfers between devices  279 us (27%)
  local copies, waits for them, and re-layouts  175 us (17%)
  other arithmetic  85.5 us (8%)
  blocking collectives  67.8 us (7%)
  loops' own time  54.5 us (5%)
  between operations  26.9 us (3%)
    reduce_scatter x2, waiting for transfers between devices, finish_grads(): lax.psum_scatter(packed, ('fsdp', 'dp'), scatter_dimension=0, tiled=True)  264 us
    dot_general x40, matrix products, matmul_right_t(): lax.dot_general(left, right, (((1,), (1,)), ((), ())), preferred_element_...  142 us
    dot_general x28, matrix products, matmul(): return jnp.dot(left, right, preferred_element_type=jnp.float32)  119 us
    dot_general x28, matrix products, matmul_left_t(): lax.dot_general(left, right, (((0,), (0,)), ((), ())), preferred_element_...  71.9 us
    unnamed x96, local copies, waits for them, and re-layouts  49.9 us
    unnamed x1, blocking collectives  39 us
    another operation x1, loops' own time, attend_bin_back(): d_query, d_key, d_value = lax.map(one_head, jnp.arange(H, dtype=jnp.int32))  31.7 us
    another operation x1, loops' own time, attend_bin(): mixed, log_total = lax.map(one_head, jnp.arange(H, dtype=jnp.int32))  22.7 us
  transfers between devices with their start and end apart: 7, of which 4 were waited for; matrix products, arithmetic and copies ran while one was open for 21% of the time, Pallas kernels for 0%

profile of v1, /device:TPU:0, one launch (start us, length us, event | category | flops | bytes accessed | tf_op | source)
XLA Modules:
  0.0 1021.9 jit_solution(17143126398018337644)
XLA Ops:
  14.8 6.1 concatenate.38
  21.3 39.0 %all-reduce = bf16[10752]{0:T(1024)(128)(2,1)S(1)} all-reduce(bf16[10752]{0:T(1024)(128)(2,1)S(1)} %dynamic-update-slice), channel_id=2, replica_groups=mesh['fsdp'=8,'dp'=4] {'fsdp'}, use_global_device_ids=true, to_apply=%add | all-reduce | flops 10752 | bytes 43008
  68.1 6.1 all-gather.7.cloned.1.call-done
  74.2 6.3 convolution_add_fusion
  92.0 10.8 %fusion.86 = (bf16[1024,12,32]{0,2,1:T(8,128)(2,1)S(1)}, bf16[1024,12,32]{0,2,1:T(8,128)(2,1)S(1)}, bf16[1024,12,32]{0,2,1:T(8,128)(2,1)S(1)}, bf16[1024,12,32]{0,2,1:T(8,128)(2,1)S(1)}) fusion(f32[1024,12,64]{0,2,1:T(8,128)} %bitcast.82, f32[12,32]{1,0:T(8,128)S(1)} %mul.400, f32[1024]{0:T(1024)S(1)} %get-tuple-element.427, f32[12,32]{1,0:T(8,128)S(1)} %mul.395, ...), kind=kLoop, calls=%fused_computation.204 | loop fusion | flops 7471104 | bytes 9448448 | tf_op jit(solution)/shard_map/convert.41
  110.2 115.0 %while.48 = (s32[]{:T(128)}, bf16[12,1024,64]{1,2,0:T(8,128)(2,1)}, f32[12,1024]{1,0:T(8,128)}, s32[12]{0:T(128)S(1)}, bf16[1024,768]{1,0:T(8,128)(2,1)}, /*inde...) while((s32[]{:T(128)}, bf16[12,1024,64]{1,2,0:T(8,128)(2,1)}, ...), condition=%wide.region_9.10_spmd.clone, body=%wide.region_6.9_spmd.clone.sunk | while | flops 283180032 | bytes 13558979 | solution.py:122
  230.8 38.9 %fusion.44 = (bf16[1024,3072]{1,0:T(8,128)(2,1)}, f32[1024,3072]{1,0:T(8,128)}) fusion(f32[3072]{0:T(1024)S(1)} %reshape.807, bf16[768,3072]{1,0:T(8,128)(2,1)} %all-gather.11.cloned.1.call-done, f32[1024,768]{0,1:T(8,128)} %copy-done.5, f32[768]{0:T(1024)S(1)} %reshape.806, f32[768]{0:T(1024)S(1)} %reshape.805, f32[1024]{0:T(1024)S(1)} %add_rsqrt_fusion, ...), kind=kOutput, calls=%fused_computation.50 | convolution fusion | flops 5043388416 | bytes 26765312 | tf_op jit(solution)/shard_map/dot_general | solution.py:19
  269.7 11.9 %fusion.96 = (bf16[3072]{0:T(1024)(128)(2,1)S(1)}, bf16[1024,3072]{1,0:T(8,128)(2,1)S(1)}) fusion(f32[1024,3072]{1,0:T(8,128)} %get-tuple-element.438, f32[3072]{0:T(1024)S(1)} %reshape.807, bf16[3072,768]{1,0:T(8,128)(2,1)} %all-gather.13.cloned.1.call-done, bf16[1024,768]{1,0:T(8,128)(2,1)S(1)} %copy-done.10), kind=kOutput, calls=%fused_computation.212 | convolution fusion | flops 4869583872 | bytes 25184256 | tf_op jit(solution)/shard_map/dot_general | solution.py:29
  281.7 7.1 convolution_convert_fusion
  288.7 6.7 fusion.97
  302.9 9.7 convolution_convert_fusion.1
  312.6 6.3 convert_element_type.380
  323.7 6.2 convert_element_type.382
  353.3 10.8 %reshape.794 = bf16[512,10496]{1,0:T(8,128)(2,1)} reshape(bf16[32,167936]{1,0:T(8,128)(2,1)} %dynamic-update-slice.15) | data formatting | bytes 21495808 | tf_op jit(solution)/shard_map/reshape | solution.py:184
  367.5 228.4 %while.49 = (s32[]{:T(128)}, f32[12,1024,64]{1,2,0:T(8,128)}, f32[12,1024,64]{1,2,0:T(8,128)}, bf16[12,1024,64]{1,2,0:T(8,128)(2,1)}, s32[12]{0:T(128)S(1)}, /*i...) while((s32[]{:T(128)}, f32[12,1024,64]{1,2,0:T(8,128)}, ...), condition=%wide.region_21.22_spmd.clone, body=%wide.region_19.21_spmd.clone.sunk | while | flops 681704448 | bytes 50886960 | solution.py:147
  595.9 12.7 %multiply_subtract_fusion = (f32[1024,12,32]{0,2,1:T(8,128)S(1)}, bf16[1024,12,32]{0,2,1:T(8,128)(2,1)S(1)}, bf16[1024,12,32]{0,2,1:T(8,128)(2,1)S(1)}, bf16[1024,12,32]{0,2,1:T(8,128)(2,1)S(1)}) fusion(f32[1024,12,64]{0,2,1:T(8,128)} %bitcast.86, f32[1024,12,64]{0,2,1:T(8,128)} %bitcast.96, f32[1024,12,64]{0,2,1:T(8,128)} %bitcast.85, ...), kind=kLoop, calls=%fused_computation.113 | loop fusion | flops 13762560 | bytes 16526336 | tf_op jit(solution)/shard_map/sub | solution.py:323
  608.6 6.4 multiply_reduce_fusion.7
  616.9 6.0 convolution_convert_fusion.2
  660.1 10.0 add_convert_fusion
  680.3 119.8 %reduce-scatter.3.cloned.1.call-done = bf16[16,3584]{1,0:T(8,128)(2,1)} async-done(((bf16[512,3584]{1,0:T(8,128)(2,1)}), bf16[16,3584]{1,0:T(8,128)(2,1)}) %reduce-scatter.3.cloned.1.call-update) | async-done | bytes 114704 | tf_op jit(solution)/shard_map/reduce_scatter | solution.py:189
  800.1 6.7 all_gather.30
  807.1 144.1 %reduce-scatter.5.cloned.1.call-done = bf16[16,10496]{1,0:T(8,128)(2,1)} async-done(((bf16[512,10496]{1,0:T(8,128)(2,1)}), bf16[16,10496]{1,0:T(8,128)(2,1)}) %reduce-scatter.5.cloned.1.call-update) | async-done | bytes 335888 | tf_op jit(solution)/shard_map/reduce_scatter | solution.py:189
  960.2 8.0 all-gather.15.cloned.1.call-done
  989.1 22.1 %all-reduce.1 = (f32[]{:T(128)}, f32[]{:T(128)}) all-reduce(f32[]{:T(128)} %get-tuple-element.346, f32[]{:T(128)S(6)} %add.267), channel_id=1, replica_groups=mesh['fsdp'=8,'dp'=4] {'fsdp'}, use_global_device_ids=true, to_apply=%region_32.33 | all-reduce | flops 2 | bytes 16 | tf_op jit(solution)/shard_map/psum | solution.py:381
  (411 shorter events, 439.0 us)
Async XLA Ops:
  7.2 56.4 %copy-start.9 = (bf16[1024,768]{1,0:T(8,128)(2,1)S(1)}, bf16[1024,768]{1,0:T(8,128)(2,1)}, u32[]{:S(2)}) copy-start(bf16[1024,768]{1,0:T(8,128)(2,1)} %param.35) | copy-start | bytes 4718596
  7.2 67.0 %all-gather.7.cloned.1.call-start = ((), (), s32[]{:S(2)}) async-start(), calls=%async_computation.2 | async-start | bytes 3649536 | tf_op jit(solution)/shard_map/all_gather | solution.py:163
  9.0 216.2 %all-gather.9.cloned.1.call-start = ((), (), s32[]{:S(2)}) async-start(), calls=%async_computation.3 | async-start | bytes 1216512 | tf_op jit(solution)/shard_map/all_gather | solution.py:163
  10.4 220.3 %all-gather.11.cloned.1.call-start = ((), (), s32[]{:S(2)}) async-start(), calls=%async_computation.4 | async-start | bytes 4866048 | tf_op jit(solution)/shard_map/all_gather | solution.py:163
  11.2 258.5 %all-gather.13.cloned.1.call-start = ((), (), s32[]{:S(2)}) async-start(), calls=%async_computation.5 | async-start | bytes 4866048 | tf_op jit(solution)/shard_map/all_gather | solution.py:163
  12.9 787.2 %reduce-scatter.3.cloned.1.call-start = ((), (), s32[]{:S(2)}) async-start(), calls=%async_computation.6 | async-start | bytes 3784704 | tf_op jit(solution)/shard_map/reduce_scatter | solution.py:189
  65.8 159.4 %copy-start.3 = (bf16[1024,768]{0,1:T(8,128)(2,1)}, bf16[1024,768]{0,1:T(8,128)(2,1)S(1)}, u32[]{:S(2)}) copy-start(bf16[1024,768]{0,1:T(8,128)(2,1)S(1)} %copy.65) | copy-start | bytes 4718596
  65.9 14.6 %copy-start.31 = (f32[768]{0:T(1024)}, f32[768]{0:T(1024)S(1)}, u32[]{:S(2)}) copy-start(f32[768]{0:T(1024)S(1)} %reshape.802) | copy-start | bytes 9220
  66.0 14.5 %copy-start.25 = (f32[768]{0:T(1024)}, f32[768]{0:T(1024)S(1)}, u32[]{:S(2)}) copy-start(f32[768]{0:T(1024)S(1)} %reshape.801) | copy-start | bytes 9220
  66.3 14.3 %copy-start.19 = (f32[1024]{0:T(1024)}, f32[1024]{0:T(1024)S(1)}, u32[]{:S(2)}) copy-start(f32[1024]{0:T(1024)S(1)} %broadcast_multiply_fusion.5) | copy-start | bytes 12292
  66.7 13.8 %copy-start.27 = (f32[1024]{0:T(1024)}, f32[1024]{0:T(1024)S(1)}, u32[]{:S(2)}) copy-start(f32[1024]{0:T(1024)S(1)} %add_rsqrt_fusion.1) | copy-start | bytes 12292
  66.8 25.2 %copy-start.15 = (f32[12,32]{1,0:T(8,128)}, f32[12,32]{1,0:T(8,128)S(1)}, u32[]{:S(2)}) copy-start(f32[12,32]{1,0:T(8,128)S(1)} %mul.400) | copy-start | bytes 4612
  66.9 25.1 %copy-start.17 = (f32[12,32]{1,0:T(8,128)}, f32[12,32]{1,0:T(8,128)S(1)}, u32[]{:S(2)}) copy-start(f32[12,32]{1,0:T(8,128)S(1)} %mul.395) | copy-start | bytes 4612
  68.1 23.9 %copy-start.21 = (f32[1024]{0:T(1024)}, f32[1024]{0:T(1024)S(1)}, u32[]{:S(2)}) copy-start(f32[1024]{0:T(1024)S(1)} %get-tuple-element.426) | copy-start | bytes 12292
  68.1 23.9 %copy-start.23 = (f32[1024]{0:T(1024)}, f32[1024]{0:T(1024)S(1)}, u32[]{:S(2)}) copy-start(f32[1024]{0:T(1024)S(1)} %get-tuple-element.427) | copy-start | bytes 12292
  230.7 39.0 %copy-start.10 = (bf16[1024,768]{1,0:T(8,128)(2,1)S(1)}, bf16[1024,768]{1,0:T(8,128)(2,1)}, u32[]{:S(2)}) copy-start(bf16[1024,768]{1,0:T(8,128)(2,1)} %param.35) | copy-start | bytes 4718596
  367.5 228.4 %copy-start.16 = (f32[12,32]{1,0:T(8,128)S(1)}, f32[12,32]{1,0:T(8,128)}, u32[]{:S(2)}) copy-start(f32[12,32]{1,0:T(8,128)} %copy-done.15) | copy-start | bytes 4612
  367.5 228.4 %copy-start.18 = (f32[12,32]{1,0:T(8,128)S(1)}, f32[12,32]{1,0:T(8,128)}, u32[]{:S(2)}) copy-start(f32[12,32]{1,0:T(8,128)} %copy-done.17) | copy-start | bytes 4612
  367.5 228.4 %copy-start.22 = (f32[1024]{0:T(1024)S(1)}, f32[1024]{0:T(1024)}, u32[]{:S(2)}) copy-start(f32[1024]{0:T(1024)} %copy-done.21) | copy-start | bytes 12292
  367.5 228.4 %copy-start.24 = (f32[1024]{0:T(1024)S(1)}, f32[1024]{0:T(1024)}, u32[]{:S(2)}) copy-start(f32[1024]{0:T(1024)} %copy-done.23) | copy-start | bytes 12292
  595.9 12.7 %copy-start.7 = (f32[12,1024,64]{1,2,0:T(8,128)S(1)}, f32[12,1024,64]{1,2,0:T(8,128)}, u32[]{:S(2)}) copy-start(f32[12,1024,64]{1,2,0:T(8,128)} %get-tuple-element.176) | copy-start | bytes 9437188
  659.4 291.8 %reduce-scatter.5.cloned.1.call-start = ((), (), s32[]{:S(2)}) async-start(), calls=%async_computation.7 | async-start | bytes 11083776 | tf_op jit(solution)/shard_map/reduce_scatter | solution.py:189
  660.0 308.2 %all-gather.15.cloned.1.call-start = ((), (), s32[]{:S(2)}) async-start(), calls=%async_computation.8 | async-start | bytes 1679360 | tf_op jit(solution)/shard_map/all_gather | solution.py:190
  972.7 40.0 %copy-start.1 = (bf16[96,3072]{1,0:T(8,128)(2,1)S(1)}, bf16[96,3072]{1,0:T(8,128)(2,1)}, u32[]{:S(2)}) copy-start(bf16[96,3072]{1,0:T(8,128)(2,1)} %param.30) | copy-start | bytes 1769476
  (32 other events, 124.1 us)
Sparse Core Ops, SparseCore 0:
  11.5 62.6 all-gather.6
  77.1 52.7 all-gather.8
  133.3 62.4 all-gather.10
  199.1 61.9 all-gather.12
  659.5 140.5 reduce-scatter.2
  802.3 148.9 reduce-scatter.4
  952.8 15.3 all-gather.14

commit v2 on v1

--- a/solution.py
+++ b/solution.py
@@ -1,12 +1,14 @@
 import jax
 import jax.numpy as jnp
 from jax import lax
+from jax.experimental import pallas as pl
 from jax.sharding import PartitionSpec as P
 
 
 H = 12
 HD = 64
 BIN = 1024
+Q_BLOCK = 256
 PACK_ROWS = 16
 
 
@@ -96,56 +98,124 @@
     )
 
 
-def join_heads(stacked):
-    return jnp.transpose(stacked, (1, 0, 2)).reshape(stacked.shape[1], H * HD)
-
-
-def head_slice(matrix, head_index):
-    return lax.dynamic_slice_in_dim(matrix, head_index * HD, HD, 1)
-
-
-def attend_bin(packed):
-    query, key_rows, value, segment = packed
-    mask = segment[:, None] == segment[None, :]
+def _nt(a, b):
+    return lax.dot_general(a, b, (((1,), (1,)), ((), ())), preferred_element_type=jnp.float32)
+
+
+def _tn(a, b):
+    return lax.dot_general(a, b, (((0,), (0,)), ((), ())), preferred_element_type=jnp.float32)
+
+
+def _nn(a, b):
+    return lax.dot_general(a, b, (((1,), (0,)), ((), ())), preferred_element_type=jnp.float32)
+
+
+def attention_forward_kernel(q_ref, k_ref, v_ref, seg_r_ref, seg_c_ref, o_ref, lse_ref):
+    rows = q_ref.shape[0]
+    seg_c = seg_c_ref[...]
     scale = HD ** (-0.5)
-
-    def one_head(head_index):
-        q_head = head_slice(query, head_index)
-        k_head = head_slice(key_rows, head_index)
-        v_head = head_slice(value, head_index)
-        scores = jnp.where(mask, matmul_right_t(q_head, k_head) * scale, masked_score)
-        top = jnp.max(scores, axis=-1, keepdims=True)
-        log_total = top + jnp.log(jnp.sum(jnp.exp(scores - top), axis=-1, keepdims=True))
-        probs = jnp.exp(scores - log_total).astype(jnp.bfloat16)
-        return (matmul(probs, v_head).astype(jnp.bfloat16), log_total[:, 0])
-
-    mixed, log_total = lax.map(one_head, jnp.arange(H, dtype=jnp.int32))
-    return (join_heads(mixed), log_total)
-
-
-def attend_bin_back(packed):
-    query, key_rows, value, d_mixed, log_total, segment = packed
-    mask = segment[:, None] == segment[None, :]
+    for half in range(q_ref.shape[1] // HD):
+        cols = slice(half * HD, (half + 1) * HD)
+        k_h = k_ref[:, cols]
+        v_h = v_ref[:, cols]
+
+        def block(i, carry):
+            at = pl.multiple_of(i * Q_BLOCK, Q_BLOCK)
+            q_h = q_ref[pl.ds(at, Q_BLOCK), cols]
+            mask = seg_r_ref[pl.ds(at, Q_BLOCK), :] == seg_c
+            scores = jnp.where(mask, _nt(q_h, k_h) * scale, masked_score)
+            top = jnp.max(scores, axis=-1, keepdims=True)
+            log_total = top + jnp.log(jnp.sum(jnp.exp(scores - top), axis=-1, keepdims=True))
+            probs = jnp.exp(scores - log_total).astype(jnp.bfloat16)
+            o_ref[pl.ds(at, Q_BLOCK), cols] = _nn(probs, v_h).astype(o_ref.dtype)
+            lse_ref[pl.ds(at, Q_BLOCK), cols] = jnp.broadcast_to(log_total, (Q_BLOCK, HD))
+            return carry
+
+        lax.fori_loop(0, rows // Q_BLOCK, block, 0)
+
+
+def attention_backward_kernel(q_ref, k_ref, v_ref, d_ref, lse_ref, seg_r_ref, seg_c_ref, dq_ref, dk_ref, dv_ref):
+    rows = q_ref.shape[0]
+    seg_c = seg_c_ref[...]
     scale = HD ** (-0.5)
-
-    def one_head(head_index):
-        q_head = head_slice(query, head_index)
-        k_head = head_slice(key_rows, head_index)
-        v_head = head_slice(value, head_index)
-        d_head = head_slice(d_mixed, head_index)
-        total_head = lax.dynamic_index_in_dim(log_total, head_index, 0, keepdims=False)
-        scores = jnp.where(mask, matmul_right_t(q_head, k_head) * scale, masked_score)
-        probs = jnp.exp(scores - total_head[:, None])
-        d_probs = matmul_right_t(d_head, v_head)
-        d_value = matmul_left_t(probs.astype(jnp.bfloat16), d_head)
-        inner = jnp.sum(probs * d_probs, axis=-1, keepdims=True)
-        d_scores = (probs * (d_probs - inner)).astype(jnp.bfloat16)
-        d_query = matmul(d_scores, k_head) * scale
-        d_key = matmul_left_t(d_scores, q_head) * scale
-        return (d_query, d_key, d_value)
-
-    d_query, d_key, d_value = lax.map(one_head, jnp.arange(H, dtype=jnp.int32))
-    return (join_heads(d_query), join_heads(d_key), join_heads(d_value))
+    for half in range(q_ref.shape[1] // HD):
+        cols = slice(half * HD, (half + 1) * HD)
+        k_h = k_ref[:, cols]
+        v_h = v_ref[:, cols]
+
+        def block(i, carry):
+            dk_acc, dv_acc = carry
+            at = pl.multiple_of(i * Q_BLOCK, Q_BLOCK)
+            q_h = q_ref[pl.ds(at, Q_BLOCK), cols]
+            d_h = d_ref[pl.ds(at, Q_BLOCK), cols]
+            log_total = lse_ref[pl.ds(at, Q_BLOCK), pl.ds(half * HD, 1)]
+            mask = seg_r_ref[pl.ds(at, Q_BLOCK), :] == seg_c
+            scores = jnp.where(mask, _nt(q_h, k_h) * scale, masked_score)
+            probs = jnp.exp(scores - log_total)
+            d_probs = _nt(d_h, v_h)
+            dv_acc = dv_acc + _tn(probs.astype(jnp.bfloat16), d_h)
+            inner = jnp.sum(probs * d_probs, axis=-1, keepdims=True)
+            d_scores = (probs * (d_probs - inner)).astype(jnp.bfloat16)
+            dq_ref[pl.ds(at, Q_BLOCK), cols] = _nn(d_scores, k_h) * scale
+            dk_acc = dk_acc + _tn(d_scores, q_h)
+            return dk_acc, dv_acc
+
+        zero = jnp.zeros((rows, HD), jnp.float32)
+        dk_acc, dv_acc = lax.fori_loop(0, rows // Q_BLOCK, block, (zero, zero))
+        dk_ref[:, cols] = dk_acc * scale
+        dv_ref[:, cols] = dv_acc
+
+
+def attention_forward(q, k, v, segment):
+    rows, width = q.shape
+    pair = 2 * HD
+    seg_r = segment.reshape(rows, 1)
+    seg_c = segment.reshape(1, rows)
+    spec = pl.BlockSpec((rows, pair), lambda j: (0, j))
+    return pl.pallas_call(
+        attention_forward_kernel,
+        grid=(width // pair,),
+        in_specs=[spec, spec, spec, pl.BlockSpec((rows, 1), lambda j: (0, 0)), pl.BlockSpec((1, rows), lambda j: (0, 0))],
+        out_specs=[spec, spec],
+        out_shape=[jax.ShapeDtypeStruct((rows, width), jnp.bfloat16), jax.ShapeDtypeStruct((rows, width), jnp.float32)],
+        cost_estimate=pl.CostEstimate(
+            flops=4 * rows * rows * width, transcendentals=2 * rows * rows * (width // HD),
+            bytes_accessed=rows * width * (2 * 4 + 4)),
+        name="attention_forward",
+    )(q, k, v, seg_r, seg_c)
+
+
+def attention_backward(q, k, v, d_mixed, log_total, segment):
+    rows, width = q.shape
+    pair = 2 * HD
+    seg_r = segment.reshape(rows, 1)
+    seg_c = segment.reshape(1, rows)
+    spec = pl.BlockSpec((rows, pair), lambda j: (0, j))
+    f32 = jax.ShapeDtypeStruct((rows, width), jnp.float32)
+    return pl.pallas_call(
+        attention_backward_kernel,
+        grid=(width // pair,),
+        in_specs=[spec, spec, spec, spec, spec, pl.BlockSpec((rows, 1), lambda j: (0, 0)), pl.BlockSpec((1, rows), lambda j: (0, 0))],
+        out_specs=[spec, spec, spec],
+        out_shape=[f32, f32, f32],
+        cost_estimate=pl.CostEstimate(
+            flops=8 * rows * rows * width, transcendentals=rows * rows * (width // HD),
+            bytes_accessed=rows * width * (2 * 4 + 4 + 12)),
+        name="attention_backward",
+    )(q, k, v, d_mixed, log_total, seg_r, seg_c)
+
+
+def attention_bins(q_low, k_low, v_low, segment):
+    outs = [attention_forward(q_low[b * BIN:(b + 1) * BIN], k_low[b * BIN:(b + 1) * BIN],
+                              v_low[b * BIN:(b + 1) * BIN], segment[b]) for b in range(segment.shape[0])]
+    return tuple(jnp.concatenate(parts, axis=0) for parts in zip(*outs))
+
+
+def attention_bins_back(q_low, k_low, v_low, d_mixed, log_total, segment):
+    outs = [attention_backward(q_low[b * BIN:(b + 1) * BIN], k_low[b * BIN:(b + 1) * BIN],
+                               v_low[b * BIN:(b + 1) * BIN], d_mixed[b * BIN:(b + 1) * BIN],
+                               log_total[b * BIN:(b + 1) * BIN], segment[b]) for b in range(segment.shape[0])]
+    return tuple(jnp.concatenate(parts, axis=0) for parts in zip(*outs))
 
 
 def square_sums(pieces):
@@ -251,11 +321,7 @@
     q_low = q_rot.reshape(row_count, width).astype(jnp.bfloat16)
     k_low = k_rot.reshape(row_count, width).astype(jnp.bfloat16)
     v_low = qkv_full[:, 2 * width :].astype(jnp.bfloat16)
-    q_bins = q_low.reshape(bin_count, BIN, width)
-    k_bins = k_low.reshape(bin_count, BIN, width)
-    v_bins = v_low.reshape(bin_count, BIN, width)
-    mixed, log_total = lax.map(attend_bin, (q_bins, k_bins, v_bins, segment))
-    mixed = mixed.reshape(row_count, width)
+    mixed, log_total = attention_bins(q_low, k_low, v_low, segment)
     residual_stream = (
         input_single_precision
         + matmul(mixed, block_parameters[4])
@@ -309,10 +375,7 @@
         (fc2_weight.shape, fc1_weight.shape, out_weight.shape, fc2_bias.shape, fc1_bias.shape,
          out_bias.shape, ln2_gain.shape, ln2_bias.shape),
     )
-    d_qrot, d_krot, d_value = lax.map(
-        attend_bin_back,
-        (q_bins, k_bins, v_bins, d_mixed.reshape(bin_count, BIN, width), log_total, segment),
-    )
+    d_qrot, d_krot, d_value = attention_bins_back(q_low, k_low, v_low, d_mixed, log_total, segment)
     d_qrot = d_qrot.reshape(row_count, H, HD)
     d_krot = d_krot.reshape(row_count, H, HD)
     d_theta = (

time: 1040 us -> 884 us (0.85)
  matrix products: 333 us -> 125 us
  Pallas kernels: 0 us -> 114 us
  loops' own time: 54.5 us -> 0 us
  waiting for transfers between devices: 279 us -> 325 us
  local copies, waits for them, and re-layouts: 175 us -> 147 us
  other arithmetic: 85.5 us -> 65.3 us
    pallas_call x0 -> x2, Pallas kernels: none -> 114 us  [the longest x1 67.1 us: attention_backward(): pl.pallas_call(attention_backward_kernel, grid=(width // pair,), in_specs...]
    dot_general x40 -> x4, matrix products: 142 us -> 28.6 us  [matmul_right_t(): lax.dot_general(left, right, (((1,), (1,)), ((), ())), preferred_element_...]
    another operation x2 -> x0, loops' own time: 54.5 us -> none  [the longest x1 31.7 us: attend_bin_back(): d_query, d_key, d_value = lax.map(one_head, jnp.arange(H, dtype=jnp.int32))]
    dot_general x28 -> x4, matrix products: 119 us -> 69.9 us  [matmul(): return jnp.dot(left, right, preferred_element_type=jnp.float32)]
    all_gather x4, waiting for transfers between devices: 6.12 us -> 53.3 us  [gather_weight(): return lax.all_gather(mine, ('fsdp', 'dp'), axis=0, tiled=True)]
    dot_general x28 -> x4, matrix products: 71.9 us -> 26.7 us  [matmul_left_t(): lax.dot_general(left, right, (((0,), (0,)), ((), ())), preferred_element_...]
    dynamic_slice x36 -> x0, local copies, waits for them, and re-layouts: 23.2 us -> none  [the longest x24 14 us: attend_bin(): mixed, log_total = lax.map(one_head, jnp.arange(H, dtype=jnp.int32))]
    dynamic_update_slice x12 -> x0, local copies, waits for them, and re-layouts: 16.7 us -> none  [attend_bin(): mixed, log_total = lax.map(one_head, jnp.arange(H, dtype=jnp.int32))]
  transfers between devices with their start and end apart: 7 -> 7, of which waited for: 4 -> 6; matrix products, arithmetic and copies ran while one was open for 21% -> 16% of each run, Pallas kernels for 0% -> 5%
where the time goes in v2:
time: 884 us; the launch traced here: 872 us
  waiting for transfers between devices  325 us (37%)
  local copies, waits for them, and re-layouts  147 us (17%)
  matrix products  125 us (14%)
  Pallas kernels  114 us (13%)
  blocking collectives  67.6 us (8%)
  other arithmetic  65.3 us (7%)
  between operations  27 us (3%)
    reduce_scatter x2, waiting for transfers between devices, finish_grads(): lax.psum_scatter(packed, ('fsdp', 'dp'), scatter_dimension=0, tiled=True)  263 us
    dot_general x4, matrix products, matmul(): return jnp.dot(left, right, preferred_element_type=jnp.float32)  69.9 us
    pallas_call x1, Pallas kernels, attention_backward(): pl.pallas_call(attention_backward_kernel, grid=(width // pair,), in_specs...  67.1 us
    all_gather x4, waiting for transfers between devices, gather_weight(): return lax.all_gather(mine, ('fsdp', 'dp'), axis=0, tiled=True)  53.3 us
    pallas_call x1, Pallas kernels, attention_forward(): pl.pallas_call(attention_forward_kernel, grid=(width // pair,), in_specs=...  47.1 us
    unnamed x96, local copies, waits for them, and re-layouts  43.7 us
    unnamed x1, blocking collectives  39 us
    dot_general x4, matrix products, matmul_right_t(): lax.dot_general(left, right, (((1,), (1,)), ((), ())), preferred_element_...  28.6 us
  transfers between devices with their start and end apart: 7, of which 6 were waited for; matrix products, arithmetic and copies ran while one was open for 16% of the time, Pallas kernels for 5%

profile of v2, /device:TPU:0, one launch (start us, length us, event | category | flops | bytes accessed | tf_op | source)
XLA Modules:
  0.0 871.7 jit_solution(2798719699662174885)
XLA Ops:
  21.3 39.0 %all-reduce = bf16[10752]{0:T(1024)(128)(2,1)S(1)} all-reduce(bf16[10752]{0:T(1024)(128)(2,1)S(1)} %dynamic-update-slice), channel_id=2, replica_groups=mesh['fsdp'=8,'dp'=4] {'fsdp'}, use_global_device_ids=true, to_apply=%add | all-reduce | flops 10752 | bytes 43008
  74.2 6.3 convolution_add_fusion
  92.1 10.8 %fusion.44 = (bf16[1024,12,32]{0,2,1:T(8,128)(2,1)S(1)}, bf16[1024,12,32]{0,2,1:T(8,128)(2,1)S(1)}, bf16[1024,12,32]{0,2,1:T(8,128)(2,1)S(1)}, bf16[1024,12,32]{0,2,1:T(8,128)(2,1)S(1)}) fusion(f32[1024,12,64]{0,2,1:T(8,128)} %bitcast.36, f32[12,32]{1,0:T(8,128)S(1)} %mul.376, f32[1024]{0:T(1024)S(1)} %get-tuple-element.136, f32[12,32]{1,0:T(8,128)S(1)} %mul.371, ...), kind=kLoop, calls=%fused_computation.158 | loop fusion | flops 7471104 | bytes 9448448 | tf_op jit(solution)/shard_map/convert.39
  110.2 47.1 %attention_forward.1 = (bf16[1024,768]{1,0:T(8,128)(2,1)}, f32[1024,768]{1,0:T(8,128)}) custom-call(bf16[1024,768]{1,0:T(8,128)(2,1)} %copy.66.q_ref, bf16[1024,768]{1,0:T(8,128)(2,1)} %copy.67.k_ref, bf16[1024,768]{1,0:T(8,128)(2,1)} %slice.300.v_ref, s32[1024,1]{1,0:T(8,128)} %copy.68.seg_r_ref, s32[1,1024]{1,0:T(1,128)} %bitcast.48), custom_call_target="tpu_custom_call" | custom-call | flops 3221225472 | bytes 9437184 | tf_op jit(solution)/shard_map/attention_forward/pallas_call | solution.py:175
  162.8 33.2 %all-gather.11.cloned.1.call-done = bf16[768,3072]{1,0:T(8,128)(2,1)} async-done(((bf16[24,3072]{1,0:T(8,128)(2,1)}), bf16[768,3072]{1,0:T(8,128)(2,1)}) %all-gather.11.cloned.1.call-update) | async-done | bytes 4718608 | tf_op jit(solution)/shard_map/all_gather | solution.py:233
  196.0 50.2 %fusion.2 = (bf16[1024,3072]{1,0:T(8,128)(2,1)}, f32[1024,3072]{1,0:T(8,128)}) fusion(f32[3072]{0:T(1024)S(1)} %reshape.772, bf16[768,3072]{1,0:T(8,128)(2,1)} %all-gather.11.cloned.1.call-done, f32[1024,768]{0,1:T(8,128)} %copy-done.5, f32[768]{0:T(1024)S(1)} %reshape.771, f32[768]{0:T(1024)S(1)} %reshape.770, f32[1024]{0:T(1024)S(1)} %add_rsqrt_fusion, ...), kind=kOutput, calls=%fused_computation.4 | convolution fusion | flops 5043388416 | bytes 26765312 | tf_op jit(solution)/shard_map/dot_general | solution.py:21
  246.2 15.1 %all-gather.13.cloned.1.call-done = bf16[3072,768]{1,0:T(8,128)(2,1)} async-done(((bf16[96,768]{1,0:T(8,128)(2,1)}), bf16[3072,768]{1,0:T(8,128)(2,1)}) %all-gather.13.cloned.1.call-update) | async-done | bytes 4718608 | tf_op jit(solution)/shard_map/all_gather | solution.py:233
  261.3 11.9 %fusion.54 = (bf16[3072]{0:T(1024)(128)(2,1)S(1)}, bf16[1024,3072]{1,0:T(8,128)(2,1)S(1)}) fusion(f32[1024,3072]{1,0:T(8,128)} %get-tuple-element.147, f32[3072]{0:T(1024)S(1)} %reshape.772, bf16[3072,768]{1,0:T(8,128)(2,1)} %all-gather.13.cloned.1.call-done, bf16[1024,768]{1,0:T(8,128)(2,1)S(1)} %copy-done.9), kind=kOutput, calls=%fused_computation.166 | convolution fusion | flops 4869583872 | bytes 25184256 | tf_op jit(solution)/shard_map/dot_general | solution.py:31
  273.2 7.1 convolution_convert_fusion
  280.2 6.7 fusion.55
  294.4 9.7 %convolution_convert_fusion.1 = bf16[3072,768]{1,0:T(8,128)(2,1)} fusion(bf16[1024,3072]{1,0:T(8,128)(2,1)} %get-tuple-element.146, bf16[1024,768]{1,0:T(8,128)(2,1)S(1)} %copy-done.9), kind=kOutput, calls=%fused_computation.28 | convolution fusion | flops 4834197504 | bytes 12582912 | tf_op jit(solution)/shard_map/dot_general | solution.py:25
  304.1 6.3 convert_element_type.366
  315.2 6.2 convert_element_type.368
  344.8 10.8 %reshape.758 = bf16[512,10496]{1,0:T(8,128)(2,1)} reshape(bf16[32,167936]{1,0:T(8,128)(2,1)} %dynamic-update-slice.15) | data formatting | bytes 21495808 | tf_op jit(solution)/shard_map/reshape | solution.py:254
  360.1 67.1 %attention_backward.1 = (f32[1024,768]{1,0:T(8,128)}, f32[1024,768]{1,0:T(8,128)}, f32[1024,768]{1,0:T(8,128)}) custom-call(bf16[1024,768]{1,0:T(8,128)(2,1)} %copy.66.q_ref, bf16[1024,768]{1,0:T(8,128)(2,1)} %copy.67.k_ref, bf16[1024,768]{1,0:T(8,128)(2,1)} %slice.300.v_ref, bf16[1024,768]{1,0:T(8,128)(2,1)} %convolution_convert_fusion.3.d_ref, ...), custom_call_target="tpu_custom_call" | custom-call | flops 6442450944 | bytes 18874368 | tf_op jit(solution)/shard_map/attention_backward/pallas_call | solution.py:195
  437.7 13.4 %multiply_subtract_fusion = (f32[1024,12,32]{0,2,1:T(8,128)S(1)}, bf16[1024,12,32]{0,2,1:T(8,128)(2,1)S(1)}, bf16[1024,12,32]{0,2,1:T(8,128)(2,1)}, bf16[1024,12,32]{0,2,1:T(8,128)(2,1)S(1)}) fusion(f32[1024,12,64]{0,2,1:T(8,128)} %bitcast.40, f32[1024,12,64]{0,2,1:T(8,128)} %bitcast.42, f32[1024,12,64]{0,2,1:T(8,128)} %bitcast.39, ...), kind=kLoop, calls=%fused_computation.67 | loop fusion | flops 13762560 | bytes 16526336 | tf_op jit(solution)/shard_map/sub | solution.py:386
  451.1 6.4 multiply_reduce_fusion.6
  464.5 8.5 convolution_convert_fusion.2
  510.3 10.0 %add_convert_fusion = bf16[1024,768]{0,1:T(8,128)(2,1)} fusion(f32[1024,768]{0,1:T(8,128)} %copy-done.5, bf16[1024,3072]{1,0:T(8,128)(2,1)} %get-tuple-element.146, bf16[3072,768]{1,0:T(8,128)(2,1)} %all-gather.13.cloned.1.call-done, f32[768]{0:T(1024)S(1)} %reshape.773), kind=kOutput, calls=%fused_computation.54 | convolution fusion | flops 4834197504 | bytes 15731712 | tf_op jit(solution)/shard_map/dot_general | solution.py:21
  530.5 118.9 %reduce-scatter.3.cloned.1.call-done = bf16[16,3584]{1,0:T(8,128)(2,1)} async-done(((bf16[512,3584]{1,0:T(8,128)(2,1)}), bf16[16,3584]{1,0:T(8,128)(2,1)}) %reduce-scatter.3.cloned.1.call-update) | async-done | bytes 114704 | tf_op jit(solution)/shard_map/reduce_scatter | solution.py:259
  649.4 6.5 all_gather.30
  656.2 144.6 %reduce-scatter.5.cloned.1.call-done = bf16[16,10496]{1,0:T(8,128)(2,1)} async-done(((bf16[512,10496]{1,0:T(8,128)(2,1)}), bf16[16,10496]{1,0:T(8,128)(2,1)}) %reduce-scatter.5.cloned.1.call-update) | async-done | bytes 335888 | tf_op jit(solution)/shard_map/reduce_scatter | solution.py:259
  809.7 8.0 all-gather.15.cloned.1.call-done
  838.6 22.1 %all-reduce.1 = (f32[]{:T(128)}, f32[]{:T(128)}) all-reduce(f32[]{:T(128)} %get-tuple-element.97, f32[]{:T(128)S(6)} %add.221), channel_id=1, replica_groups=mesh['fsdp'=8,'dp'=4] {'fsdp'}, use_global_device_ids=true, to_apply=%region_25.26 | all-reduce | flops 2 | bytes 16 | tf_op jit(solution)/shard_map/psum | solution.py:444
  (220 shorter events, 179.0 us)
Async XLA Ops:
  7.2 56.4 %copy-start.8 = (bf16[1024,768]{1,0:T(8,128)(2,1)S(1)}, bf16[1024,768]{1,0:T(8,128)(2,1)}, u32[]{:S(2)}) copy-start(bf16[1024,768]{1,0:T(8,128)(2,1)} %param.31) | copy-start | bytes 4718596
  7.2 67.0 %all-gather.7.cloned.1.call-start = ((), (), s32[]{:S(2)}) async-start(), calls=%async_computation.2 | async-start | bytes 3649536 | tf_op jit(solution)/shard_map/all_gather | solution.py:233
  9.0 148.3 %all-gather.9.cloned.1.call-start = ((), (), s32[]{:S(2)}) async-start(), calls=%async_computation.3 | async-start | bytes 1216512 | tf_op jit(solution)/shard_map/all_gather | solution.py:233
  10.4 185.5 %all-gather.11.cloned.1.call-start = ((), (), s32[]{:S(2)}) async-start(), calls=%async_computation.4 | async-start | bytes 4866048 | tf_op jit(solution)/shard_map/all_gather | solution.py:233
  11.2 250.1 %all-gather.13.cloned.1.call-start = ((), (), s32[]{:S(2)}) async-start(), calls=%async_computation.5 | async-start | bytes 4866048 | tf_op jit(solution)/shard_map/all_gather | solution.py:233
  12.9 636.5 %reduce-scatter.3.cloned.1.call-start = ((), (), s32[]{:S(2)}) async-start(), calls=%async_computation.6 | async-start | bytes 3784704 | tf_op jit(solution)/shard_map/reduce_scatter | solution.py:259
  65.8 91.5 %copy-start.2 = (bf16[1024,768]{0,1:T(8,128)(2,1)}, bf16[1024,768]{0,1:T(8,128)(2,1)S(1)}, u32[]{:S(2)}) copy-start(bf16[1024,768]{0,1:T(8,128)(2,1)S(1)} %copy.63) | copy-start | bytes 4718596
  65.9 14.6 %copy-start.31 = (f32[768]{0:T(1024)}, f32[768]{0:T(1024)S(1)}, u32[]{:S(2)}) copy-start(f32[768]{0:T(1024)S(1)} %reshape.767) | copy-start | bytes 9220
  66.0 14.6 %copy-start.24 = (f32[768]{0:T(1024)}, f32[768]{0:T(1024)S(1)}, u32[]{:S(2)}) copy-start(f32[768]{0:T(1024)S(1)} %reshape.766) | copy-start | bytes 9220
  66.2 14.3 %copy-start.18 = (f32[1024]{0:T(1024)}, f32[1024]{0:T(1024)S(1)}, u32[]{:S(2)}) copy-start(f32[1024]{0:T(1024)S(1)} %broadcast_multiply_fusion.5) | copy-start | bytes 12292
  66.7 13.8 %copy-start.26 = (f32[1024]{0:T(1024)}, f32[1024]{0:T(1024)S(1)}, u32[]{:S(2)}) copy-start(f32[1024]{0:T(1024)S(1)} %add_rsqrt_fusion.1) | copy-start | bytes 12292
  66.8 25.3 %copy-start.14 = (f32[12,32]{1,0:T(8,128)}, f32[12,32]{1,0:T(8,128)S(1)}, u32[]{:S(2)}) copy-start(f32[12,32]{1,0:T(8,128)S(1)} %mul.376) | copy-start | bytes 4612
  66.9 25.2 %copy-start.16 = (f32[12,32]{1,0:T(8,128)}, f32[12,32]{1,0:T(8,128)S(1)}, u32[]{:S(2)}) copy-start(f32[12,32]{1,0:T(8,128)S(1)} %mul.371) | copy-start | bytes 4612
  67.2 13.3 %copy-start.29 = (s32[1024]{0:T(1024)}, s32[1024]{0:T(1024)S(1)}, u32[]{:S(2)}) copy-start(s32[1024]{0:T(1024)S(1)} %get-tuple-element.138) | copy-start | bytes 12292
  67.2 24.9 %copy-start.20 = (f32[1024]{0:T(1024)}, f32[1024]{0:T(1024)S(1)}, u32[]{:S(2)}) copy-start(f32[1024]{0:T(1024)S(1)} %get-tuple-element.135) | copy-start | bytes 12292
  67.3 24.9 %copy-start.22 = (f32[1024]{0:T(1024)}, f32[1024]{0:T(1024)S(1)}, u32[]{:S(2)}) copy-start(f32[1024]{0:T(1024)S(1)} %get-tuple-element.136) | copy-start | bytes 12292
  162.8 98.4 %copy-start.9 = (bf16[1024,768]{1,0:T(8,128)(2,1)S(1)}, bf16[1024,768]{1,0:T(8,128)(2,1)}, u32[]{:S(2)}) copy-start(bf16[1024,768]{1,0:T(8,128)(2,1)} %param.31) | copy-start | bytes 4718596
  261.3 11.9 %copy-start.6 = (f32[1024,768]{0,1:T(8,128)S(1)}, f32[1024,768]{0,1:T(8,128)}, u32[]{:S(2)}) copy-start(f32[1024,768]{0,1:T(8,128)} %copy-done.5) | copy-start | bytes 9437188
  344.8 10.8 %copy-start.36 = (bf16[768,768]{1,0:T(8,128)(2,1)S(1)}, bf16[768,768]{1,0:T(8,128)(2,1)}, u32[]{:S(2)}) copy-start(bf16[768,768]{1,0:T(8,128)(2,1)} %all-gather.9.cloned.1.call-done) | copy-start | bytes 3538948
  437.7 13.4 %copy-start.4 = (f32[1024,768]{0,1:T(8,128)S(1)}, f32[1024,768]{0,1:T(8,128)}, u32[]{:S(2)}) copy-start(f32[1024,768]{0,1:T(8,128)} %copy.77) | copy-start | bytes 9437188
  464.4 8.5 copy-start.10
  509.6 291.2 %reduce-scatter.5.cloned.1.call-start = ((), (), s32[]{:S(2)}) async-start(), calls=%async_computation.7 | async-start | bytes 11083776 | tf_op jit(solution)/shard_map/reduce_scatter | solution.py:259
  510.2 307.5 %all-gather.15.cloned.1.call-start = ((), (), s32[]{:S(2)}) async-start(), calls=%async_computation.8 | async-start | bytes 1679360 | tf_op jit(solution)/shard_map/all_gather | solution.py:260
  822.2 40.0 %copy-start.1 = (bf16[96,3072]{1,0:T(8,128)(2,1)S(1)}, bf16[96,3072]{1,0:T(8,128)(2,1)}, u32[]{:S(2)}) copy-start(bf16[96,3072]{1,0:T(8,128)(2,1)} %param.26) | copy-start | bytes 1769476
  (21 other events, 94.6 us)
Sparse Core Ops, SparseCore 0:
  11.5 62.6 all-gather.6
  77.1 52.6 all-gather.8
  133.3 62.6 all-gather.10
  199.3 61.9 all-gather.12
  509.7 139.6 reduce-scatter.2
  651.5 149.2 reduce-scatter.4
  802.3 15.3 all-gather.14

commit v3 on v2

--- a/solution.py
+++ b/solution.py
@@ -243,27 +243,58 @@
     return out
 
 
-def reduce_grads(grads):
+def column_chunks(matrix, width):
+    return [matrix[:, j * width : (j + 1) * width] for j in range(matrix.shape[1] // width)]
+
+
+def pack_rows(matrices, vectors):
     blocks = lax.psum(1, ("fsdp", "dp"))
-    flats = [g.reshape(blocks, -1).astype(jnp.bfloat16) for g in grads]
-    sizes = [f.shape[1] for f in flats]
-    total = sum(sizes)
-    padded = -(-total // (PACK_ROWS * 128)) * PACK_ROWS * 128
+    width = matrices[0].shape[1]
+    parts = [m.reshape(blocks, m.shape[0] // blocks, width).astype(jnp.bfloat16) for m in matrices]
+    flat = jnp.concatenate([v.reshape(blocks, -1) for v in vectors], axis=1)
+    small = flat.shape[1]
+    small_rows = -(-small // width)
+    flat = jnp.pad(flat, ((0, 0), (0, small_rows * width - small)))
+    parts.append(flat.reshape(blocks, small_rows, width).astype(jnp.bfloat16))
+    rows = [p.shape[1] for p in parts]
+    total = sum(rows)
+    padded = -(-total // PACK_ROWS) * PACK_ROWS
     if padded > total:
-        flats.append(jnp.zeros((blocks, padded - total), jnp.bfloat16))
-    packed = jnp.concatenate(flats, axis=1).reshape(blocks * PACK_ROWS, padded // PACK_ROWS)
-    return packed, sizes
-
-
-def finish_grads(packed, sizes, shapes):
-    mine = lax.psum_scatter(packed, ("fsdp", "dp"), scatter_dimension=0, tiled=True)
+        parts.append(jnp.zeros((blocks, padded - total, width), jnp.bfloat16))
+    layout = (rows, [v.shape[0] // blocks for v in vectors])
+    return jnp.concatenate(parts, axis=1), layout
+
+
+def unpack_rows(owned, layout):
+    rows, vector_sizes = layout
+    groups = owned.shape[0]
+    out, at = [], 0
+    for r in rows[:-1]:
+        out.append(owned[:, at : at + r, :].reshape(groups * r, owned.shape[2]).astype(jnp.float32))
+        at += r
+    flat = owned[:, at : at + rows[-1], :].reshape(groups, -1)
+    vectors, at = [], 0
+    for n in vector_sizes:
+        vectors.append(flat[:, at : at + n].reshape(-1).astype(jnp.float32))
+        at += n
+    return out, vectors
+
+
+def sum_on_sparse_core(packed, layout):
+    blocks, padded, width = packed.shape
+    mine = lax.psum_scatter(
+        packed.reshape(blocks * padded, width), ("fsdp", "dp"), scatter_dimension=0, tiled=True
+    )
     owned = lax.all_gather(mine, "dp", axis=0, tiled=True)
-    owned = owned.reshape(lax.psum(1, "dp"), -1)
-    out, at = [], 0
-    for n, shape in zip(sizes, shapes):
-        out.append(owned[:, at : at + n].reshape(shape).astype(jnp.float32))
-        at += n
-    return out
+    return unpack_rows(owned.reshape(-1, padded, width), layout)
+
+
+def sum_by_exchange(packed, layout):
+    _, padded, width = packed.shape
+    received = lax.all_to_all(packed, ("fsdp", "dp"), 0, 0, tiled=False)
+    mine = jnp.sum(received.astype(jnp.float32), axis=0)
+    owned = lax.all_gather(mine, "dp", axis=0, tiled=True)
+    return unpack_rows(owned.reshape(-1, padded, width), layout)
 
 
 def shards(
@@ -364,17 +395,13 @@
     out_bias_grad = jnp.sum(d_att.astype(jnp.float32), axis=0)
     out_weight_grad = matmul_left_t(mixed, d_att)
     d_mixed = matmul_right_t(d_att, block_parameters[4]).astype(jnp.bfloat16)
-    early_packed, early_sizes = reduce_grads(
-        (fc2_weight_grad, fc1_weight_grad, out_weight_grad, fc2_bias_grad, fc1_bias_grad,
-         out_bias_grad, second_norm_gain_gradient, ln2_bias_grad)
+    width = out_weight_grad.shape[1]
+    early_packed, early_layout = pack_rows(
+        [fc2_weight_grad, *column_chunks(fc1_weight_grad, width), out_weight_grad],
+        [fc2_bias_grad, fc1_bias_grad, out_bias_grad, second_norm_gain_gradient, ln2_bias_grad],
     )
     early_packed, d_mixed = lax.optimization_barrier((early_packed, d_mixed))
-    early_owned = finish_grads(
-        early_packed,
-        early_sizes,
-        (fc2_weight.shape, fc1_weight.shape, out_weight.shape, fc2_bias.shape, fc1_bias.shape,
-         out_bias.shape, ln2_gain.shape, ln2_bias.shape),
-    )
+    early_mats, early_vecs = sum_on_sparse_core(early_packed, early_layout)
     d_qrot, d_krot, d_value = attention_bins_back(q_low, k_low, v_low, d_mixed, log_total, segment)
     d_qrot = d_qrot.reshape(row_count, H, HD)
     d_krot = d_krot.reshape(row_count, H, HD)
@@ -414,17 +441,17 @@
             block_parameters[0].astype(jnp.float32),
         )
     ).astype(jnp.bfloat16)
-    late_packed, late_sizes = reduce_grads(
-        (qkv_weight_grad, qkv_bias_grad, first_norm_gain_gradient, ln1_bias_grad, frequencies_grad)
-    )
-    late_owned = finish_grads(
-        late_packed,
-        late_sizes,
-        (qkv_weight.shape, qkv_bias.shape, ln1_gain.shape, ln1_bias.shape, frequencies.shape),
-    )
-    (fc2_weight_g, fc1_weight_g, out_weight_g, fc2_bias_g, fc1_bias_g, out_bias_g, ln2_gain_g,
-     ln2_bias_g) = early_owned
-    qkv_weight_g, qkv_bias_g, ln1_gain_g, ln1_bias_g, frequencies_g = late_owned
+    late_packed, late_layout = pack_rows(
+        column_chunks(qkv_weight_grad, width),
+        [qkv_bias_grad, first_norm_gain_gradient, ln1_bias_grad, frequencies_grad],
+    )
+    late_mats, late_vecs = sum_by_exchange(late_packed, late_layout)
+    fc2_weight_g = early_mats[0]
+    fc1_weight_g = jnp.concatenate(early_mats[1:-1], axis=1)
+    out_weight_g = early_mats[-1]
+    fc2_bias_g, fc1_bias_g, out_bias_g, ln2_gain_g, ln2_bias_g = early_vecs
+    qkv_weight_g = jnp.concatenate(late_mats, axis=1)
+    qkv_bias_g, ln1_gain_g, ln1_bias_g, frequencies_g = late_vecs
     pieces = (
         ln1_gain_g,
         ln1_bias_g,

time: 884 us -> 696 us (0.79)
  waiting for transfers between devices: 325 us -> 122 us
  other arithmetic: 65.3 us -> 74.7 us
    reduce_scatter x2 -> x1, waiting for transfers between devices: 263 us -> 0.01 us  [sum_on_sparse_core(): lax.psum_scatter(packed.reshape(blocks * padded, width), ('fsdp', 'dp'),...]
    all_to_all x0 -> x1, waiting for transfers between devices: none -> 68.6 us  [sum_by_exchange(): received = lax.all_to_all(packed, ('fsdp', 'dp'), 0, 0, tiled=False)]
    concatenate x2 -> x3, local copies, waits for them, and re-layouts: 3.55 us -> 65.3 us  [the longest x2 65.2 us: pack_rows(): return (jnp.concatenate(parts, axis=1), layout)]
    unnamed x96 -> x81, local copies, waits for them, and re-layouts: 43.7 us -> 13.7 us
    convert_element_type x25 -> x8, local copies, waits for them, and re-layouts: 32.2 us -> 3.19 us  [the longest x5 3.03 us: unpack_rows(): vectors.append(flat[:, at:at + n].reshape(-1).astype(jnp.float32))]
    reshape x4 -> x12, local copies, waits for them, and re-layouts: 18.8 us -> 3.77 us  [the longest x4 2.44 us: unpack_rows(): vectors.append(flat[:, at:at + n].reshape(-1).astype(jnp.float32))]
  transfers between devices with their start and end apart: 7 -> 7, of which waited for: 6 -> 4; matrix products, arithmetic and copies ran while one was open for 16% -> 32% of each run, Pallas kernels for 5% -> 17%
where the time goes in v3:
time: 696 us; the launch traced here: 683 us
  local copies, waits for them, and re-layouts  142 us (20%)
  matrix products  130 us (19%)
  waiting for transfers between devices  122 us (18%)
  Pallas kernels  114 us (16%)
  other arithmetic  74.7 us (11%)
  blocking collectives  69 us (10%)
  between operations  27.2 us (4%)
    dot_general x4, matrix products, matmul(): return jnp.dot(left, right, preferred_element_type=jnp.float32)  70.1 us
    all_to_all x1, waiting for transfers between devices, sum_by_exchange(): received = lax.all_to_all(packed, ('fsdp', 'dp'), 0, 0, tiled=False)  68.6 us
    pallas_call x1, Pallas kernels, attention_backward(): pl.pallas_call(attention_backward_kernel, grid=(width // pair,), in_specs...  67 us
    concatenate x2, local copies, waits for them, and re-layouts, pack_rows(): return (jnp.concatenate(parts, axis=1), layout)  65.2 us
    all_gather x4, waiting for transfers between devices, gather_weight(): return lax.all_gather(mine, ('fsdp', 'dp'), axis=0, tiled=True)  53.5 us
    pallas_call x1, Pallas kernels, attention_forward(): pl.pallas_call(attention_forward_kernel, grid=(width // pair,), in_specs=...  46.9 us
    unnamed x1, blocking collectives  39 us
    dot_general x4, matrix products, matmul_right_t(): lax.dot_general(left, right, (((1,), (1,)), ((), ())), preferred_element_...  31.6 us
  transfers between devices with their start and end apart: 7, of which 4 were waited for; matrix products, arithmetic and copies ran while one was open for 32% of the time, Pallas kernels for 17%

profile of v3, /device:TPU:0, one launch (start us, length us, event | category | flops | bytes accessed | tf_op | source)
XLA Modules:
  0.0 682.9 jit_solution(8696839293026523385)
XLA Ops:
  14.8 6.1 concatenate.55
  21.3 39.0 %all-reduce.2 = bf16[10752]{0:T(1024)(128)(2,1)S(1)} all-reduce(bf16[10752]{0:T(1024)(128)(2,1)S(1)} %dynamic-update-slice), channel_id=2, replica_groups=mesh['fsdp'=8,'dp'=4] {'fsdp'}, use_global_device_ids=true, to_apply=%add.2 | all-reduce | flops 10752 | bytes 43008
  69.2 5.1 all-gather.7.cloned.1.call-done
  74.2 6.3 convolution_add_fusion
  92.1 10.8 %fusion.54 = (bf16[1024,12,32]{0,2,1:T(8,128)(2,1)S(1)}, bf16[1024,12,32]{0,2,1:T(8,128)(2,1)S(1)}, bf16[1024,12,32]{0,2,1:T(8,128)(2,1)S(1)}, bf16[1024,12,32]{0,2,1:T(8,128)(2,1)S(1)}) fusion(f32[1024,12,64]{0,2,1:T(8,128)} %bitcast.70, f32[12,32]{1,0:T(8,128)S(1)} %mul.374, f32[1024]{0:T(1024)S(1)} %get-tuple-element.166, f32[12,32]{1,0:T(8,128)S(1)} %mul.369, ...), kind=kLoop, calls=%fused_computation.164 | loop fusion | flops 7471104 | bytes 9448448 | tf_op jit(solution)/shard_map/convert.62
  110.3 46.9 %attention_forward.1 = (bf16[1024,768]{1,0:T(8,128)(2,1)}, f32[1024,768]{1,0:T(8,128)}) custom-call(bf16[1024,768]{1,0:T(8,128)(2,1)} %copy.100.q_ref, bf16[1024,768]{1,0:T(8,128)(2,1)} %copy.101.k_ref, bf16[1024,768]{1,0:T(8,128)(2,1)} %slice.363.v_ref, s32[1024,1]{1,0:T(8,128)} %copy.102.seg_r_ref, s32[1,1024]{1,0:T(1,128)} %bitcast.111), custom_call_target="tpu_custom_call" | custom-call | flops 3221225472 | bytes 9437184 | tf_op jit(solution)/shard_map/attention_forward/pallas_call | solution.py:175
  162.7 33.3 %all-gather.11.cloned.1.call-done = bf16[768,3072]{1,0:T(8,128)(2,1)} async-done(((bf16[24,3072]{1,0:T(8,128)(2,1)}), bf16[768,3072]{1,0:T(8,128)(2,1)}) %all-gather.11.cloned.1.call-update) | async-done | bytes 4718608 | tf_op jit(solution)/shard_map/all_gather | solution.py:233
  196.0 50.1 %fusion.2 = (bf16[1024,3072]{1,0:T(8,128)(2,1)}, f32[1024,3072]{1,0:T(8,128)}) fusion(f32[3072]{0:T(1024)S(1)} %reshape.836, bf16[768,3072]{1,0:T(8,128)(2,1)} %all-gather.11.cloned.1.call-done, f32[1024,768]{0,1:T(8,128)} %copy-done.4, f32[768]{0:T(1024)S(1)} %reshape.835, f32[768]{0:T(1024)S(1)} %reshape.834, f32[1024]{0:T(1024)S(1)} %add_rsqrt_fusion, ...), kind=kOutput, calls=%fused_computation.4 | convolution fusion | flops 5043388416 | bytes 26765312 | tf_op jit(solution)/shard_map/dot_general | solution.py:21
  246.1 15.1 %all-gather.13.cloned.1.call-done = bf16[3072,768]{1,0:T(8,128)(2,1)} async-done(((bf16[96,768]{1,0:T(8,128)(2,1)}), bf16[3072,768]{1,0:T(8,128)(2,1)}) %all-gather.13.cloned.1.call-update) | async-done | bytes 4718608 | tf_op jit(solution)/shard_map/all_gather | solution.py:233
  261.3 11.9 %fusion.68 = (bf16[3072]{0:T(1024)(128)(2,1)S(1)}, bf16[1024,3072]{1,0:T(8,128)(2,1)S(1)}) fusion(f32[1024,3072]{1,0:T(8,128)} %get-tuple-element.181, f32[3072]{0:T(1024)S(1)} %reshape.836, bf16[3072,768]{1,0:T(8,128)(2,1)} %all-gather.13.cloned.1.call-done, bf16[1024,768]{1,0:T(8,128)(2,1)S(1)} %copy-done.9), kind=kOutput, calls=%fused_computation.176 | convolution fusion | flops 4869583872 | bytes 25184256 | tf_op jit(solution)/shard_map/dot_general | solution.py:31
  273.2 7.1 %convolution_convert_fusion = bf16[768,3072]{1,0:T(8,128)(2,1)} fusion(bf16[1024,3072]{1,0:T(8,128)(2,1)S(1)} %get-tuple-element.183, f32[1024,768]{0,1:T(8,128)S(1)} %copy-done.5, f32[768]{0:T(1024)S(1)} %reshape.835, f32[768]{0:T(1024)S(1)} %reshape.834, f32[1024]{0:T(1024)S(1)} %add_rsqrt_fusion, f32[1024]{0:T(1024)S(1)} %broadcast_multiply_fusion.4), kind=kOutput, calls=%fused_computation.28 | convolution fusion | flops 4838129664 | bytes 14170112 | tf_op jit(solution)/shard_map/dot_general | solution.py:25
  280.3 6.8 fusion.69
  309.5 9.7 %convolution_convert_fusion.1 = bf16[3072,768]{1,0:T(8,128)(2,1)} fusion(bf16[1024,3072]{1,0:T(8,128)(2,1)} %get-tuple-element.180, bf16[1024,768]{1,0:T(8,128)(2,1)S(1)} %copy-done.9), kind=kOutput, calls=%fused_computation.29 | convolution fusion | flops 4834197504 | bytes 12582912 | tf_op jit(solution)/shard_map/dot_general | solution.py:25
  319.3 48.6 %concatenate.59 = bf16[32,224,768]{2,1,0:T(8,128)(2,1)} concatenate(bf16[32,96,768]{2,1,0:T(8,128)(2,1)} %bitcast.82, bf16[32,24,768]{2,1,0:T(8,128)(2,1)} %bitcast.86, bf16[32,24,768]{2,1,0:T(8,128)(2,1)} %bitcast.85, bf16[32,24,768]{2,1,0:T(8,128)(2,1)} %bitcast.84, bf16[32,24,768]{2,1,0:T(8,128)(2,1)S(1)} %bitcast.83, bf16[32,24,768]{2,1,0:T(8,128)(2,1)} %bitcast.98, ...), dimensions={1} | concatenate | bytes 22020096 | tf_op jit(solution)/shard_map/concatenate | solution.py:265
  372.4 67.0 %attention_backward.1 = (f32[1024,768]{1,0:T(8,128)}, f32[1024,768]{1,0:T(8,128)}, f32[1024,768]{1,0:T(8,128)}) custom-call(bf16[1024,768]{1,0:T(8,128)(2,1)} %copy.100.q_ref, bf16[1024,768]{1,0:T(8,128)(2,1)} %copy.101.k_ref, bf16[1024,768]{1,0:T(8,128)(2,1)} %slice.363.v_ref, bf16[1024,768]{1,0:T(8,128)(2,1)} %convolution_convert_fusion.3.d_ref, ...), custom_call_target="tpu_custom_call" | custom-call | flops 6442450944 | bytes 18874368 | tf_op jit(solution)/shard_map/attention_backward/pallas_call | solution.py:195
  446.9 12.1 %multiply_subtract_fusion = (f32[1024,12,32]{0,2,1:T(8,128)}, bf16[1024,12,32]{0,2,1:T(8,128)(2,1)S(1)}, bf16[1024,12,32]{0,2,1:T(8,128)(2,1)S(1)}, bf16[1024,12,32]{0,2,1:T(8,128)(2,1)S(1)}) fusion(f32[1024,12,64]{0,2,1:T(8,128)} %bitcast.72, f32[1024,12,64]{0,2,1:T(8,128)} %bitcast.74, f32[1024,12,64]{0,2,1:T(8,128)} %bitcast.69, ...), kind=kLoop, calls=%fused_computation.68 | loop fusion | flops 13762560 | bytes 16526336 | tf_op jit(solution)/shard_map/sub | solution.py:413
  462.0 8.3 %multiply_reduce_fusion.6 = (bf16[12,32]{1,0:T(8,128)(2,1)S(1)}, bf16[12,32]{1,0:T(8,128)(2,1)S(1)}, bf16[1024,12,32]{0,2,1:T(8,128)(2,1)S(1)}) fusion(f32[1024,12,32]{0,2,1:T(8,128)} %get-tuple-element.135, f32[1024]{0:T(1024)S(1)} %copy-done.21, f32[1024]{0:T(1024)S(1)} %copy-done.23, f32[1024,12,64]{0,2,1:T(8,128)} %bitcast.73, ...), kind=kLoop, calls=%fused_computation.67 | loop fusion | flops 4717824 | bytes 5517824 | tf_op jit(solution)/shard_map/reduce_sum | solution.py:419
  478.5 8.5 %fusion.70 = (bf16[768]{0:T(1024)(128)(2,1)S(1)}, f32[1024,768]{1,0:T(8,128)}) fusion(bf16[768,2304]{1,0:T(8,128)(2,1)} %all-gather.7.cloned.1.call-done, bf16[1024,768]{1,0:T(8,128)(2,1)} %copy-done.12, bf16[1024,768]{1,0:T(8,128)(2,1)} %copy.114, bf16[1024,768]{1,0:T(8,128)(2,1)S(1)} %copy.113), kind=kOutput, calls=%fused_computation.178 | convolution fusion | flops 3638820096 | bytes 11404800 | tf_op jit(solution)/shard_map/dot_general | solution.py:31
  494.2 6.5 convolution_convert_fusion.2
  502.4 16.6 %concatenate.67 = bf16[32,80,768]{2,1,0:T(8,128)(2,1)} concatenate(bf16[32,24,768]{2,1,0:T(8,128)(2,1)} %bitcast.81, bf16[32,24,768]{2,1,0:T(8,128)(2,1)} %bitcast.80, bf16[32,24,768]{2,1,0:T(8,128)(2,1)S(1)} %bitcast.79, bf16[32,1,768]{2,1,0:T(2,128)(2,1)S(1)} %copy.117, bf16[32,7,768]{2,1,0:T(8,128)(2,1)S(1)} %broadcast.388), dimensions={1} | concatenate | bytes 7864320 | tf_op jit(solution)/shard_map/concatenate | solution.py:265
  522.8 10.2 %add_convert_fusion = bf16[1024,768]{0,1:T(8,128)(2,1)} fusion(f32[1024,768]{0,1:T(8,128)} %copy-done.4, bf16[1024,3072]{1,0:T(8,128)(2,1)} %get-tuple-element.180, bf16[3072,768]{1,0:T(8,128)(2,1)} %all-gather.13.cloned.1.call-done, f32[768]{0:T(1024)S(1)} %reshape.837), kind=kOutput, calls=%fused_computation.55 | convolution fusion | flops 4834197504 | bytes 15731712 | tf_op jit(solution)/shard_map/dot_general | solution.py:21
  542.3 68.6 %all-to-all-done = bf16[32,80,768]{2,1,0:T(8,128)(2,1)} async-done(((bf16[32,80,768]{2,1,0:T(8,128)(2,1)}), bf16[32,80,768]{2,1,0:T(8,128)(2,1)}, u32[]{:S(2)}, u32[]{:S(2)}) %all-to-all-start) | async-done | bytes 3932192 | tf_op jit(solution)/shard_map/all_to_all | solution.py:294
  613.7 9.3 %all_gather.30 = f32[320,768]{1,0:T(8,128)S(1)} all-gather(f32[80,768]{1,0:T(8,128)S(1)} %convert_reduce_fusion), channel_id=1, replica_groups=mesh['fsdp'=8,'dp'=4] {'dp'}, dimensions={0}, use_global_device_ids=true | all-gather | bytes 1228800 | tf_op jit(solution)/shard_map/all_gather | solution.py:296
  648.3 20.7 %all-reduce.3 = (f32[]{:T(128)}, f32[]{:T(128)}) all-reduce(f32[]{:T(128)} %get-tuple-element.109, f32[]{:T(128)S(6)} %add.223), channel_id=1, replica_groups=mesh['fsdp'=8,'dp'=4] {'fsdp'}, use_global_device_ids=true, to_apply=%region_25.26 | all-reduce | flops 2 | bytes 16 | tf_op jit(solution)/shard_map/psum | solution.py:471
  (199 shorter events, 131.0 us)
Async XLA Ops:
  7.2 56.5 %copy-start.8 = (bf16[1024,768]{1,0:T(8,128)(2,1)S(1)}, bf16[1024,768]{1,0:T(8,128)(2,1)}, u32[]{:S(2)}) copy-start(bf16[1024,768]{1,0:T(8,128)(2,1)} %param.31) | copy-start | bytes 4718596
  7.2 67.0 %all-gather.7.cloned.1.call-start = ((), (), s32[]{:S(2)}) async-start(), calls=%async_computation.2 | async-start | bytes 3649536 | tf_op jit(solution)/shard_map/all_gather | solution.py:233
  9.0 148.2 %all-gather.9.cloned.1.call-start = ((), (), s32[]{:S(2)}) async-start(), calls=%async_computation.3 | async-start | bytes 1216512 | tf_op jit(solution)/shard_map/all_gather | solution.py:233
  10.5 185.5 %all-gather.11.cloned.1.call-start = ((), (), s32[]{:S(2)}) async-start(), calls=%async_computation.4 | async-start | bytes 4866048 | tf_op jit(solution)/shard_map/all_gather | solution.py:233
  11.2 250.0 %all-gather.13.cloned.1.call-start = ((), (), s32[]{:S(2)}) async-start(), calls=%async_computation.5 | async-start | bytes 4866048 | tf_op jit(solution)/shard_map/all_gather | solution.py:233
  12.9 520.1 %reduce-scatter.2.cloned.1.call-start = ((), (), s32[]{:S(2)}) async-start(), calls=%async_computation.6 | async-start | bytes 11354112 | tf_op jit(solution)/shard_map/reduce_scatter | solution.py:285
  65.7 91.5 %copy-start.2 = (bf16[1024,768]{0,1:T(8,128)(2,1)}, bf16[1024,768]{0,1:T(8,128)(2,1)S(1)}, u32[]{:S(2)}) copy-start(bf16[1024,768]{0,1:T(8,128)(2,1)S(1)} %copy.97) | copy-start | bytes 4718596
  66.0 14.6 %copy-start.18 = (f32[1024]{0:T(1024)}, f32[1024]{0:T(1024)S(1)}, u32[]{:S(2)}) copy-start(f32[1024]{0:T(1024)S(1)} %broadcast_multiply_fusion.5) | copy-start | bytes 12292
  66.4 14.1 %copy-start.24 = (f32[1024]{0:T(1024)}, f32[1024]{0:T(1024)S(1)}, u32[]{:S(2)}) copy-start(f32[1024]{0:T(1024)S(1)} %add_rsqrt_fusion.1) | copy-start | bytes 12292
  66.5 14.0 %copy-start.26 = (f32[768]{0:T(1024)}, f32[768]{0:T(1024)S(1)}, u32[]{:S(2)}) copy-start(f32[768]{0:T(1024)S(1)} %reshape.830) | copy-start | bytes 9220
  66.6 14.0 %copy-start.31 = (f32[768]{0:T(1024)}, f32[768]{0:T(1024)S(1)}, u32[]{:S(2)}) copy-start(f32[768]{0:T(1024)S(1)} %reshape.831) | copy-start | bytes 9220
  66.8 25.3 %copy-start.14 = (f32[12,32]{1,0:T(8,128)}, f32[12,32]{1,0:T(8,128)S(1)}, u32[]{:S(2)}) copy-start(f32[12,32]{1,0:T(8,128)S(1)} %mul.369) | copy-start | bytes 4612
  66.9 25.3 %copy-start.16 = (f32[12,32]{1,0:T(8,128)}, f32[12,32]{1,0:T(8,128)S(1)}, u32[]{:S(2)}) copy-start(f32[12,32]{1,0:T(8,128)S(1)} %mul.374) | copy-start | bytes 4612
  67.2 13.4 %copy-start.29 = (s32[1024]{0:T(1024)}, s32[1024]{0:T(1024)S(1)}, u32[]{:S(2)}) copy-start(s32[1024]{0:T(1024)S(1)} %get-tuple-element.172) | copy-start | bytes 12292
  67.2 24.9 %copy-start.20 = (f32[1024]{0:T(1024)}, f32[1024]{0:T(1024)S(1)}, u32[]{:S(2)}) copy-start(f32[1024]{0:T(1024)S(1)} %get-tuple-element.165) | copy-start | bytes 12292
  67.2 24.9 %copy-start.22 = (f32[1024]{0:T(1024)}, f32[1024]{0:T(1024)S(1)}, u32[]{:S(2)}) copy-start(f32[1024]{0:T(1024)S(1)} %get-tuple-element.166) | copy-start | bytes 12292
  162.7 98.6 %copy-start.9 = (bf16[1024,768]{1,0:T(8,128)(2,1)S(1)}, bf16[1024,768]{1,0:T(8,128)(2,1)}, u32[]{:S(2)}) copy-start(bf16[1024,768]{1,0:T(8,128)(2,1)} %param.31) | copy-start | bytes 4718596
  261.3 11.9 %copy-start.5 = (f32[1024,768]{0,1:T(8,128)S(1)}, f32[1024,768]{0,1:T(8,128)}, u32[]{:S(2)}) copy-start(f32[1024,768]{0,1:T(8,128)} %copy-done.4) | copy-start | bytes 9437188
  273.2 7.1 %copy-start.34 = (bf16[768,3072]{1,0:T(8,128)(2,1)S(1)}, bf16[768,3072]{1,0:T(8,128)(2,1)}, u32[]{:S(2)}) copy-start(bf16[768,3072]{1,0:T(8,128)(2,1)} %all-gather.11.cloned.1.call-done) | copy-start | bytes 14155780
  319.3 48.6 %copy-start.35 = (bf16[768,768]{1,0:T(8,128)(2,1)S(1)}, bf16[768,768]{1,0:T(8,128)(2,1)}, u32[]{:S(2)}) copy-start(bf16[768,768]{1,0:T(8,128)(2,1)} %all-gather.9.cloned.1.call-done) | copy-start | bytes 3538948
  462.0 16.5 %copy-start.10 = (bf16[1024,768]{1,0:T(8,128)(2,1)}, bf16[1024,768]{1,0:T(8,128)(2,1)S(1)}, u32[]{:S(2)}) copy-start(bf16[1024,768]{1,0:T(8,128)(2,1)S(1)} %copy.113) | copy-start | bytes 4718596
  519.0 92.0 %all-to-all-start = ((bf16[32,80,768]{2,1,0:T(8,128)(2,1)}), bf16[32,80,768]{2,1,0:T(8,128)(2,1)}, u32[]{:S(2)}, u32[]{:S(2)}) async-start(bf16[32,80,768]{2,1,0:T(8,128)(2,1)} %concatenate.67), calls=%async_computation | async-start | bytes 7864320 | tf_op jit(solution)/shard_map/all_to_all | solution.py:294
  522.7 108.5 %all-gather.15.cloned.1.call-start = ((), (), s32[]{:S(2)}) async-start(), calls=%async_computation.7 | async-start | bytes 1720320 | tf_op jit(solution)/shard_map/all_gather | solution.py:288
  628.2 45.2 %copy-start.1 = (bf16[96,3072]{1,0:T(8,128)(2,1)S(1)}, bf16[96,3072]{1,0:T(8,128)(2,1)}, u32[]{:S(2)}) copy-start(bf16[96,3072]{1,0:T(8,128)(2,1)} %param.26) | copy-start | bytes 1769476
  (19 other events, 66.0 us)
Sparse Core Ops, SparseCore 0:
  11.5 62.7 all-gather.6
  77.1 52.6 all-gather.8
  133.3 62.6 all-gather.10
  199.3 61.9 all-gather.12
  372.5 142.3 reduce-scatter.1
  533.2 26.0 all-gather.14

commit v4 on v3

--- a/solution.py
+++ b/solution.py
@@ -218,19 +218,24 @@
     return tuple(jnp.concatenate(parts, axis=0) for parts in zip(*outs))
 
 
-def square_sums(pieces):
-    freq_sq = jnp.sum(pieces[12] * pieces[12])
-    other_sq = jnp.float32(0.0)
-    for member in pieces[:12]:
-        other_sq = other_sq + jnp.sum(member * member)
-    return (freq_sq, other_sq)
-
-
-def gather_weight(shard):
-    pieces = lax.psum(1, "dp")
-    part = shard.shape[0] // pieces
-    mine = lax.dynamic_slice_in_dim(shard, lax.axis_index("dp") * part, part, 0)
-    return lax.all_gather(mine, ("fsdp", "dp"), axis=0, tiled=True)
+def quarter(shard):
+    part = shard.shape[0] // lax.psum(1, "dp")
+    return lax.dynamic_slice_in_dim(shard, lax.axis_index("dp") * part, part, 0)
+
+
+def gather_side_by_side(left, right):
+    joined = jnp.concatenate([quarter(left), quarter(right)], axis=1)
+    whole = lax.all_gather(joined, ("fsdp", "dp"), axis=0, tiled=True)
+    return whole[:, : left.shape[1]], whole[:, left.shape[1] :]
+
+
+def gather_stacked(top, bottom):
+    upper = quarter(top)
+    lower = quarter(bottom).reshape(-1, top.shape[1])
+    whole = lax.all_gather(jnp.concatenate([upper, lower], axis=0)[None], ("fsdp", "dp"), axis=0, tiled=True)
+    first = whole[:, : upper.shape[0]].reshape(-1, top.shape[1])
+    second = whole[:, upper.shape[0] :].reshape(-1, bottom.shape[1])
+    return first, second
 
 
 def gather_small(vectors):
@@ -257,21 +262,20 @@
     flat = jnp.pad(flat, ((0, 0), (0, small_rows * width - small)))
     parts.append(flat.reshape(blocks, small_rows, width).astype(jnp.bfloat16))
     rows = [p.shape[1] for p in parts]
-    total = sum(rows)
-    padded = -(-total // PACK_ROWS) * PACK_ROWS
-    if padded > total:
-        parts.append(jnp.zeros((blocks, padded - total, width), jnp.bfloat16))
-    layout = (rows, [v.shape[0] // blocks for v in vectors])
+    spans = [-(-r // PACK_ROWS) * PACK_ROWS if r >= PACK_ROWS else r for r in rows]
+    spans[-1] += -sum(spans) % PACK_ROWS
+    parts = [jnp.pad(p, ((0, 0), (0, s - r), (0, 0))) if s > r else p for p, r, s in zip(parts, rows, spans)]
+    layout = (rows, spans, [v.shape[0] // blocks for v in vectors])
     return jnp.concatenate(parts, axis=1), layout
 
 
 def unpack_rows(owned, layout):
-    rows, vector_sizes = layout
+    rows, spans, vector_sizes = layout
     groups = owned.shape[0]
     out, at = [], 0
-    for r in rows[:-1]:
+    for r, s in zip(rows[:-1], spans[:-1]):
         out.append(owned[:, at : at + r, :].reshape(groups * r, owned.shape[2]).astype(jnp.float32))
-        at += r
+        at += s
     flat = owned[:, at : at + rows[-1], :].reshape(groups, -1)
     vectors, at = [], 0
     for n in vector_sizes:
@@ -286,7 +290,7 @@
         packed.reshape(blocks * padded, width), ("fsdp", "dp"), scatter_dimension=0, tiled=True
     )
     owned = lax.all_gather(mine, "dp", axis=0, tiled=True)
-    return unpack_rows(owned.reshape(-1, padded, width), layout)
+    return unpack_rows(owned.reshape(-1, padded, width), layout), mine
 
 
 def sum_by_exchange(packed, layout):
@@ -294,7 +298,19 @@
     received = lax.all_to_all(packed, ("fsdp", "dp"), 0, 0, tiled=False)
     mine = jnp.sum(received.astype(jnp.float32), axis=0)
     owned = lax.all_gather(mine, "dp", axis=0, tiled=True)
-    return unpack_rows(owned.reshape(-1, padded, width), layout)
+    return unpack_rows(owned.reshape(-1, padded, width), layout), mine
+
+
+def square_sums_of_block(mine, layout, last_vectors):
+    rows, spans, vector_sizes = layout
+    values = mine.astype(jnp.float32)
+    small_at = sum(spans[:-1])
+    flat = values[small_at : small_at + rows[-1]].reshape(-1)
+    split = sum(vector_sizes[: len(vector_sizes) - last_vectors])
+    end = sum(vector_sizes)
+    last = jnp.sum(flat[split:end] * flat[split:end])
+    rest = jnp.sum(values[:small_at] * values[:small_at]) + jnp.sum(flat[:split] * flat[:split])
+    return last, rest
 
 
 def shards(
@@ -318,18 +334,20 @@
     small_local = (ln1_gain, ln1_bias, qkv_bias, out_bias, ln2_gain, ln2_bias, fc1_bias, fc2_bias, frequencies)
     (g_ln1_gain, g_ln1_bias, g_qkv_bias, g_out_bias, g_ln2_gain, g_ln2_bias, g_fc1_bias, g_fc2_bias,
      g_frequencies) = gather_small(small_local)
+    g_qkv_weight, g_out_weight = gather_side_by_side(qkv_weight, out_weight)
+    g_fc1_weight, g_fc2_weight = gather_stacked(fc1_weight, fc2_weight)
     block_parameters = (
         g_ln1_gain,
         g_ln1_bias,
-        gather_weight(qkv_weight),
+        g_qkv_weight,
         g_qkv_bias,
-        gather_weight(out_weight),
+        g_out_weight,
         g_out_bias,
         g_ln2_gain,
         g_ln2_bias,
-        gather_weight(fc1_weight),
+        g_fc1_weight,
         g_fc1_bias,
-        gather_weight(fc2_weight),
+        g_fc2_weight,
         g_fc2_bias,
         g_frequencies,
     )
@@ -401,7 +419,7 @@
         [fc2_bias_grad, fc1_bias_grad, out_bias_grad, second_norm_gain_gradient, ln2_bias_grad],
     )
     early_packed, d_mixed = lax.optimization_barrier((early_packed, d_mixed))
-    early_mats, early_vecs = sum_on_sparse_core(early_packed, early_layout)
+    (early_mats, early_vecs), early_mine = sum_on_sparse_core(early_packed, early_layout)
     d_qrot, d_krot, d_value = attention_bins_back(q_low, k_low, v_low, d_mixed, log_total, segment)
     d_qrot = d_qrot.reshape(row_count, H, HD)
     d_krot = d_krot.reshape(row_count, H, HD)
@@ -445,7 +463,10 @@
         column_chunks(qkv_weight_grad, width),
         [qkv_bias_grad, first_norm_gain_gradient, ln1_bias_grad, frequencies_grad],
     )
-    late_mats, late_vecs = sum_by_exchange(late_packed, late_layout)
+    (late_mats, late_vecs), late_mine = sum_by_exchange(late_packed, late_layout)
+    _, early_sq = square_sums_of_block(early_mine, early_layout, 0)
+    freq_sq, late_sq = square_sums_of_block(late_mine, late_layout, 1)
+    freq_sq, other_sq = lax.psum((freq_sq, early_sq + late_sq), ("fsdp", "dp"))
     fc2_weight_g = early_mats[0]
     fc1_weight_g = jnp.concatenate(early_mats[1:-1], axis=1)
     out_weight_g = early_mats[-1]
@@ -467,8 +488,6 @@
         fc2_bias_g,
         frequencies_g,
     )
-    freq_sq, other_sq = square_sums(pieces)
-    freq_sq, other_sq = lax.psum((freq_sq, other_sq), "fsdp")
     return (
         block_out,
         tokens_grad,

time: 696 us -> 661 us (0.950)
  blocking collectives: 69 us -> 212 us
  waiting for transfers between devices: 122 us -> 17.9 us
  local copies, waits for them, and re-layouts: 142 us -> 101 us
  matrix products: 130 us -> 114 us
    all_to_all x0 -> x1, blocking collectives: none -> 135 us  [sum_by_exchange(): received = lax.all_to_all(packed, ('fsdp', 'dp'), 0, 0, tiled=False)]
    all_to_all x1 -> x0, waiting for transfers between devices: 68.6 us -> none  [sum_by_exchange(): received = lax.all_to_all(packed, ('fsdp', 'dp'), 0, 0, tiled=False)]
    concatenate x2 -> x1, local copies, waits for them, and re-layouts: 65.2 us -> 0.99 us  [pack_rows(): return (jnp.concatenate(parts, axis=1), layout)]
    all_gather x4 -> x3, waiting for transfers between devices: 53.5 us -> 17.3 us  [the longest x1 17.3 us: gather_side_by_side(): whole = lax.all_gather(joined, ('fsdp', 'dp'), axis=0, tiled=True)]
    psum x1, blocking collectives: 20.7 us -> 38.5 us  [shards(): freq_sq, other_sq = lax.psum((freq_sq, early_sq + late_sq), ('fsdp', 'dp'))]
    unnamed x81 -> x123, local copies, waits for them, and re-layouts: 13.7 us -> 27.3 us
    dot_general x4, matrix products: 70.1 us -> 58.8 us  [matmul(): return jnp.dot(left, right, preferred_element_type=jnp.float32)]
    all_gather x1 -> x0, blocking collectives: 9.35 us -> none  [sum_by_exchange(): owned = lax.all_gather(mine, 'dp', axis=0, tiled=True)]
  transfers between devices with their start and end apart: 7 -> 5, of which waited for: 4 -> 1; matrix products, arithmetic and copies ran while one was open for 32% -> 22% of each run, Pallas kernels for 17% -> 18%
where the time goes in v4:
time: 661 us; the launch traced here: 651 us
  blocking collectives  212 us (32%)
  Pallas kernels  115 us (17%)
  matrix products  114 us (17%)
  local copies, waits for them, and re-layouts  101 us (15%)
  other arithmetic  68.5 us (10%)
  between operations  21.8 us (3%)
  waiting for transfers between devices  17.9 us (3%)
    all_to_all x1, blocking collectives, sum_by_exchange(): received = lax.all_to_all(packed, ('fsdp', 'dp'), 0, 0, tiled=False)  135 us
    pallas_call x1, Pallas kernels, attention_backward(): pl.pallas_call(attention_backward_kernel, grid=(width // pair,), in_specs...  67.2 us
    dot_general x4, matrix products, matmul(): return jnp.dot(left, right, preferred_element_type=jnp.float32)  58.8 us
    pallas_call x1, Pallas kernels, attention_forward(): pl.pallas_call(attention_forward_kernel, grid=(width // pair,), in_specs=...  47.5 us
    unnamed x1, blocking collectives  39 us
    psum x1, blocking collectives, shards(): freq_sq, other_sq = lax.psum((freq_sq, early_sq + late_sq), ('fsdp', 'dp'))  38.5 us
    dot_general x4, matrix products, matmul_right_t(): lax.dot_general(left, right, (((1,), (1,)), ((), ())), preferred_element_...  30.9 us
    unnamed x123, local copies, waits for them, and re-layouts  27.3 us
  transfers between devices with their start and end apart: 5, of which 1 were waited for; matrix products, arithmetic and copies ran while one was open for 22% of the time, Pallas kernels for 18%

profile of v4, /device:TPU:0, one launch (start us, length us, event | category | flops | bytes accessed | tf_op | source)
XLA Modules:
  0.0 650.6 jit_solution(1503235409243332242)
XLA Ops:
  15.5 39.0 %all-reduce.12 = bf16[10752]{0:T(1024)(128)(2,1)S(1)} all-reduce(bf16[10752]{0:T(1024)(128)(2,1)S(1)} %dynamic-update-slice), channel_id=2, replica_groups=mesh['fsdp'=8,'dp'=4] {'fsdp'}, use_global_device_ids=true, to_apply=%add.12 | all-reduce | flops 10752 | bytes 43008
  60.5 17.3 %all-gather.7.cloned.1.call-done = bf16[768,3072]{1,0:T(8,128)(2,1)} async-done(((bf16[24,3072]{1,0:T(8,128)(2,1)}), bf16[768,3072]{1,0:T(8,128)(2,1)}) %all-gather.7.cloned.1.call-update) | async-done | bytes 4718608 | tf_op jit(solution)/shard_map/all_gather | solution.py:228
  77.8 6.3 convolution_add_fusion
  95.8 10.8 %fusion.73 = (bf16[1024,12,32]{0,2,1:T(8,128)(2,1)S(1)}, bf16[1024,12,32]{0,2,1:T(8,128)(2,1)S(1)}, bf16[1024,12,32]{0,2,1:T(8,128)(2,1)S(1)}, bf16[1024,12,32]{0,2,1:T(8,128)(2,1)S(1)}) fusion(f32[1024,12,64]{0,2,1:T(8,128)} %bitcast.69, f32[12,32]{1,0:T(8,128)S(1)} %mul.342, f32[1024]{0:T(1024)S(1)} %get-tuple-element.155, f32[12,32]{1,0:T(8,128)S(1)} %mul.337, ...), kind=kLoop, calls=%fused_computation.190 | loop fusion | flops 7471104 | bytes 9448448 | tf_op jit(solution)/shard_map/convert.62
  113.9 47.5 %attention_forward.1 = (bf16[1024,768]{1,0:T(8,128)(2,1)}, f32[1024,768]{1,0:T(8,128)}) custom-call(bf16[1024,768]{1,0:T(8,128)(2,1)} %copy.100.q_ref, bf16[1024,768]{1,0:T(8,128)(2,1)} %copy.101.k_ref, bf16[1024,768]{1,0:T(8,128)(2,1)} %slice.424.v_ref, s32[1024,1]{1,0:T(8,128)} %copy.102.seg_r_ref, s32[1,1024]{1,0:T(1,128)} %bitcast.112), custom_call_target="tpu_custom_call" | custom-call | flops 3221225472 | bytes 9437184 | tf_op jit(solution)/shard_map/attention_forward/pallas_call | solution.py:175
  166.9 8.4 %fusion.79 = (bf16[32,24,3072]{2,1,0:T(8,128)(2,1)}, bf16[32,24,3072]{2,1,0:T(8,128)(2,1)}) fusion(bf16[32,48,3072]{2,1,0:T(8,128)(2,1)} %bitcast.77), kind=kLoop, calls=%fused_computation.194 | loop fusion | bytes 18874368 | tf_op jit(solution)/shard_map/slice | solution.py:237
  175.3 8.5 %reshape.825 = bf16[3072,768]{1,0:T(8,128)(2,1)} reshape(bf16[32,24,3072]{2,1,0:T(8,128)(2,1)} %get-tuple-element.115) | data formatting | bytes 9437184 | tf_op jit(solution)/shard_map/reshape | solution.py:237
  183.8 39.0 %fusion.2 = (bf16[1024,3072]{1,0:T(8,128)(2,1)}, f32[1024,3072]{1,0:T(8,128)}) fusion(f32[3072]{0:T(1024)S(1)} %reshape.856, bf16[768,3072]{1,0:T(8,128)(2,1)} %bitcast.92, f32[1024,768]{0,1:T(8,128)} %copy-done.5, f32[768]{0:T(1024)S(1)} %reshape.855, f32[768]{0:T(1024)S(1)} %reshape.854, f32[1024]{0:T(1024)S(1)} %add_rsqrt_fusion, ...), kind=kOutput, calls=%fused_computation.8 | convolution fusion | flops 5043388416 | bytes 26765312 | tf_op jit(solution)/shard_map/dot_general | solution.py:21
  222.8 11.8 %fusion.88 = (bf16[3072]{0:T(1024)(128)(2,1)S(1)}, bf16[1024,3072]{1,0:T(8,128)(2,1)S(1)}) fusion(f32[1024,3072]{1,0:T(8,128)} %get-tuple-element.170, f32[3072]{0:T(1024)S(1)} %reshape.856, bf16[3072,768]{1,0:T(8,128)(2,1)S(1)} %copy-done.15, bf16[1024,768]{1,0:T(8,128)(2,1)S(1)} %copy-done.12), kind=kOutput, calls=%fused_computation.203 | convolution fusion | flops 4869583872 | bytes 25184256 | tf_op jit(solution)/shard_map/dot_general | solution.py:31
  234.6 6.7 %fusion.89 = (bf16[768]{0:T(1024)(128)(2,1)S(1)}, f32[1024,768]{1,0:T(8,128)}) fusion(bf16[1024,3072]{1,0:T(8,128)(2,1)S(1)} %get-tuple-element.172, bf16[768,3072]{1,0:T(8,128)(2,1)S(1)} %bitcast.93), kind=kOutput, calls=%fused_computation.204 | convolution fusion | flops 4832623616 | bytes 14157312 | tf_op jit(solution)/shard_map/dot_general | solution.py:31
  241.3 7.0 %convolution_convert_fusion = bf16[768,3072]{1,0:T(8,128)(2,1)} fusion(bf16[1024,3072]{1,0:T(8,128)(2,1)S(1)} %get-tuple-element.172, f32[1024,768]{0,1:T(8,128)S(1)} %copy-done.6, f32[768]{0:T(1024)S(1)} %reshape.855, f32[768]{0:T(1024)S(1)} %reshape.854, f32[1024]{0:T(1024)S(1)} %add_rsqrt_fusion, f32[1024]{0:T(1024)S(1)} %broadcast_multiply_fusion.4), kind=kOutput, calls=%fused_computation.43 | convolution fusion | flops 4838129664 | bytes 14170112 | tf_op jit(solution)/shard_map/dot_general | solution.py:25
  251.9 3.8 multiply_reduce_fusion
  255.7 8.5 %convolution_convert_fusion.1 = bf16[3072,768]{1,0:T(8,128)(2,1)S(1)} fusion(bf16[1024,3072]{1,0:T(8,128)(2,1)} %get-tuple-element.169, bf16[1024,768]{1,0:T(8,128)(2,1)S(1)} %copy-done.12), kind=kOutput, calls=%fused_computation.44 | convolution fusion | flops 4834197504 | bytes 12582912 | tf_op jit(solution)/shard_map/dot_general | solution.py:25
  287.4 3.9 convolution_convert_fusion.3.d_ref
  291.3 67.2 %attention_backward.1 = (f32[1024,768]{1,0:T(8,128)}, f32[1024,768]{1,0:T(8,128)}, f32[1024,768]{1,0:T(8,128)}) custom-call(bf16[1024,768]{1,0:T(8,128)(2,1)} %copy.100.q_ref, bf16[1024,768]{1,0:T(8,128)(2,1)} %copy.101.k_ref, bf16[1024,768]{1,0:T(8,128)(2,1)} %slice.424.v_ref, bf16[1024,768]{1,0:T(8,128)(2,1)} %convolution_convert_fusion.3.d_ref, ...), custom_call_target="tpu_custom_call" | custom-call | flops 6442450944 | bytes 18874368 | tf_op jit(solution)/shard_map/attention_backward/pallas_call | solution.py:195
  360.6 4.1 copy.112
  368.4 13.6 %multiply_subtract_fusion = (f32[1024,12,32]{0,2,1:T(8,128)S(1)}, bf16[1024,12,32]{0,2,1:T(8,128)(2,1)S(1)}, bf16[1024,12,32]{0,2,1:T(8,128)(2,1)}, bf16[1024,12,32]{0,2,1:T(8,128)(2,1)S(1)}) fusion(f32[1024,12,64]{0,2,1:T(8,128)} %bitcast.73, f32[1024,12,64]{0,2,1:T(8,128)} %bitcast.76, f32[1024,12,64]{0,2,1:T(8,128)} %bitcast.72, ...), kind=kLoop, calls=%fused_computation.86 | loop fusion | flops 13762560 | bytes 16526336 | tf_op jit(solution)/shard_map/sub | solution.py:431
  382.0 6.4 multiply_reduce_fusion.6
  397.3 8.5 %fusion.90 = (bf16[768]{0:T(1024)(128)(2,1)S(1)}, f32[1024,768]{1,0:T(8,128)}) fusion(bf16[768,3072]{1,0:T(8,128)(2,1)} %all-gather.7.cloned.1.call-done, bf16[1024,768]{1,0:T(8,128)(2,1)S(1)} %convert.125, bf16[1024,768]{1,0:T(8,128)(2,1)} %copy.114, bf16[1024,768]{1,0:T(8,128)(2,1)} %copy.113), kind=kOutput, calls=%fused_computation.205 | convolution fusion | flops 3638820096 | bytes 11404800 | tf_op jit(solution)/shard_map/dot_general | solution.py:31
  416.1 6.4 convolution_convert_fusion.2
  423.2 134.8 %all_to_all.5 = bf16[32,112,768]{2,1,0:T(8,128)(2,1)S(1)} all-to-all(bf16[32,112,768]{2,1,0:T(8,128)(2,1)S(1)} %fusion.23), channel_id=1, replica_groups=mesh['fsdp'=8,'dp'=4] {'fsdp','dp'}, dimensions={0} | all-to-all | bytes 11010048 | tf_op jit(solution)/shard_map/all_to_all | solution.py:298
  560.2 10.1 %add_convert_fusion = bf16[1024,768]{0,1:T(8,128)(2,1)} fusion(f32[1024,768]{0,1:T(8,128)} %copy-done.5, bf16[1024,3072]{1,0:T(8,128)(2,1)} %get-tuple-element.169, bf16[3072,768]{1,0:T(8,128)(2,1)} %reshape.825, f32[768]{0:T(1024)S(1)} %reshape.857), kind=kOutput, calls=%fused_computation.70 | convolution fusion | flops 4834197504 | bytes 15731712 | tf_op jit(solution)/shard_map/dot_general | solution.py:21
  572.9 5.1 fusion.37
  592.3 38.5 %all-reduce.13 = (f32[]{:T(128)}, f32[]{:T(128)}) all-reduce(f32[]{:T(128)} %fusion.68, f32[]{:T(128)S(6)} %add.211), channel_id=1, replica_groups=mesh['fsdp'=8,'dp'=4] {'fsdp','dp'}, use_global_device_ids=true, to_apply=%region_25.26 | all-reduce | flops 2 | bytes 16 | tf_op jit(solution)/shard_map/psum | solution.py:469
  (243 shorter events, 115.6 us)
Async XLA Ops:
  7.2 70.6 %all-gather.7.cloned.1.call-start = ((), (), s32[]{:S(2)}) async-start(), calls=%async_computation.2 | async-start | bytes 4866048 | tf_op jit(solution)/shard_map/all_gather | solution.py:228
  9.8 157.1 %all-gather.13.cloned.1.call-start = ((), (), s32[]{:S(2)}) async-start(), calls=%async_computation.6 | async-start | bytes 9732096 | tf_op jit(solution)/shard_map/all_gather | solution.py:235
  11.8 548.0 %reduce-scatter.2.cloned.1.call-start = ((), (), s32[]{:S(2)}) async-start(), calls=%async_computation.4 | async-start | bytes 13787136 | tf_op jit(solution)/shard_map/reduce_scatter | solution.py:289
  13.5 44.0 %copy-start.39 = (s32[5,3]{0,1:T(4,128)S(1)}, s32[5,3]{0,1:T(4,128)}, u32[]{:S(2)}) copy-start(s32[5,3]{0,1:T(4,128)} %param.17) | copy-start | bytes 184
  57.2 104.2 %copy-start.2 = (bf16[1024,768]{0,1:T(8,128)(2,1)}, bf16[1024,768]{0,1:T(8,128)(2,1)S(1)}, u32[]{:S(2)}) copy-start(bf16[1024,768]{0,1:T(8,128)(2,1)S(1)} %copy.97) | copy-start | bytes 4718596
  57.3 26.9 %copy-start.37 = (f32[768]{0:T(1024)}, f32[768]{0:T(1024)S(1)}, u32[]{:S(2)}) copy-start(f32[768]{0:T(1024)S(1)} %reshape.851) | copy-start | bytes 9220
  57.4 26.8 %copy-start.30 = (f32[768]{0:T(1024)}, f32[768]{0:T(1024)S(1)}, u32[]{:S(2)}) copy-start(f32[768]{0:T(1024)S(1)} %reshape.850) | copy-start | bytes 9220
  57.4 38.3 %copy-start.20 = (f32[12,32]{1,0:T(8,128)}, f32[12,32]{1,0:T(8,128)S(1)}, u32[]{:S(2)}) copy-start(f32[12,32]{1,0:T(8,128)S(1)} %mul.342) | copy-start | bytes 4612
  57.5 38.2 %copy-start.22 = (f32[12,32]{1,0:T(8,128)}, f32[12,32]{1,0:T(8,128)S(1)}, u32[]{:S(2)}) copy-start(f32[12,32]{1,0:T(8,128)S(1)} %mul.337) | copy-start | bytes 4612
  57.9 26.3 %copy-start.35 = (s32[1024]{0:T(1024)}, s32[1024]{0:T(1024)S(1)}, u32[]{:S(2)}) copy-start(s32[1024]{0:T(1024)S(1)} %get-tuple-element.161) | copy-start | bytes 12292
  57.9 37.9 %copy-start.26 = (f32[1024]{0:T(1024)}, f32[1024]{0:T(1024)S(1)}, u32[]{:S(2)}) copy-start(f32[1024]{0:T(1024)S(1)} %get-tuple-element.154) | copy-start | bytes 12292
  57.9 37.9 %copy-start.28 = (f32[1024]{0:T(1024)}, f32[1024]{0:T(1024)S(1)}, u32[]{:S(2)}) copy-start(f32[1024]{0:T(1024)S(1)} %get-tuple-element.155) | copy-start | bytes 12292
  60.1 24.1 %copy-start.24 = (f32[1024]{0:T(1024)}, f32[1024]{0:T(1024)S(1)}, u32[]{:S(2)}) copy-start(f32[1024]{0:T(1024)S(1)} %broadcast_multiply_fusion.5) | copy-start | bytes 12292
  60.5 23.7 %copy-start.32 = (f32[1024]{0:T(1024)}, f32[1024]{0:T(1024)S(1)}, u32[]{:S(2)}) copy-start(f32[1024]{0:T(1024)S(1)} %add_rsqrt_fusion.1) | copy-start | bytes 12292
  183.8 39.0 %copy-start.12 = (bf16[1024,768]{1,0:T(8,128)(2,1)S(1)}, bf16[1024,768]{1,0:T(8,128)(2,1)}, u32[]{:S(2)}) copy-start(bf16[1024,768]{1,0:T(8,128)(2,1)} %param.31) | copy-start | bytes 4718596
  183.8 39.0 %copy-start.15 = (bf16[3072,768]{1,0:T(8,128)(2,1)S(1)}, bf16[3072,768]{1,0:T(8,128)(2,1)}, u32[]{:S(2)}) copy-start(bf16[3072,768]{1,0:T(8,128)(2,1)} %reshape.825) | copy-start | bytes 14155780
  222.8 11.8 %copy-start.16 = (bf16[32,24,3072]{2,1,0:T(8,128)(2,1)S(1)}, bf16[32,24,3072]{2,1,0:T(8,128)(2,1)}, u32[]{:S(2)}) copy-start(bf16[32,24,3072]{2,1,0:T(8,128)(2,1)} %get-tuple-element.116) | copy-start | bytes 14155780
  291.3 292.6 %all-gather.9.cloned.1.call-start = ((), (), s32[]{:S(2)}) async-start(), calls=%async_computation.3 | async-start | bytes 1720320 | tf_op jit(solution)/shard_map/all_gather | solution.py:300
  360.6 36.8 %copy-start.13 = (bf16[1024,768]{1,0:T(8,128)(2,1)}, bf16[1024,768]{1,0:T(8,128)(2,1)S(1)}, u32[]{:S(2)}) copy-start(bf16[1024,768]{1,0:T(8,128)(2,1)S(1)} %convert.125) | copy-start | bytes 4718596
  368.3 13.6 %copy-start.4 = (f32[1024,768]{0,1:T(8,128)S(1)}, f32[1024,768]{0,1:T(8,128)}, u32[]{:S(2)}) copy-start(f32[1024,768]{0,1:T(8,128)} %copy.112) | copy-start | bytes 9437188
  559.6 72.5 %all-gather.11.cloned.1.call-start = ((), (), s32[]{:S(2)}) async-start(), calls=%async_computation.5 | async-start | bytes 2088960 | tf_op jit(solution)/shard_map/all_gather | solution.py:292
  572.9 7.7 %copy-start.17 = (f32[112,768]{1,0:T(8,128)S(1)}, f32[112,768]{1,0:T(8,128)}, u32[]{:S(2)}) copy-start(f32[112,768]{1,0:T(8,128)} %convert_reduce_fusion) | copy-start | bytes 1032196
  578.0 10.9 %copy-start.18 = (bf16[272,768]{1,0:T(8,128)(2,1)S(1)}, bf16[272,768]{1,0:T(8,128)(2,1)}, u32[]{:S(2)}) copy-start(bf16[272,768]{1,0:T(8,128)(2,1)} %reduce-scatter.2.cloned.1.call-done) | copy-start | bytes 1253380
  632.2 9.4 %copy-start.1 = (bf16[384,768]{1,0:T(8,128)(2,1)S(1)}, bf16[384,768]{1,0:T(8,128)(2,1)}, u32[]{:S(2)}) copy-start(bf16[384,768]{1,0:T(8,128)(2,1)} %param.28) | copy-start | bytes 1769476
  (34 other events, 133.2 us)
Sparse Core Ops, SparseCore 0:
  11.5 66.2 all-gather.6
  81.3 79.9 all-gather.12
  291.4 170.9 reduce-scatter.1
  559.8 16.2 all-gather.8
  577.4 20.1 all-gather.10

commit v5 on v4

--- a/solution.py
+++ b/solution.py
@@ -9,7 +9,6 @@
 HD = 64
 BIN = 1024
 Q_BLOCK = 256
-PACK_ROWS = 16
 
 
 norm_eps = 1e-06
@@ -248,35 +247,30 @@
     return out
 
 
-def column_chunks(matrix, width):
-    return [matrix[:, j * width : (j + 1) * width] for j in range(matrix.shape[1] // width)]
-
-
-def pack_rows(matrices, vectors):
+def pack_columns(matrices, vectors):
     blocks = lax.psum(1, ("fsdp", "dp"))
-    width = matrices[0].shape[1]
-    parts = [m.reshape(blocks, m.shape[0] // blocks, width).astype(jnp.bfloat16) for m in matrices]
+    rows = matrices[0].shape[0]
+    per_block = rows // blocks
     flat = jnp.concatenate([v.reshape(blocks, -1) for v in vectors], axis=1)
     small = flat.shape[1]
-    small_rows = -(-small // width)
-    flat = jnp.pad(flat, ((0, 0), (0, small_rows * width - small)))
-    parts.append(flat.reshape(blocks, small_rows, width).astype(jnp.bfloat16))
-    rows = [p.shape[1] for p in parts]
-    spans = [-(-r // PACK_ROWS) * PACK_ROWS if r >= PACK_ROWS else r for r in rows]
-    spans[-1] += -sum(spans) % PACK_ROWS
-    parts = [jnp.pad(p, ((0, 0), (0, s - r), (0, 0))) if s > r else p for p, r, s in zip(parts, rows, spans)]
-    layout = (rows, spans, [v.shape[0] // blocks for v in vectors])
+    small_cols = -(-small // per_block)
+    flat = jnp.pad(flat, ((0, 0), (0, small_cols * per_block - small)))
+    flat = flat.reshape(rows, small_cols)
+    padded_cols = -(-small_cols // 128) * 128
+    flat = jnp.pad(flat, ((0, 0), (0, padded_cols - small_cols)))
+    parts = [m.astype(jnp.bfloat16) for m in matrices] + [flat.astype(jnp.bfloat16)]
+    layout = ([m.shape[1] for m in matrices], small_cols, padded_cols, [v.shape[0] // blocks for v in vectors])
     return jnp.concatenate(parts, axis=1), layout
 
 
-def unpack_rows(owned, layout):
-    rows, spans, vector_sizes = layout
-    groups = owned.shape[0]
+def unpack_columns(owned, layout):
+    widths, small_cols, _, vector_sizes = layout
+    groups = lax.psum(1, "dp")
     out, at = [], 0
-    for r, s in zip(rows[:-1], spans[:-1]):
-        out.append(owned[:, at : at + r, :].reshape(groups * r, owned.shape[2]).astype(jnp.float32))
-        at += s
-    flat = owned[:, at : at + rows[-1], :].reshape(groups, -1)
+    for w in widths:
+        out.append(owned[:, at : at + w].astype(jnp.float32))
+        at += w
+    flat = owned[:, at : at + small_cols].reshape(groups, -1)
     vectors, at = [], 0
     for n in vector_sizes:
         vectors.append(flat[:, at : at + n].reshape(-1).astype(jnp.float32))
@@ -284,33 +278,34 @@
     return out, vectors
 
 
-def sum_on_sparse_core(packed, layout):
-    blocks, padded, width = packed.shape
-    mine = lax.psum_scatter(
-        packed.reshape(blocks * padded, width), ("fsdp", "dp"), scatter_dimension=0, tiled=True
-    )
-    owned = lax.all_gather(mine, "dp", axis=0, tiled=True)
-    return unpack_rows(owned.reshape(-1, padded, width), layout), mine
-
-
-def sum_by_exchange(packed, layout):
-    _, padded, width = packed.shape
-    received = lax.all_to_all(packed, ("fsdp", "dp"), 0, 0, tiled=False)
-    mine = jnp.sum(received.astype(jnp.float32), axis=0)
-    owned = lax.all_gather(mine, "dp", axis=0, tiled=True)
-    return unpack_rows(owned.reshape(-1, padded, width), layout), mine
-
-
 def square_sums_of_block(mine, layout, last_vectors):
-    rows, spans, vector_sizes = layout
+    widths, small_cols, _, vector_sizes = layout
     values = mine.astype(jnp.float32)
-    small_at = sum(spans[:-1])
-    flat = values[small_at : small_at + rows[-1]].reshape(-1)
+    at = sum(widths)
+    flat = values[:, at : at + small_cols].reshape(-1)
     split = sum(vector_sizes[: len(vector_sizes) - last_vectors])
     end = sum(vector_sizes)
     last = jnp.sum(flat[split:end] * flat[split:end])
-    rest = jnp.sum(values[:small_at] * values[:small_at]) + jnp.sum(flat[:split] * flat[:split])
+    rest = jnp.sum(values[:, :at] * values[:, :at]) + jnp.sum(flat[:split] * flat[:split])
     return last, rest
+
+
+def sum_on_sparse_core(packed, layout):
+    mine = lax.psum_scatter(packed, ("fsdp", "dp"), scatter_dimension=0, tiled=True)
+    owned = lax.all_gather(mine, "dp", axis=0, tiled=True)
+    return unpack_columns(owned, layout), mine
+
+
+def sum_by_exchange(packed, layout, carried):
+    blocks = lax.psum(1, ("fsdp", "dp"))
+    received = lax.all_to_all(packed, ("fsdp", "dp"), 0, 0, tiled=True)
+    mine = jnp.sum(received.reshape(blocks, -1, packed.shape[1]).astype(jnp.float32), axis=0)
+    freq_part, rest_part = square_sums_of_block(mine, layout, 1)
+    rest_part = rest_part + carried
+    extra = jnp.zeros((mine.shape[0], 128), jnp.float32).at[0, 0].set(freq_part).at[0, 1].set(rest_part)
+    owned = lax.all_gather(jnp.concatenate([mine, extra], axis=1), "dp", axis=0, tiled=True)
+    partials = jnp.sum(owned[:: mine.shape[0], packed.shape[1] : packed.shape[1] + 2], axis=0)
+    return unpack_columns(owned[:, : packed.shape[1]], layout), partials
 
 
 def shards(
@@ -413,9 +408,8 @@
     out_bias_grad = jnp.sum(d_att.astype(jnp.float32), axis=0)
     out_weight_grad = matmul_left_t(mixed, d_att)
     d_mixed = matmul_right_t(d_att, block_parameters[4]).astype(jnp.bfloat16)
-    width = out_weight_grad.shape[1]
-    early_packed, early_layout = pack_rows(
-        [fc2_weight_grad, *column_chunks(fc1_weight_grad, width), out_weight_grad],
+    early_packed, early_layout = pack_columns(
+        [fc2_weight_grad.reshape(fc1_weight_grad.shape[0], -1), fc1_weight_grad, out_weight_grad],
         [fc2_bias_grad, fc1_bias_grad, out_bias_grad, second_norm_gain_gradient, ln2_bias_grad],
     )
     early_packed, d_mixed = lax.optimization_barrier((early_packed, d_mixed))
@@ -459,19 +453,19 @@
             block_parameters[0].astype(jnp.float32),
         )
     ).astype(jnp.bfloat16)
-    late_packed, late_layout = pack_rows(
-        column_chunks(qkv_weight_grad, width),
+    late_packed, late_layout = pack_columns(
+        [qkv_weight_grad],
         [qkv_bias_grad, first_norm_gain_gradient, ln1_bias_grad, frequencies_grad],
     )
-    (late_mats, late_vecs), late_mine = sum_by_exchange(late_packed, late_layout)
+    late_packed, tokens_grad = lax.optimization_barrier((late_packed, tokens_grad))
     _, early_sq = square_sums_of_block(early_mine, early_layout, 0)
-    freq_sq, late_sq = square_sums_of_block(late_mine, late_layout, 1)
-    freq_sq, other_sq = lax.psum((freq_sq, early_sq + late_sq), ("fsdp", "dp"))
-    fc2_weight_g = early_mats[0]
-    fc1_weight_g = jnp.concatenate(early_mats[1:-1], axis=1)
-    out_weight_g = early_mats[-1]
+    (late_mats, late_vecs), partials = sum_by_exchange(late_packed, late_layout, early_sq)
+    freq_sq, other_sq = lax.psum((partials[0], partials[1]), "fsdp")
+    fc2_weight_g = early_mats[0].reshape(fc2_weight.shape)
+    fc1_weight_g = early_mats[1]
+    out_weight_g = early_mats[2]
     fc2_bias_g, fc1_bias_g, out_bias_g, ln2_gain_g, ln2_bias_g = early_vecs
-    qkv_weight_g = jnp.concatenate(late_mats, axis=1)
+    qkv_weight_g = late_mats[0]
     qkv_bias_g, ln1_gain_g, ln1_bias_g, frequencies_g = late_vecs
     pieces = (
         ln1_gain_g,

time: 661 us -> 603 us (0.912)
  blocking collectives: 212 us -> 69 us
  waiting for transfers between devices: 17.9 us -> 83.3 us
  other arithmetic: 68.5 us -> 81.3 us
  Pallas kernels: 115 us -> 127 us
    all_to_all x1 -> x0, blocking collectives: 135 us -> none  [sum_by_exchange(): received = lax.all_to_all(packed, ('fsdp', 'dp'), 0, 0, tiled=False)]
    all_to_all x0 -> x1, waiting for transfers between devices: none -> 68.8 us  [sum_by_exchange(): received = lax.all_to_all(packed, ('fsdp', 'dp'), 0, 0, tiled=True)]
    psum x1, blocking collectives: 38.5 us -> 20.6 us  [shards(): freq_sq, other_sq = lax.psum((partials[0], partials[1]), 'fsdp')]
    another operation x2 -> x3, other arithmetic: 12.9 us -> 26.7 us
    sub x1 -> x0, other arithmetic: 13.6 us -> none  [shards(): d_theta + d_krot[..., half_head:] * k_rot[..., :half_head]]
    pallas_call x1, Pallas kernels: 47.5 us -> 60.5 us  [attention_forward(): pl.pallas_call(attention_forward_kernel, grid=(width // pair,), in_specs=...]
    unnamed x123 -> x109, local copies, waits for them, and re-layouts: 27.3 us -> 15 us
    all_gather x0 -> x1, blocking collectives: none -> 9.3 us  [sum_by_exchange(): lax.all_gather(jnp.concatenate([mine, extra], axis=1), 'dp', axis=0, tile...]
  transfers between devices with their start and end apart: 5 -> 5, of which waited for: 1 -> 2; matrix products, arithmetic and copies ran while one was open for 22% -> 25% of each run, Pallas kernels for 18% -> 22%
where the time goes in v5:
time: 603 us; the launch traced here: 592 us
  Pallas kernels  127 us (21%)
  matrix products  111 us (18%)
  local copies, waits for them, and re-layouts  94.5 us (16%)
  waiting for transfers between devices  83.3 us (14%)
  other arithmetic  81.3 us (13%)
  blocking collectives  69 us (11%)
  between operations  22 us (4%)
    all_to_all x1, waiting for transfers between devices, sum_by_exchange(): received = lax.all_to_all(packed, ('fsdp', 'dp'), 0, 0, tiled=True)  68.8 us
    pallas_call x1, Pallas kernels, attention_backward(): pl.pallas_call(attention_backward_kernel, grid=(width // pair,), in_specs...  66.9 us
    pallas_call x1, Pallas kernels, attention_forward(): pl.pallas_call(attention_forward_kernel, grid=(width // pair,), in_specs=...  60.5 us
    dot_general x4, matrix products, matmul(): return jnp.dot(left, right, preferred_element_type=jnp.float32)  57.1 us
    unnamed x1, blocking collectives  39.1 us
    dot_general x4, matrix products, matmul_right_t(): lax.dot_general(left, right, (((1,), (1,)), ((), ())), preferred_element_...  28.9 us
    another operation x3, other arithmetic  26.7 us
    dot_general x4, matrix products, matmul_left_t(): lax.dot_general(left, right, (((0,), (0,)), ((), ())), preferred_element_...  24.9 us
  transfers between devices with their start and end apart: 5, of which 2 were waited for; matrix products, arithmetic and copies ran while one was open for 25% of the time, Pallas kernels for 22%

profile of v5, /device:TPU:0, one launch (start us, length us, event | category | flops | bytes accessed | tf_op | source)
XLA Modules:
  0.0 592.4 jit_solution(3784011981006990239)
XLA Ops:
  20.1 39.1 %all-reduce.3 = bf16[10752]{0:T(1024)(128)(2,1)S(1)} all-reduce(bf16[10752]{0:T(1024)(128)(2,1)S(1)} %dynamic-update-slice.4), channel_id=2, replica_groups=mesh['fsdp'=8,'dp'=4] {'fsdp'}, use_global_device_ids=true, to_apply=%add.3 | all-reduce | flops 10752 | bytes 43008
  63.4 14.5 %all-gather.6.cloned.1.call-done = bf16[768,3072]{1,0:T(8,128)(2,1)} async-done(((bf16[24,3072]{1,0:T(8,128)(2,1)}), bf16[768,3072]{1,0:T(8,128)(2,1)}) %all-gather.6.cloned.1.call-update) | async-done | bytes 4718608 | tf_op jit(solution)/shard_map/all_gather | solution.py:227
  77.9 6.3 %convolution_add_fusion = f32[1024,2304]{1,0:T(8,128)S(1)} fusion(f32[2304]{0:T(1024)S(1)} %reshape.874, bf16[768,3072]{1,0:T(8,128)(2,1)} %all-gather.6.cloned.1.call-done, bf16[1024,768]{0,1:T(8,128)(2,1)S(1)} %copy.87, f32[768]{0:T(1024)S(1)} %reshape.873, f32[768]{0:T(1024)S(1)} %reshape.872, f32[1024]{0:T(1024)S(1)} %add_rsqrt_fusion.1, ...), kind=kOutput, calls=%fused_computation.32 | convolution fusion | flops 3630956544 | bytes 14572544 | tf_op jit(solution)/shard_map/dot_general | solution.py:20
  96.0 10.8 %fusion.58 = (bf16[1024,12,32]{0,2,1:T(8,128)(2,1)S(1)}, bf16[1024,12,32]{0,2,1:T(8,128)(2,1)S(1)}, bf16[1024,12,32]{0,2,1:T(8,128)(2,1)S(1)}, bf16[1024,12,32]{0,2,1:T(8,128)(2,1)S(1)}) fusion(f32[1024,12,64]{0,2,1:T(8,128)} %bitcast.43, f32[12,32]{1,0:T(8,128)S(1)} %mul.342, f32[1024]{0:T(1024)S(1)} %get-tuple-element.167, f32[12,32]{1,0:T(8,128)S(1)} %mul.337, ...), kind=kLoop, calls=%fused_computation.161 | loop fusion | flops 7471104 | bytes 9448448 | tf_op jit(solution)/shard_map/convert.51
  114.1 60.5 %attention_forward.1 = (bf16[1024,768]{1,0:T(8,128)(2,1)}, f32[1024,768]{1,0:T(8,128)}) custom-call(bf16[1024,768]{1,0:T(8,128)(2,1)} %copy.90.q_ref, bf16[1024,768]{1,0:T(8,128)(2,1)} %copy.91.k_ref, bf16[1024,768]{1,0:T(8,128)(2,1)} %slice.410.v_ref, s32[1024,1]{1,0:T(8,128)} %copy.92.seg_r_ref, s32[1,1024]{1,0:T(1,128)} %bitcast.57), custom_call_target="tpu_custom_call" | custom-call | flops 3221225472 | bytes 9437184 | tf_op jit(solution)/shard_map/attention_forward/pallas_call | solution.py:174
  180.2 8.2 %fusion.64 = (bf16[32,24,3072]{2,1,0:T(8,128)(2,1)}, bf16[32,24,3072]{2,1,0:T(8,128)(2,1)}) fusion(bf16[32,48,3072]{2,1,0:T(8,128)(2,1)} %bitcast.49), kind=kLoop, calls=%fused_computation.165 | loop fusion | bytes 18874368 | tf_op jit(solution)/shard_map/slice | solution.py:236
  188.4 8.5 %reshape.845 = bf16[3072,768]{1,0:T(8,128)(2,1)} reshape(bf16[32,24,3072]{2,1,0:T(8,128)(2,1)} %get-tuple-element.143) | data formatting | bytes 9437184 | tf_op jit(solution)/shard_map/reshape | solution.py:236
  196.9 37.0 %fusion.3 = (bf16[1024,3072]{1,0:T(8,128)(2,1)}, f32[1024,3072]{1,0:T(8,128)S(1)}) fusion(f32[3072]{0:T(1024)S(1)} %reshape.878, bf16[768,3072]{1,0:T(8,128)(2,1)} %bitcast.54, f32[1024,768]{0,1:T(8,128)} %copy-done.5, f32[768]{0:T(1024)S(1)} %reshape.877, f32[768]{0:T(1024)S(1)} %reshape.876, f32[1024]{0:T(1024)S(1)} %add_rsqrt_fusion, ...), kind=kOutput, calls=%fused_computation.6 | convolution fusion | flops 5043388416 | bytes 26765312 | tf_op jit(solution)/shard_map/dot_general | solution.py:20
  233.9 9.2 %fusion.71 = (bf16[3072]{0:T(1024)(128)(2,1)S(1)}, bf16[1024,3072]{1,0:T(8,128)(2,1)S(1)}) fusion(f32[1024,3072]{1,0:T(8,128)S(1)} %get-tuple-element.193, f32[3072]{0:T(1024)S(1)} %reshape.878, bf16[3072,768]{1,0:T(8,128)(2,1)S(1)} %copy-done.17, bf16[1024,768]{1,0:T(8,128)(2,1)S(1)} %copy-done.12), kind=kOutput, calls=%fused_computation.172 | convolution fusion | flops 4869583872 | bytes 25184256 | tf_op jit(solution)/shard_map/dot_general | solution.py:30
  243.1 7.1 %convolution_convert_fusion = bf16[768,3072]{1,0:T(8,128)(2,1)} fusion(bf16[1024,3072]{1,0:T(8,128)(2,1)S(1)} %get-tuple-element.189, f32[1024,768]{0,1:T(8,128)S(1)} %copy-done.6, f32[768]{0:T(1024)S(1)} %reshape.877, f32[768]{0:T(1024)S(1)} %reshape.876, f32[1024]{0:T(1024)S(1)} %add_rsqrt_fusion, f32[1024]{0:T(1024)S(1)} %broadcast_multiply_fusion.4), kind=kOutput, calls=%fused_computation.33 | convolution fusion | flops 4838129664 | bytes 14170112 | tf_op jit(solution)/shard_map/dot_general | solution.py:24
  250.2 6.7 %fusion.72 = (bf16[768]{0:T(1024)(128)(2,1)S(1)}, f32[1024,768]{1,0:T(8,128)}) fusion(bf16[1024,3072]{1,0:T(8,128)(2,1)S(1)} %get-tuple-element.189, bf16[768,3072]{1,0:T(8,128)(2,1)S(1)} %bitcast.55), kind=kOutput, calls=%fused_computation.173 | convolution fusion | flops 4832623616 | bytes 14157312 | tf_op jit(solution)/shard_map/dot_general | solution.py:30
  270.6 9.9 %convolution_convert_fusion.1 = bf16[3072,768]{1,0:T(8,128)(2,1)} fusion(bf16[1024,3072]{1,0:T(8,128)(2,1)} %get-tuple-element.192, bf16[1024,768]{1,0:T(8,128)(2,1)S(1)} %copy-done.12), kind=kOutput, calls=%fused_computation.34 | convolution fusion | flops 4834197504 | bytes 12582912 | tf_op jit(solution)/shard_map/dot_general | solution.py:24
  280.5 8.5 %convert_element_type.252 = bf16[768,3072]{1,0:T(8,128)(2,1)} reshape(bf16[3072,768]{1,0:T(8,128)(2,1)} %convolution_convert_fusion.1) | data formatting | bytes 9437184 | tf_op jit(solution)/shard_map/convert_element_type | solution.py:261
  289.0 8.8 %fusion.17 = bf16[768,7040]{1,0:T(8,128)(2,1)} fusion(bf16[768,8]{1,0:T(8,128)(2,1)S(1)} %reshape.851, bf16[768,768]{1,0:T(8,128)(2,1)S(1)} %convolution_convert_fusion.4, bf16[768,3072]{1,0:T(8,128)(2,1)} %convolution_convert_fusion, bf16[768,3072]{1,0:T(8,128)(2,1)} %convert_element_type.252), kind=kLoop, calls=%fused_computation.28 | loop fusion | flops 54067200 | bytes 21442560 | tf_op jit(solution)/shard_map/concatenate | solution.py:263
  297.8 4.8 convolution_convert_fusion.3.d_ref
  302.6 66.9 %attention_backward.1 = (f32[1024,768]{1,0:T(8,128)}, f32[1024,768]{1,0:T(8,128)}, f32[1024,768]{1,0:T(8,128)}) custom-call(bf16[1024,768]{1,0:T(8,128)(2,1)} %copy.90.q_ref, bf16[1024,768]{1,0:T(8,128)(2,1)} %copy.91.k_ref, bf16[1024,768]{1,0:T(8,128)(2,1)} %slice.410.v_ref, bf16[1024,768]{1,0:T(8,128)(2,1)} %convolution_convert_fusion.3.d_ref, ...), custom_call_target="tpu_custom_call" | custom-call | flops 6442450944 | bytes 18874368 | tf_op jit(solution)/shard_map/attention_backward/pallas_call | solution.py:194
  376.8 13.7 %subtract_convert_fusion.1 = (bf16[1024,12,32]{0,2,1:T(8,128)(2,1)S(1)}, f32[1024,12,32]{0,2,1:T(8,128)S(1)}, bf16[1024,12,32]{0,2,1:T(8,128)(2,1)S(1)}, bf16[1024,12,32]{0,2,1:T(8,128)(2,1)}) fusion(f32[1024,12,64]{0,2,1:T(8,128)} %bitcast.45, f32[12,32]{1,0:T(8,128)S(1)} %copy-done.23, f32[1024]{0:T(1024)S(1)} %copy-done.29, f32[12,32]{1,0:T(8,128)S(1)} %copy-done.21, ...), kind=kLoop, calls=%fused_computation.81 | loop fusion | flops 13762560 | bytes 16526336 | tf_op jit(solution)/shard_map/convert.35
  390.5 6.4 %multiply_reduce_fusion.6 = (bf16[12,32]{1,0:T(8,128)(2,1)S(1)}, bf16[12,32]{1,0:T(8,128)(2,1)S(1)}, bf16[1024,12,32]{0,2,1:T(8,128)(2,1)S(1)}) fusion(f32[1024,12,32]{0,2,1:T(8,128)S(1)} %get-tuple-element.148, f32[1024]{0:T(1024)S(1)} %copy-done.27, f32[1024]{0:T(1024)S(1)} %copy-done.29, f32[1024,12,64]{0,2,1:T(8,128)S(1)} %bitcast.46, ...), kind=kLoop, calls=%fused_computation.76 | loop fusion | flops 4717824 | bytes 5517824 | tf_op jit(solution)/shard_map/reduce_sum | solution.py:431
  408.1 8.2 %fusion.73 = (bf16[768]{0:T(1024)(128)(2,1)S(1)}, f32[1024,768]{1,0:T(8,128)}) fusion(bf16[768,3072]{1,0:T(8,128)(2,1)} %all-gather.6.cloned.1.call-done, bf16[1024,768]{1,0:T(8,128)(2,1)S(1)} %convert.109, bf16[1024,768]{1,0:T(8,128)(2,1)S(1)} %copy-done.14, bf16[1024,768]{1,0:T(8,128)(2,1)S(1)} %copy.103), kind=kOutput, calls=%fused_computation.174 | convolution fusion | flops 3638820096 | bytes 11404800 | tf_op jit(solution)/shard_map/dot_general | solution.py:30
  426.8 6.4 %convolution_convert_fusion.2 = bf16[768,2304]{1,0:T(8,128)(2,1)S(1)} fusion(bf16[1024,768]{0,1:T(8,128)(2,1)S(1)} %copy-done.3, f32[768]{0:T(1024)S(1)} %copy-done.38, f32[768]{0:T(1024)S(1)} %copy-done.31, f32[1024]{0:T(1024)S(1)} %copy-done.33, f32[1024]{0:T(1024)S(1)} %copy-done.25, bf16[1024,768]{1,0:T(8,128)(2,1)} %copy-done.15, ...), kind=kOutput, calls=%fused_computation.35 | convolution fusion | flops 3644522496 | bytes 9844736 | tf_op jit(solution)/shard_map/dot_general | solution.py:24
  444.1 10.4 %add_convert_fusion = bf16[1024,768]{0,1:T(8,128)(2,1)} fusion(f32[1024,768]{0,1:T(8,128)} %copy-done.5, bf16[1024,3072]{1,0:T(8,128)(2,1)} %get-tuple-element.192, bf16[3072,768]{1,0:T(8,128)(2,1)} %reshape.845, f32[768]{0:T(1024)S(1)} %reshape.879), kind=kOutput, calls=%fused_computation.61 | convolution fusion | flops 4834197504 | bytes 15731712 | tf_op jit(solution)/shard_map/dot_general | solution.py:20
  458.7 68.8 %all-to-all-done = bf16[32,24,2432]{2,1,0:T(8,128)(2,1)} async-done(((bf16[32,24,2432]{2,1,0:T(8,128)(2,1)}), bf16[32,24,2432]{2,1,0:T(8,128)(2,1)}, u32[]{:S(2)}, u32[]{:S(2)}) %all-to-all-start) | async-done | bytes 3735584 | tf_op jit(solution)/shard_map/all_to_all | solution.py:301
  538.1 9.3 %all_gather.22 = f32[96,2560]{1,0:T(8,128)S(1)} all-gather(f32[24,2560]{1,0:T(8,128)S(1)} %pad_maximum_fusion.6), channel_id=1, replica_groups=mesh['fsdp'=8,'dp'=4] {'dp'}, dimensions={0}, use_global_device_ids=true | all-gather | bytes 1228800 | tf_op jit(solution)/shard_map/all_gather | solution.py:306
  548.1 20.6 %all-reduce.5 = (f32[]{:T(128)}, f32[]{:T(128)}) all-reduce(f32[]{:T(128)} %bitcast.23, f32[]{:T(128)} %bitcast.24), channel_id=1, replica_groups=mesh['fsdp'=8,'dp'=4] {'fsdp'}, use_global_device_ids=true, to_apply=%region_30.31 | all-reduce | flops 2 | bytes 16 | tf_op jit(solution)/shard_map/psum | solution.py:463
  (234 shorter events, 119.7 us)
Async XLA Ops:
  7.2 70.7 %all-gather.6.cloned.1.call-start = ((), (), s32[]{:S(2)}) async-start(), calls=%async_computation.2 | async-start | bytes 4866048 | tf_op jit(solution)/shard_map/all_gather | solution.py:227
  9.7 170.5 %all-gather.10.cloned.1.call-start = ((), (), s32[]{:S(2)}) async-start(), calls=%async_computation.4 | async-start | bytes 9732096 | tf_op jit(solution)/shard_map/all_gather | solution.py:234
  11.6 432.5 %reduce-scatter.4.cloned.1.call-start = ((), (), s32[]{:S(2)}) async-start(), calls=%async_computation.5 | async-start | bytes 11151360
  13.3 161.3 %copy-start.2 = (bf16[1024,768]{0,1:T(8,128)(2,1)}, bf16[1024,768]{0,1:T(8,128)(2,1)S(1)}, u32[]{:S(2)}) copy-start(bf16[1024,768]{0,1:T(8,128)(2,1)S(1)} %copy.87) | copy-start | bytes 4718596
  13.5 46.9 %copy-start.39 = (s32[5,3]{0,1:T(4,128)S(1)}, s32[5,3]{0,1:T(4,128)}, u32[]{:S(2)}) copy-start(s32[5,3]{0,1:T(4,128)} %param.21) | copy-start | bytes 184
  60.0 24.2 %copy-start.30 = (f32[768]{0:T(1024)}, f32[768]{0:T(1024)S(1)}, u32[]{:S(2)}) copy-start(f32[768]{0:T(1024)S(1)} %reshape.872) | copy-start | bytes 9220
  60.0 24.2 %copy-start.37 = (f32[768]{0:T(1024)}, f32[768]{0:T(1024)S(1)}, u32[]{:S(2)}) copy-start(f32[768]{0:T(1024)S(1)} %reshape.873) | copy-start | bytes 9220
  60.3 35.7 %copy-start.20 = (f32[12,32]{1,0:T(8,128)}, f32[12,32]{1,0:T(8,128)S(1)}, u32[]{:S(2)}) copy-start(f32[12,32]{1,0:T(8,128)S(1)} %mul.337) | copy-start | bytes 4612
  60.4 35.6 %copy-start.22 = (f32[12,32]{1,0:T(8,128)}, f32[12,32]{1,0:T(8,128)S(1)}, u32[]{:S(2)}) copy-start(f32[12,32]{1,0:T(8,128)S(1)} %mul.342) | copy-start | bytes 4612
  60.7 23.5 %copy-start.35 = (s32[1024]{0:T(1024)}, s32[1024]{0:T(1024)S(1)}, u32[]{:S(2)}) copy-start(s32[1024]{0:T(1024)S(1)} %get-tuple-element.172) | copy-start | bytes 12292
  60.7 35.2 %copy-start.26 = (f32[1024]{0:T(1024)}, f32[1024]{0:T(1024)S(1)}, u32[]{:S(2)}) copy-start(f32[1024]{0:T(1024)S(1)} %get-tuple-element.166) | copy-start | bytes 12292
  60.7 35.2 %copy-start.28 = (f32[1024]{0:T(1024)}, f32[1024]{0:T(1024)S(1)}, u32[]{:S(2)}) copy-start(f32[1024]{0:T(1024)S(1)} %get-tuple-element.167) | copy-start | bytes 12292
  63.0 21.3 %copy-start.24 = (f32[1024]{0:T(1024)}, f32[1024]{0:T(1024)S(1)}, u32[]{:S(2)}) copy-start(f32[1024]{0:T(1024)S(1)} %broadcast_multiply_fusion.5) | copy-start | bytes 12292
  63.4 20.8 %copy-start.32 = (f32[1024]{0:T(1024)}, f32[1024]{0:T(1024)S(1)}, u32[]{:S(2)}) copy-start(f32[1024]{0:T(1024)S(1)} %add_rsqrt_fusion.1) | copy-start | bytes 12292
  196.9 37.0 %copy-start.12 = (bf16[1024,768]{1,0:T(8,128)(2,1)S(1)}, bf16[1024,768]{1,0:T(8,128)(2,1)}, u32[]{:S(2)}) copy-start(bf16[1024,768]{1,0:T(8,128)(2,1)} %param.35) | copy-start | bytes 4718596
  196.9 37.0 %copy-start.17 = (bf16[3072,768]{1,0:T(8,128)(2,1)S(1)}, bf16[3072,768]{1,0:T(8,128)(2,1)}, u32[]{:S(2)}) copy-start(bf16[3072,768]{1,0:T(8,128)(2,1)} %reshape.845) | copy-start | bytes 14155780
  233.9 9.2 %copy-start.6 = (f32[1024,768]{0,1:T(8,128)S(1)}, f32[1024,768]{0,1:T(8,128)}, u32[]{:S(2)}) copy-start(f32[1024,768]{0,1:T(8,128)} %copy-done.5) | copy-start | bytes 9437188
  376.8 13.7 %copy-start.4 = (f32[1024,768]{0,1:T(8,128)S(1)}, f32[1024,768]{0,1:T(8,128)}, u32[]{:S(2)}) copy-start(f32[1024,768]{0,1:T(8,128)} %copy.101) | copy-start | bytes 9437188
  408.1 8.2 %copy-start.15 = (bf16[1024,768]{1,0:T(8,128)(2,1)}, bf16[1024,768]{1,0:T(8,128)(2,1)S(1)}, u32[]{:S(2)}) copy-start(bf16[1024,768]{1,0:T(8,128)(2,1)S(1)} %convert.109) | copy-start | bytes 4718596
  439.6 87.8 %all-to-all-start = ((bf16[32,24,2432]{2,1,0:T(8,128)(2,1)}), bf16[32,24,2432]{2,1,0:T(8,128)(2,1)}, u32[]{:S(2)}, u32[]{:S(2)}) async-start(bf16[32,24,2432]{2,1,0:T(8,128)(2,1)} %bitcast.47), calls=%async_computation | async-start | bytes 7471104 | tf_op jit(solution)/shard_map/all_to_all | solution.py:301
  443.3 130.3 %all-gather.8.cloned.1.call-start = ((), (), s32[]{:S(2)}) async-start(), calls=%async_computation.3 | async-start | bytes 1689600 | tf_op jit(solution)/shard_map/all_gather | solution.py:295
  444.1 10.4 %copy-start.16 = (bf16[1024,768]{0,1:T(8,128)(2,1)S(1)}, bf16[1024,768]{0,1:T(8,128)(2,1)}, u32[]{:S(2)}) copy-start(bf16[1024,768]{0,1:T(8,128)(2,1)} %fusion.33) | copy-start | bytes 4718596
  456.1 77.9 %copy-start.19 = (bf16[24,7040]{1,0:T(8,128)(2,1)S(1)}, bf16[24,7040]{1,0:T(8,128)(2,1)}, u32[]{:S(2)}) copy-start(bf16[24,7040]{1,0:T(8,128)(2,1)} %reduce-scatter.4.cloned.1.call-done) | copy-start | bytes 1013764
  574.6 8.7 %copy-start.1 = (bf16[384,768]{1,0:T(8,128)(2,1)S(1)}, bf16[384,768]{1,0:T(8,128)(2,1)}, u32[]{:S(2)}) copy-start(bf16[384,768]{1,0:T(8,128)(2,1)} %param.32) | copy-start | bytes 1769476
  (32 other events, 140.1 us)
Sparse Core Ops, SparseCore 0:
  11.5 66.3 all-gather.5
  81.4 80.0 all-gather.9
  302.7 136.3 reduce-scatter.3
  445.4 33.0 all-gather.7

commit v6 on v5

--- a/solution.py
+++ b/solution.py
@@ -124,8 +124,10 @@
             mask = seg_r_ref[pl.ds(at, Q_BLOCK), :] == seg_c
             scores = jnp.where(mask, _nt(q_h, k_h) * scale, masked_score)
             top = jnp.max(scores, axis=-1, keepdims=True)
-            log_total = top + jnp.log(jnp.sum(jnp.exp(scores - top), axis=-1, keepdims=True))
-            probs = jnp.exp(scores - log_total).astype(jnp.bfloat16)
+            shifted = jnp.exp(scores - top)
+            total = jnp.sum(shifted, axis=-1, keepdims=True)
+            log_total = top + jnp.log(total)
+            probs = (shifted * (1.0 / total)).astype(jnp.bfloat16)
             o_ref[pl.ds(at, Q_BLOCK), cols] = _nn(probs, v_h).astype(o_ref.dtype)
             lse_ref[pl.ds(at, Q_BLOCK), cols] = jnp.broadcast_to(log_total, (Q_BLOCK, HD))
             return carry
@@ -222,29 +224,27 @@
     return lax.dynamic_slice_in_dim(shard, lax.axis_index("dp") * part, part, 0)
 
 
-def gather_side_by_side(left, right):
-    joined = jnp.concatenate([quarter(left), quarter(right)], axis=1)
+def gather_with_small(left, right, vectors):
+    rows = quarter(left).shape[0]
+    flat = quarter(jnp.concatenate(vectors))
+    cols = -(-flat.shape[0] // rows)
+    tile = jnp.pad(flat, (0, rows * cols - flat.shape[0])).reshape(rows, cols)
+    tile = jnp.pad(tile, ((0, 0), (0, -cols % 128)))
+    joined = jnp.concatenate([quarter(left), quarter(right), tile], axis=1)
     whole = lax.all_gather(joined, ("fsdp", "dp"), axis=0, tiled=True)
-    return whole[:, : left.shape[1]], whole[:, left.shape[1] :]
-
-
-def gather_stacked(top, bottom):
-    upper = quarter(top)
-    lower = quarter(bottom).reshape(-1, top.shape[1])
-    whole = lax.all_gather(jnp.concatenate([upper, lower], axis=0)[None], ("fsdp", "dp"), axis=0, tiled=True)
-    first = whole[:, : upper.shape[0]].reshape(-1, top.shape[1])
-    second = whole[:, upper.shape[0] :].reshape(-1, bottom.shape[1])
-    return first, second
-
-
-def gather_small(vectors):
-    sizes = [v.shape[0] for v in vectors]
-    packed = lax.all_gather(jnp.concatenate(vectors), "fsdp", axis=0, tiled=False)
+    split = left.shape[1] + right.shape[1]
+    groups = lax.psum(1, "fsdp")
+    small = whole[:, split : split + cols].reshape(lax.psum(1, ("fsdp", "dp")), -1)[:, : flat.shape[0]]
+    small = small.reshape(groups, -1)
     out, at = [], 0
-    for n in sizes:
-        out.append(packed[:, at : at + n].reshape(-1))
-        at += n
-    return out
+    for v in vectors:
+        out.append(small[:, at : at + v.shape[0]].reshape(-1))
+        at += v.shape[0]
+    return whole[:, : left.shape[1]], whole[:, left.shape[1] : split], out
+
+
+def gather_alone(shard):
+    return lax.all_gather(quarter(shard), ("fsdp", "dp"), axis=0, tiled=True)
 
 
 def pack_columns(matrices, vectors):
@@ -326,11 +326,12 @@
     frequencies,
     cotangent,
 ):
-    small_local = (ln1_gain, ln1_bias, qkv_bias, out_bias, ln2_gain, ln2_bias, fc1_bias, fc2_bias, frequencies)
+    small_local = [ln1_gain, ln1_bias, qkv_bias, out_bias, ln2_gain, ln2_bias, fc1_bias, fc2_bias, frequencies]
+    g_qkv_weight, g_out_weight, small_whole = gather_with_small(qkv_weight, out_weight, small_local)
     (g_ln1_gain, g_ln1_bias, g_qkv_bias, g_out_bias, g_ln2_gain, g_ln2_bias, g_fc1_bias, g_fc2_bias,
-     g_frequencies) = gather_small(small_local)
-    g_qkv_weight, g_out_weight = gather_side_by_side(qkv_weight, out_weight)
-    g_fc1_weight, g_fc2_weight = gather_stacked(fc1_weight, fc2_weight)
+     g_frequencies) = small_whole
+    g_fc1_weight = gather_alone(fc1_weight)
+    g_fc2_weight = gather_alone(fc2_weight)
     block_parameters = (
         g_ln1_gain,
         g_ln1_bias,

time: 603 us -> 587 us (0.973)
  waiting for transfers between devices: 83.3 us -> 125 us
  blocking collectives: 69 us -> 29.9 us
  Pallas kernels: 127 us -> 115 us
  local copies, waits for them, and re-layouts: 94.5 us -> 85.3 us
    all_gather x2 -> x3, waiting for transfers between devices: 14.5 us -> 55.7 us  [the longest x1 55.7 us: gather_with_small(): whole = lax.all_gather(joined, ('fsdp', 'dp'), axis=0, tiled=True)]
    unnamed x1 -> x0, blocking collectives: 39.1 us -> none
    pallas_call x1, Pallas kernels: 60.5 us -> 48 us  [attention_forward(): pl.pallas_call(attention_forward_kernel, grid=(width // pair,), in_specs=...]
    reshape x2 -> x1, local copies, waits for them, and re-layouts: 8.55 us -> 0.1 us  [gather_with_small(): tile = jnp.pad(flat, (0, rows * cols - flat.shape[0])).reshape(rows, cols)]
    slice x1, local copies, waits for them, and re-layouts: 8.23 us -> 0.94 us  [gather_with_small(): whole[:, split:split + cols].reshape(lax.psum(1, ('fsdp', 'dp')), -1)]
    concatenate x1, local copies, waits for them, and re-layouts: 0.09 us -> 6.13 us  [gather_with_small(): flat = quarter(jnp.concatenate(vectors))]
    unnamed x109 -> x84, local copies, waits for them, and re-layouts: 15 us -> 13.5 us
  transfers between devices with their start and end apart: 5 -> 6, of which waited for: 2 -> 2; matrix products, arithmetic and copies ran while one was open for 25% -> 33% of each run, Pallas kernels for 22% -> 20%
where the time goes in v6:
time: 587 us; the launch traced here: 576 us
  waiting for transfers between devices  125 us (21%)
  matrix products  115 us (20%)
  Pallas kernels  115 us (20%)
  local copies, waits for them, and re-layouts  85.3 us (15%)
  other arithmetic  80.4 us (14%)
  blocking collectives  29.9 us (5%)
  between operations  21.1 us (4%)
    all_to_all x1, waiting for transfers between devices, sum_by_exchange(): received = lax.all_to_all(packed, ('fsdp', 'dp'), 0, 0, tiled=True)  69.1 us
    pallas_call x1, Pallas kernels, attention_backward(): pl.pallas_call(attention_backward_kernel, grid=(width // pair,), in_specs...  66.9 us
    dot_general x4, matrix products, matmul(): return jnp.dot(left, right, preferred_element_type=jnp.float32)  59 us
    all_gather x1, waiting for transfers between devices, gather_with_small(): whole = lax.all_gather(joined, ('fsdp', 'dp'), axis=0, tiled=True)  55.7 us
    pallas_call x1, Pallas kernels, attention_forward(): pl.pallas_call(attention_forward_kernel, grid=(width // pair,), in_specs=...  48 us
    dot_general x4, matrix products, matmul_right_t(): lax.dot_general(left, right, (((1,), (1,)), ((), ())), preferred_element_...  31.5 us
    another operation x3, other arithmetic  26.6 us
    dot_general x4, matrix products, matmul_left_t(): lax.dot_general(left, right, (((0,), (0,)), ((), ())), preferred_element_...  24.8 us
  transfers between devices with their start and end apart: 6, of which 2 were waited for; matrix products, arithmetic and copies ran while one was open for 33% of the time, Pallas kernels for 20%

profile of v6, /device:TPU:0, one launch (start us, length us, event | category | flops | bytes accessed | tf_op | source)
XLA Modules:
  0.0 575.6 jit_solution(13991219973417685472)
XLA Ops:
  9.0 6.1 %concatenate.56 = bf16[1344]{0:T(1024)(128)(2,1)S(1)} concatenate(bf16[96]{0:T(256)(128)(2,1)} %param.22, bf16[96]{0:T(256)(128)(2,1)} %param.23, bf16[288]{0:T(512)(128)(2,1)} %param.25, bf16[96]{0:T(256)(128)(2,1)} %param.27, bf16[96]{0:T(256)(128)(2,1)} %param.28, bf16[96]{0:T(256)(128)(2,1)} %param.29, bf16[384]{0:T(512)(128)(2,1)} %param.31, bf16[96]{0:T(256)(128)(2,1)} %param.33, ...), dimensions={0} | concatenate | bytes 5376 | tf_op jit(solution)/shard_map/concatenate | solution.py:229
  27.5 55.7 %all-gather.5.cloned.1.call-done = bf16[768,3200]{1,0:T(8,128)(2,1)} async-done(((bf16[24,3200]{1,0:T(8,128)(2,1)}), bf16[768,3200]{1,0:T(8,128)(2,1)}) %all-gather.5.cloned.1.call-update) | async-done | bytes 4915216 | tf_op jit(solution)/shard_map/all_gather | solution.py:234
  85.2 6.3 %convolution_add_fusion = f32[1024,2304]{1,0:T(8,128)S(1)} fusion(f32[2304]{0:T(1024)S(1)} %reshape.866, bf16[768,3200]{1,0:T(8,128)(2,1)} %all-gather.5.cloned.1.call-done, bf16[1024,768]{0,1:T(8,128)(2,1)S(1)} %copy.87, f32[768]{0:T(1024)S(1)} %reshape.865, f32[768]{0:T(1024)S(1)} %reshape.864, f32[1024]{0:T(1024)S(1)} %add_rsqrt_fusion.1, ...), kind=kOutput, calls=%fused_computation.32 | convolution fusion | flops 3630956544 | bytes 14572544 | tf_op jit(solution)/shard_map/dot_general | solution.py:20
  103.6 10.8 %fusion.60 = (bf16[1024,12,32]{0,2,1:T(8,128)(2,1)S(1)}, bf16[1024,12,32]{0,2,1:T(8,128)(2,1)S(1)}, bf16[1024,12,32]{0,2,1:T(8,128)(2,1)S(1)}, bf16[1024,12,32]{0,2,1:T(8,128)(2,1)S(1)}) fusion(f32[1024,12,64]{0,2,1:T(8,128)} %bitcast.40, f32[12,32]{1,0:T(8,128)S(1)} %mul.346, f32[1024]{0:T(1024)S(1)} %get-tuple-element.165, f32[12,32]{1,0:T(8,128)S(1)} %mul.341, ...), kind=kLoop, calls=%fused_computation.162 | loop fusion | flops 7471104 | bytes 9448448 | tf_op jit(solution)/shard_map/convert.51
  121.8 48.0 %attention_forward.1 = (bf16[1024,768]{1,0:T(8,128)(2,1)}, f32[1024,768]{1,0:T(8,128)}) custom-call(bf16[1024,768]{1,0:T(8,128)(2,1)} %copy.90.q_ref, bf16[1024,768]{1,0:T(8,128)(2,1)} %copy.91.k_ref, bf16[1024,768]{1,0:T(8,128)(2,1)} %slice.405.v_ref, s32[1024,1]{1,0:T(8,128)} %copy.92.seg_r_ref, s32[1,1024]{1,0:T(1,128)} %bitcast.51), custom_call_target="tpu_custom_call" | custom-call | flops 3221225472 | bytes 9437184 | tf_op jit(solution)/shard_map/attention_forward/pallas_call | solution.py:176
  175.5 39.1 %fusion.3 = (bf16[1024,3072]{1,0:T(8,128)(2,1)}, f32[1024,3072]{1,0:T(8,128)}) fusion(f32[3072]{0:T(1024)S(1)} %reshape.870, bf16[768,3072]{1,0:T(8,128)(2,1)} %all-gather.7.cloned.1.call-done, f32[1024,768]{0,1:T(8,128)} %copy-done.5, f32[768]{0:T(1024)S(1)} %reshape.869, f32[768]{0:T(1024)S(1)} %reshape.868, f32[1024]{0:T(1024)S(1)} %add_rsqrt_fusion, ...), kind=kOutput, calls=%fused_computation.6 | convolution fusion | flops 5043388416 | bytes 26765312 | tf_op jit(solution)/shard_map/dot_general | solution.py:20
  214.7 11.9 %fusion.72 = (bf16[3072]{0:T(1024)(128)(2,1)S(1)}, bf16[1024,3072]{1,0:T(8,128)(2,1)S(1)}) fusion(f32[1024,3072]{1,0:T(8,128)} %get-tuple-element.191, f32[3072]{0:T(1024)S(1)} %reshape.870, bf16[3072,768]{1,0:T(8,128)(2,1)} %all-gather.9.cloned.1.call-done, bf16[1024,768]{1,0:T(8,128)(2,1)S(1)} %copy-done.12), kind=kOutput, calls=%fused_computation.172 | convolution fusion | flops 4869583872 | bytes 25184256 | tf_op jit(solution)/shard_map/dot_general | solution.py:30
  226.6 7.2 %convolution_convert_fusion = bf16[768,3072]{1,0:T(8,128)(2,1)} fusion(bf16[1024,3072]{1,0:T(8,128)(2,1)S(1)} %get-tuple-element.187, f32[1024,768]{0,1:T(8,128)S(1)} %copy-done.6, f32[768]{0:T(1024)S(1)} %reshape.869, f32[768]{0:T(1024)S(1)} %reshape.868, f32[1024]{0:T(1024)S(1)} %add_rsqrt_fusion, f32[1024]{0:T(1024)S(1)} %broadcast_multiply_fusion.4), kind=kOutput, calls=%fused_computation.33 | convolution fusion | flops 4838129664 | bytes 14170112 | tf_op jit(solution)/shard_map/dot_general | solution.py:24
  233.7 6.7 %fusion.73 = (bf16[768]{0:T(1024)(128)(2,1)S(1)}, f32[1024,768]{1,0:T(8,128)}) fusion(bf16[1024,3072]{1,0:T(8,128)(2,1)S(1)} %get-tuple-element.187, bf16[768,3072]{1,0:T(8,128)(2,1)S(1)} %copy-done.38), kind=kOutput, calls=%fused_computation.173 | convolution fusion | flops 4832623616 | bytes 14157312 | tf_op jit(solution)/shard_map/dot_general | solution.py:30
  244.1 4.0 multiply_reduce_fusion
  254.1 9.8 %convolution_convert_fusion.1 = bf16[3072,768]{1,0:T(8,128)(2,1)} fusion(bf16[1024,3072]{1,0:T(8,128)(2,1)} %get-tuple-element.190, bf16[1024,768]{1,0:T(8,128)(2,1)S(1)} %copy-done.12), kind=kOutput, calls=%fused_computation.34 | convolution fusion | flops 4834197504 | bytes 12582912 | tf_op jit(solution)/shard_map/dot_general | solution.py:24
  263.9 8.5 %convert_element_type.254 = bf16[768,3072]{1,0:T(8,128)(2,1)} reshape(bf16[3072,768]{1,0:T(8,128)(2,1)} %convolution_convert_fusion.1) | data formatting | bytes 9437184 | tf_op jit(solution)/shard_map/convert_element_type | solution.py:261
  272.4 8.8 %fusion.17 = bf16[768,7040]{1,0:T(8,128)(2,1)} fusion(bf16[768,8]{1,0:T(8,128)(2,1)S(1)} %reshape.843, bf16[768,768]{1,0:T(8,128)(2,1)S(1)} %convolution_convert_fusion.4, bf16[768,3072]{1,0:T(8,128)(2,1)} %convolution_convert_fusion, bf16[768,3072]{1,0:T(8,128)(2,1)} %convert_element_type.254), kind=kLoop, calls=%fused_computation.28 | loop fusion | flops 54067200 | bytes 21442560 | tf_op jit(solution)/shard_map/concatenate | solution.py:263
  281.2 4.8 convolution_convert_fusion.3.d_ref
  286.0 66.9 %attention_backward.1 = (f32[1024,768]{1,0:T(8,128)}, f32[1024,768]{1,0:T(8,128)}, f32[1024,768]{1,0:T(8,128)}) custom-call(bf16[1024,768]{1,0:T(8,128)(2,1)} %copy.90.q_ref, bf16[1024,768]{1,0:T(8,128)(2,1)} %copy.91.k_ref, bf16[1024,768]{1,0:T(8,128)(2,1)} %slice.405.v_ref, bf16[1024,768]{1,0:T(8,128)(2,1)} %convolution_convert_fusion.3.d_ref, ...), custom_call_target="tpu_custom_call" | custom-call | flops 6442450944 | bytes 18874368 | tf_op jit(solution)/shard_map/attention_backward/pallas_call | solution.py:196
  356.5 3.9 copy.102
  360.4 13.6 %subtract_convert_fusion.1 = (bf16[1024,12,32]{0,2,1:T(8,128)(2,1)S(1)}, f32[1024,12,32]{0,2,1:T(8,128)S(1)}, bf16[1024,12,32]{0,2,1:T(8,128)(2,1)S(1)}, bf16[1024,12,32]{0,2,1:T(8,128)(2,1)}) fusion(f32[1024,12,64]{0,2,1:T(8,128)} %bitcast.42, f32[12,32]{1,0:T(8,128)S(1)} %copy-done.21, f32[1024]{0:T(1024)S(1)} %copy-done.27, f32[12,32]{1,0:T(8,128)S(1)} %copy-done.19, ...), kind=kLoop, calls=%fused_computation.81 | loop fusion | flops 13762560 | bytes 16526336 | tf_op jit(solution)/shard_map/convert.35
  374.0 6.4 %multiply_reduce_fusion.6 = (bf16[12,32]{1,0:T(8,128)(2,1)S(1)}, bf16[12,32]{1,0:T(8,128)(2,1)S(1)}, bf16[1024,12,32]{0,2,1:T(8,128)(2,1)S(1)}) fusion(f32[1024,12,32]{0,2,1:T(8,128)S(1)} %get-tuple-element.146, f32[1024]{0:T(1024)S(1)} %copy-done.25, f32[1024]{0:T(1024)S(1)} %copy-done.27, f32[1024,12,64]{0,2,1:T(8,128)S(1)} %bitcast.43, ...), kind=kLoop, calls=%fused_computation.76 | loop fusion | flops 4717824 | bytes 5517824 | tf_op jit(solution)/shard_map/reduce_sum | solution.py:432
  391.4 8.1 %fusion.74 = (bf16[768]{0:T(1024)(128)(2,1)S(1)}, f32[1024,768]{1,0:T(8,128)}) fusion(bf16[768,3200]{1,0:T(8,128)(2,1)} %all-gather.5.cloned.1.call-done, bf16[1024,768]{1,0:T(8,128)(2,1)S(1)} %convert.109, bf16[1024,768]{1,0:T(8,128)(2,1)S(1)} %copy-done.14, bf16[1024,768]{1,0:T(8,128)(2,1)S(1)} %copy.103), kind=kOutput, calls=%fused_computation.174 | convolution fusion | flops 3638820096 | bytes 11404800 | tf_op jit(solution)/shard_map/dot_general | solution.py:30
  410.0 6.4 %convolution_convert_fusion.2 = bf16[768,2304]{1,0:T(8,128)(2,1)S(1)} fusion(bf16[1024,768]{0,1:T(8,128)(2,1)S(1)} %copy-done.3, f32[768]{0:T(1024)S(1)} %copy-done.36, f32[768]{0:T(1024)S(1)} %copy-done.31, f32[1024]{0:T(1024)S(1)} %copy-done.29, f32[1024]{0:T(1024)S(1)} %copy-done.23, bf16[1024,768]{1,0:T(8,128)(2,1)} %copy-done.15, ...), kind=kOutput, calls=%fused_computation.35 | convolution fusion | flops 3644522496 | bytes 9844736 | tf_op jit(solution)/shard_map/dot_general | solution.py:24
  427.3 10.2 %add_convert_fusion = bf16[1024,768]{0,1:T(8,128)(2,1)} fusion(f32[1024,768]{0,1:T(8,128)} %copy-done.5, bf16[1024,3072]{1,0:T(8,128)(2,1)} %get-tuple-element.190, bf16[3072,768]{1,0:T(8,128)(2,1)} %all-gather.9.cloned.1.call-done, f32[768]{0:T(1024)S(1)} %reshape.871), kind=kOutput, calls=%fused_computation.61 | convolution fusion | flops 4834197504 | bytes 15731712 | tf_op jit(solution)/shard_map/dot_general | solution.py:20
  441.6 69.1 %all-to-all-done = bf16[32,24,2432]{2,1,0:T(8,128)(2,1)} async-done(((bf16[32,24,2432]{2,1,0:T(8,128)(2,1)}), bf16[32,24,2432]{2,1,0:T(8,128)(2,1)}, u32[]{:S(2)}, u32[]{:S(2)}) %all-to-all-start) | async-done | bytes 3735584 | tf_op jit(solution)/shard_map/all_to_all | solution.py:301
  521.4 9.3 %all_gather.18 = f32[96,2560]{1,0:T(8,128)S(1)} all-gather(f32[24,2560]{1,0:T(8,128)S(1)} %pad_maximum_fusion.5), channel_id=1, replica_groups=mesh['fsdp'=8,'dp'=4] {'dp'}, dimensions={0}, use_global_device_ids=true | all-gather | bytes 1228800 | tf_op jit(solution)/shard_map/all_gather | solution.py:306
  531.3 20.6 %all-reduce.5 = (f32[]{:T(128)}, f32[]{:T(128)}) all-reduce(f32[]{:T(128)} %bitcast.20, f32[]{:T(128)} %bitcast.21), channel_id=1, replica_groups=mesh['fsdp'=8,'dp'=4] {'fsdp'}, use_global_device_ids=true, to_apply=%region_30.31 | all-reduce | flops 2 | bytes 16 | tf_op jit(solution)/shard_map/psum | solution.py:464
  (210 shorter events, 112.4 us)
Async XLA Ops:
  7.2 8.9 %copy-start = (bf16[96,3072]{1,0:T(8,128)(2,1)S(1)}, bf16[96,3072]{1,0:T(8,128)(2,1)}, u32[]{:S(2)}) copy-start(bf16[96,3072]{1,0:T(8,128)(2,1)} %param.30) | copy-start | bytes 1769476
  7.2 75.9 %all-gather.5.cloned.1.call-start = ((), (), s32[]{:S(2)}) async-start(), calls=%async_computation.2 | async-start | bytes 5068800 | tf_op jit(solution)/shard_map/all_gather | solution.py:234
  16.0 159.5 %all-gather.7.cloned.1.call-start = ((), (), s32[]{:S(2)}) async-start(), calls=%async_computation.3 | async-start | bytes 4866048 | tf_op jit(solution)/shard_map/all_gather | solution.py:247
  16.8 197.9 %all-gather.9.cloned.1.call-start = ((), (), s32[]{:S(2)}) async-start(), calls=%async_computation.4 | async-start | bytes 4866048 | tf_op jit(solution)/shard_map/all_gather | solution.py:247
  18.5 408.8 %reduce-scatter.4.cloned.1.call-start = ((), (), s32[]{:S(2)}) async-start(), calls=%async_computation.6 | async-start | bytes 11151360
  20.2 149.5 %copy-start.2 = (bf16[1024,768]{0,1:T(8,128)(2,1)}, bf16[1024,768]{0,1:T(8,128)(2,1)S(1)}, u32[]{:S(2)}) copy-start(bf16[1024,768]{0,1:T(8,128)(2,1)S(1)} %copy.87) | copy-start | bytes 4718596
  20.5 64.7 %copy-start.22 = (f32[1024]{0:T(1024)}, f32[1024]{0:T(1024)S(1)}, u32[]{:S(2)}) copy-start(f32[1024]{0:T(1024)S(1)} %broadcast_multiply_fusion.5) | copy-start | bytes 12292
  21.0 70.6 %copy-start.28 = (f32[1024]{0:T(1024)}, f32[1024]{0:T(1024)S(1)}, u32[]{:S(2)}) copy-start(f32[1024]{0:T(1024)S(1)} %add_rsqrt_fusion.1) | copy-start | bytes 12292
  21.4 70.2 %copy-start.33 = (s32[1024]{0:T(1024)}, s32[1024]{0:T(1024)S(1)}, u32[]{:S(2)}) copy-start(s32[1024]{0:T(1024)S(1)} %get-tuple-element.170) | copy-start | bytes 12292
  21.4 82.2 %copy-start.24 = (f32[1024]{0:T(1024)}, f32[1024]{0:T(1024)S(1)}, u32[]{:S(2)}) copy-start(f32[1024]{0:T(1024)S(1)} %get-tuple-element.164) | copy-start | bytes 12292
  21.4 82.2 %copy-start.26 = (f32[1024]{0:T(1024)}, f32[1024]{0:T(1024)S(1)}, u32[]{:S(2)}) copy-start(f32[1024]{0:T(1024)S(1)} %get-tuple-element.165) | copy-start | bytes 12292
  103.5 10.9 %copy-start.18 = (f32[12,32]{1,0:T(8,128)}, f32[12,32]{1,0:T(8,128)S(1)}, u32[]{:S(2)}) copy-start(f32[12,32]{1,0:T(8,128)S(1)} %mul.341) | copy-start | bytes 4612
  103.6 10.8 %copy-start.20 = (f32[12,32]{1,0:T(8,128)}, f32[12,32]{1,0:T(8,128)S(1)}, u32[]{:S(2)}) copy-start(f32[12,32]{1,0:T(8,128)S(1)} %mul.346) | copy-start | bytes 4612
  175.5 39.2 %copy-start.12 = (bf16[1024,768]{1,0:T(8,128)(2,1)S(1)}, bf16[1024,768]{1,0:T(8,128)(2,1)}, u32[]{:S(2)}) copy-start(bf16[1024,768]{1,0:T(8,128)(2,1)} %param.35) | copy-start | bytes 4718596
  214.7 11.9 %copy-start.6 = (f32[1024,768]{0,1:T(8,128)S(1)}, f32[1024,768]{0,1:T(8,128)}, u32[]{:S(2)}) copy-start(f32[1024,768]{0,1:T(8,128)} %copy-done.5) | copy-start | bytes 9437188
  226.6 7.2 %copy-start.38 = (bf16[768,3072]{1,0:T(8,128)(2,1)S(1)}, bf16[768,3072]{1,0:T(8,128)(2,1)}, u32[]{:S(2)}) copy-start(bf16[768,3072]{1,0:T(8,128)(2,1)} %all-gather.7.cloned.1.call-done) | copy-start | bytes 14155780
  360.4 13.6 %copy-start.4 = (f32[1024,768]{0,1:T(8,128)S(1)}, f32[1024,768]{0,1:T(8,128)}, u32[]{:S(2)}) copy-start(f32[1024,768]{0,1:T(8,128)} %copy.101) | copy-start | bytes 9437188
  383.4 7.8 %copy-start.13 = (bf16[1024,768]{1,0:T(8,128)(2,1)}, bf16[1024,768]{1,0:T(8,128)(2,1)S(1)}, u32[]{:S(2)}) copy-start(bf16[1024,768]{1,0:T(8,128)(2,1)S(1)} %copy.103) | copy-start | bytes 4718596
  391.4 8.1 %copy-start.15 = (bf16[1024,768]{1,0:T(8,128)(2,1)}, bf16[1024,768]{1,0:T(8,128)(2,1)S(1)}, u32[]{:S(2)}) copy-start(bf16[1024,768]{1,0:T(8,128)(2,1)S(1)} %convert.109) | copy-start | bytes 4718596
  422.9 87.8 %all-to-all-start = ((bf16[32,24,2432]{2,1,0:T(8,128)(2,1)}), bf16[32,24,2432]{2,1,0:T(8,128)(2,1)}, u32[]{:S(2)}, u32[]{:S(2)}) async-start(bf16[32,24,2432]{2,1,0:T(8,128)(2,1)} %bitcast.44), calls=%async_computation | async-start | bytes 7471104 | tf_op jit(solution)/shard_map/all_to_all | solution.py:301
  426.5 130.3 %all-gather.11.cloned.1.call-start = ((), (), s32[]{:S(2)}) async-start(), calls=%async_computation.5 | async-start | bytes 1689600 | tf_op jit(solution)/shard_map/all_gather | solution.py:295
  427.3 10.2 %copy-start.16 = (bf16[1024,768]{0,1:T(8,128)(2,1)S(1)}, bf16[1024,768]{0,1:T(8,128)(2,1)}, u32[]{:S(2)}) copy-start(bf16[1024,768]{0,1:T(8,128)(2,1)} %fusion.33) | copy-start | bytes 4718596
  439.0 78.1 %copy-start.17 = (bf16[24,7040]{1,0:T(8,128)(2,1)S(1)}, bf16[24,7040]{1,0:T(8,128)(2,1)}, u32[]{:S(2)}) copy-start(bf16[24,7040]{1,0:T(8,128)(2,1)} %reduce-scatter.4.cloned.1.call-done) | copy-start | bytes 1013764
  557.8 8.7 %copy-start.1 = (bf16[96,3072]{1,0:T(8,128)(2,1)S(1)}, bf16[96,3072]{1,0:T(8,128)(2,1)}, u32[]{:S(2)}) copy-start(bf16[96,3072]{1,0:T(8,128)(2,1)} %param.30) | copy-start | bytes 1769476
  (22 other events, 78.2 us)
Sparse Core Ops, SparseCore 0:
  16.1 66.9 all-gather.4
  86.6 61.9 all-gather.6
  152.1 61.9 all-gather.8
  286.1 135.9 reduce-scatter.3
  428.6 33.0 all-gather.10

commit v7 on v6

--- a/solution.py
+++ b/solution.py
@@ -54,21 +54,22 @@
     )
 
 
-def rotary_tables(frequencies, grid_row, grid_col):
+def lane_tables(frequencies, grid_row, grid_col, width):
     half_width = frequencies.shape[0] // 2
     freq_float = frequencies.astype(jnp.float32)
     freq_row = freq_float[:half_width].reshape(H, HD // 2)
     freq_col = freq_float[half_width:].reshape(H, HD // 2)
-    theta = grid_row[:, None, None] * freq_row[None] + grid_col[:, None, None] * freq_col[None]
-    return (jnp.cos(theta), jnp.sin(theta))
-
-
-def rotate(heads, cosine, sine):
-    half_width = heads.shape[-1] // 2
-    first = heads[..., :half_width]
-    second = heads[..., half_width:]
-    return jnp.concatenate(
-        [first * cosine - second * sine, first * sine + second * cosine], axis=-1
+    lane_row = jnp.concatenate([freq_row, freq_row], axis=1).reshape(width)
+    lane_col = jnp.concatenate([freq_col, freq_col], axis=1).reshape(width)
+    theta = grid_row[:, None] * lane_row[None] + grid_col[:, None] * lane_col[None]
+    first = (jnp.arange(width, dtype=jnp.int32) % HD) < HD // 2
+    sine = jnp.sin(theta)
+    return jnp.cos(theta), jnp.where(first[None], -sine, sine), first
+
+
+def swap_halves(values, first):
+    return jnp.where(
+        first[None], jnp.roll(values, -(HD // 2), axis=1), jnp.roll(values, HD // 2, axis=1)
     )
 
 
@@ -124,10 +125,8 @@
             mask = seg_r_ref[pl.ds(at, Q_BLOCK), :] == seg_c
             scores = jnp.where(mask, _nt(q_h, k_h) * scale, masked_score)
             top = jnp.max(scores, axis=-1, keepdims=True)
-            shifted = jnp.exp(scores - top)
-            total = jnp.sum(shifted, axis=-1, keepdims=True)
-            log_total = top + jnp.log(total)
-            probs = (shifted * (1.0 / total)).astype(jnp.bfloat16)
+            log_total = top + jnp.log(jnp.sum(jnp.exp(scores - top), axis=-1, keepdims=True))
+            probs = jnp.exp(scores - log_total).astype(jnp.bfloat16)
             o_ref[pl.ds(at, Q_BLOCK), cols] = _nn(probs, v_h).astype(o_ref.dtype)
             lse_ref[pl.ds(at, Q_BLOCK), cols] = jnp.broadcast_to(log_total, (Q_BLOCK, HD))
             return carry
@@ -349,9 +348,7 @@
     )
     row_count, width = tokens.shape
     bin_count = row_count // BIN
-    half_head = HD // 2
     segment, grid_row, grid_col = image_layout(image_table, bin_count, BIN)
-    cosine, sine = rotary_tables(block_parameters[12], grid_row, grid_col)
     input_single_precision = tokens.astype(jnp.float32)
     first_centered_normalized, first_inverse_deviation = layer_norm_forward(input_single_precision)
     first_activation = (
@@ -361,10 +358,13 @@
     qkv_full = matmul(first_activation, block_parameters[2]) + block_parameters[3].astype(
         jnp.float32
     )
-    q_rot = rotate(qkv_full[:, :width].reshape(row_count, H, HD), cosine, sine)
-    k_rot = rotate(qkv_full[:, width : 2 * width].reshape(row_count, H, HD), cosine, sine)
-    q_low = q_rot.reshape(row_count, width).astype(jnp.bfloat16)
-    k_low = k_rot.reshape(row_count, width).astype(jnp.bfloat16)
+    lane_cos, lane_sin, first_half = lane_tables(block_parameters[12], grid_row, grid_col, width)
+    q_full = qkv_full[:, :width]
+    k_full = qkv_full[:, width : 2 * width]
+    q_rot = q_full * lane_cos + swap_halves(q_full, first_half) * lane_sin
+    k_rot = k_full * lane_cos + swap_halves(k_full, first_half) * lane_sin
+    q_low = q_rot.astype(jnp.bfloat16)
+    k_low = k_rot.astype(jnp.bfloat16)
     v_low = qkv_full[:, 2 * width :].astype(jnp.bfloat16)
     mixed, log_total = attention_bins(q_low, k_low, v_low, segment)
     residual_stream = (
@@ -416,25 +416,15 @@
     early_packed, d_mixed = lax.optimization_barrier((early_packed, d_mixed))
     (early_mats, early_vecs), early_mine = sum_on_sparse_core(early_packed, early_layout)
     d_qrot, d_krot, d_value = attention_bins_back(q_low, k_low, v_low, d_mixed, log_total, segment)
-    d_qrot = d_qrot.reshape(row_count, H, HD)
-    d_krot = d_krot.reshape(row_count, H, HD)
-    d_theta = (
-        d_qrot[..., half_head:] * q_rot[..., :half_head]
-        - d_qrot[..., :half_head] * q_rot[..., half_head:]
-    )
-    d_theta = (
-        d_theta
-        + d_krot[..., half_head:] * k_rot[..., :half_head]
-        - d_krot[..., :half_head] * k_rot[..., half_head:]
-    )
-    frequencies_grad = jnp.concatenate(
-        [
-            jnp.sum(grid_row[:, None, None] * d_theta, axis=0).reshape(-1),
-            jnp.sum(grid_col[:, None, None] * d_theta, axis=0).reshape(-1),
-        ]
-    )
-    d_query = rotate(d_qrot, cosine, -sine).reshape(row_count, width)
-    d_key = rotate(d_krot, cosine, -sine).reshape(row_count, width)
+    q_terms = d_qrot * swap_halves(q_rot, first_half)
+    k_terms = d_krot * swap_halves(k_rot, first_half)
+    d_theta = swap_halves(q_terms, first_half) - q_terms
+    d_theta = d_theta + swap_halves(k_terms, first_half) - k_terms
+    row_sums = jnp.sum(grid_row[:, None] * d_theta, axis=0).reshape(H, 2, HD // 2)[:, 0]
+    col_sums = jnp.sum(grid_col[:, None] * d_theta, axis=0).reshape(H, 2, HD // 2)[:, 0]
+    frequencies_grad = jnp.concatenate([row_sums.reshape(-1), col_sums.reshape(-1)])
+    d_query = d_qrot * lane_cos + swap_halves(d_qrot * lane_sin, first_half)
+    d_key = d_krot * lane_cos + swap_halves(d_krot * lane_sin, first_half)
     d_qkv = jnp.concatenate([d_query, d_key, d_value.reshape(row_count, width)], axis=1).astype(
         jnp.bfloat16
     )

time: 587 us -> 672 us (1.14)
  other arithmetic: 80.4 us -> 107 us
  waiting for transfers between devices: 125 us -> 147 us
  local copies, waits for them, and re-layouts: 85.3 us -> 102 us
  Pallas kernels: 115 us -> 128 us
  matrix products: 115 us -> 125 us
    unnamed x6, waiting for transfers between devices: 0.09 us -> 88.6 us
    all_to_all x1, waiting for transfers between devices: 69.1 us -> 2.33 us  [sum_by_exchange(): received = lax.all_to_all(packed, ('fsdp', 'dp'), 0, 0, tiled=True)]
    slice x4 -> x17, local copies, waits for them, and re-layouts: 10.5 us -> 35.8 us  [the longest x10 21.3 us: swap_halves(): jnp.roll(values, HD // 2, axis=1)]
    convert_element_type x0 -> x1, other arithmetic: none -> 17.4 us  [shards(): k_low = k_rot.astype(jnp.bfloat16)]
    mul x0 -> x1, other arithmetic: none -> 13.4 us  [shards(): d_query = d_qrot * lane_cos + swap_halves(d_qrot * lane_sin, first_half)]
    pallas_call x1, Pallas kernels: 48 us -> 61 us  [attention_forward(): pl.pallas_call(attention_forward_kernel, grid=(width // pair,), in_specs=...]
    pallas_call x2 -> x0, local copies, waits for them, and re-layouts: 7.44 us -> none  [attention_backward(): pl.pallas_call(attention_backward_kernel, grid=(width // pair,), in_specs...]
    unnamed x84 -> x100, local copies, waits for them, and re-layouts: 13.5 us -> 19.3 us
  transfers between devices with their start and end apart: 6 -> 6, of which waited for: 2 -> 3; matrix products, arithmetic and copies ran while one was open for 33% -> 32% of each run, Pallas kernels for 20% -> 9%
where the time goes in v7:
time: 672 us; the launch traced here: 662 us
  waiting for transfers between devices  147 us (22%)
  Pallas kernels  128 us (19%)
  matrix products  125 us (19%)
  other arithmetic  107 us (16%)
  local copies, waits for them, and re-layouts  102 us (15%)
  blocking collectives  29.3 us (4%)
  between operations  21 us (3%)
    unnamed x6, waiting for transfers between devices  88.6 us
    pallas_call x1, Pallas kernels, attention_backward(): pl.pallas_call(attention_backward_kernel, grid=(width // pair,), in_specs...  67 us
    dot_general x4, matrix products, matmul(): return jnp.dot(left, right, preferred_element_type=jnp.float32)  61.2 us
    pallas_call x1, Pallas kernels, attention_forward(): pl.pallas_call(attention_forward_kernel, grid=(width // pair,), in_specs=...  61 us
    all_gather x1, waiting for transfers between devices, gather_with_small(): whole = lax.all_gather(joined, ('fsdp', 'dp'), axis=0, tiled=True)  55.8 us
    dot_general x4, matrix products, matmul_right_t(): lax.dot_general(left, right, (((1,), (1,)), ((), ())), preferred_element_...  33.7 us
    dot_general x4, matrix products, matmul_left_t(): lax.dot_general(left, right, (((0,), (0,)), ((), ())), preferred_element_...  29.8 us
    another operation x3, other arithmetic  29.4 us
  transfers between devices with their start and end apart: 6, of which 3 were waited for; matrix products, arithmetic and copies ran while one was open for 32% of the time, Pallas kernels for 9%

profile of v7, /device:TPU:0, one launch (start us, length us, event | category | flops | bytes accessed | tf_op | source)
XLA Modules:
  0.0 662.1 jit_solution(6130891284177588846)
XLA Ops:
  7.3 6.2 concatenate.96
  27.4 55.8 %all-gather.5.cloned.1.call-done = bf16[768,3200]{1,0:T(8,128)(2,1)} async-done(((bf16[24,3200]{1,0:T(8,128)(2,1)}), bf16[768,3200]{1,0:T(8,128)(2,1)}) %all-gather.5.cloned.1.call-update) | async-done | bytes 4915216 | tf_op jit(solution)/shard_map/all_gather | solution.py:233
  85.3 8.6 %convolution_add_fusion = f32[1024,2304]{1,0:T(8,128)} fusion(f32[2304]{0:T(1024)S(1)} %reshape.856, bf16[768,3200]{1,0:T(8,128)(2,1)} %all-gather.5.cloned.1.call-done, bf16[1024,768]{0,1:T(8,128)(2,1)S(1)} %copy.79, f32[768]{0:T(1024)S(1)} %reshape.855, f32[768]{0:T(1024)S(1)} %reshape.854, f32[1024]{0:T(1024)S(1)} %add_rsqrt_fusion.1, ...), kind=kOutput, calls=%fused_computation.32 | convolution fusion | flops 3630956544 | bytes 14572544 | tf_op jit(solution)/shard_map/dot_general | solution.py:20
  93.9 11.6 %fusion.83 = (f32[1024,736]{1,0:T(8,128)}, f32[1024,736]{1,0:T(8,128)}, f32[1024,736]{1,0:T(8,128)}, f32[1024,736]{1,0:T(8,128)}) fusion(f32[1024,2304]{1,0:T(8,128)} %convolution_add_fusion), kind=kLoop, calls=%fused_computation.185 | loop fusion | bytes 24117248 | tf_op jit(solution)/shard_map/jit(_roll_static)/slice | solution.py:72
  112.0 17.4 %fusion.79 = (bf16[1024,768]{1,0:T(8,128)(2,1)}, f32[1024,768]{1,0:T(8,128)S(1)}, bf16[1024,768]{1,0:T(8,128)(2,1)}, f32[1024,768]{1,0:T(8,128)}) fusion(f32[1024,736]{1,0:T(8,128)} %get-tuple-element.167, f32[1024,32]{1,0:T(8,128)S(1)} %get-tuple-element.171, f32[1024,32]{1,0:T(8,128)S(1)} %get-tuple-element.170, f32[1024,736]{1,0:T(8,128)} %get-tuple-element.166, ...), kind=kLoop, calls=%fused_computation.183 | loop fusion | flops 14942208 | bytes 28326656 | tf_op jit(solution)/shard_map/convert_element_type | solution.py:367
  129.4 9.3 %fusion.94 = (f32[1024,736]{1,0:T(8,128)}, f32[1024,736]{1,0:T(8,128)}, f32[1024,736]{1,0:T(8,128)}, f32[1024,736]{1,0:T(8,128)}) fusion(f32[1024,768]{1,0:T(8,128)} %get-tuple-element.165, f32[1024,768]{1,0:T(8,128)S(1)} %get-tuple-element.161), kind=kLoop, calls=%fused_computation.196 | loop fusion | bytes 24117248 | tf_op jit(solution)/shard_map/jit(_roll_static)/slice | solution.py:72
  141.7 61.0 %attention_forward.1 = (bf16[1024,768]{1,0:T(8,128)(2,1)}, f32[1024,768]{1,0:T(8,128)}) custom-call(bf16[1024,768]{1,0:T(8,128)(2,1)} %get-tuple-element.164.q_ref, bf16[1024,768]{1,0:T(8,128)(2,1)} %get-tuple-element.160.k_ref, bf16[1024,768]{1,0:T(8,128)(2,1)} %slice.507.v_ref, s32[1024,1]{1,0:T(8,128)} %copy.80.seg_r_ref, s32[1,1024]{1,0:T(1,128)} %bitcast.32), custom_call_target="tpu_custom_call" | custom-call | flops 3221225472 | bytes 9437184 | tf_op jit(solution)/shard_map/attention_forward/pallas_call | solution.py:175
  208.3 39.1 %fusion.3 = (bf16[1024,3072]{1,0:T(8,128)(2,1)}, f32[1024,3072]{1,0:T(8,128)}) fusion(f32[3072]{0:T(1024)S(1)} %reshape.860, bf16[768,3072]{1,0:T(8,128)(2,1)} %all-gather.7.cloned.1.call-done, f32[1024,768]{0,1:T(8,128)} %copy-done.4, f32[768]{0:T(1024)S(1)} %reshape.859, f32[768]{0:T(1024)S(1)} %reshape.858, f32[1024]{0:T(1024)S(1)} %add_rsqrt_fusion, ...), kind=kOutput, calls=%fused_computation.6 | convolution fusion | flops 5043388416 | bytes 26765312 | tf_op jit(solution)/shard_map/dot_general | solution.py:20
  247.5 13.5 %fusion.102 = (bf16[3072]{0:T(1024)(128)(2,1)S(1)}, bf16[1024,3072]{1,0:T(8,128)(2,1)}) fusion(f32[1024,3072]{1,0:T(8,128)} %get-tuple-element.238, f32[3072]{0:T(1024)S(1)} %reshape.860, bf16[3072,768]{1,0:T(8,128)(2,1)} %all-gather.9.cloned.1.call-done, bf16[1024,768]{1,0:T(8,128)(2,1)S(1)} %copy-done.16), kind=kOutput, calls=%fused_computation.204 | convolution fusion | flops 4869583872 | bytes 25184256 | tf_op jit(solution)/shard_map/dot_general | solution.py:30
  261.0 9.9 %convolution_convert_fusion = bf16[768,3072]{1,0:T(8,128)(2,1)} fusion(bf16[1024,3072]{1,0:T(8,128)(2,1)} %get-tuple-element.234, f32[1024,768]{0,1:T(8,128)} %copy-done.4, f32[768]{0:T(1024)S(1)} %reshape.859, f32[768]{0:T(1024)S(1)} %reshape.858, f32[1024]{0:T(1024)S(1)} %add_rsqrt_fusion, f32[1024]{0:T(1024)S(1)} %broadcast_multiply_fusion.4), kind=kOutput, calls=%fused_computation.33 | convolution fusion | flops 4838129664 | bytes 14170112 | tf_op jit(solution)/shard_map/dot_general | solution.py:24
  270.9 6.8 %fusion.103 = (bf16[768]{0:T(1024)(128)(2,1)S(1)}, f32[1024,768]{1,0:T(8,128)}) fusion(bf16[1024,3072]{1,0:T(8,128)(2,1)S(1)} %copy-done.47, bf16[768,3072]{1,0:T(8,128)(2,1)S(1)} %copy-done.46), kind=kOutput, calls=%fused_computation.205 | convolution fusion | flops 4832623616 | bytes 14157312 | tf_op jit(solution)/shard_map/dot_general | solution.py:30
  295.0 9.7 %convolution_convert_fusion.1 = bf16[3072,768]{1,0:T(8,128)(2,1)} fusion(bf16[1024,3072]{1,0:T(8,128)(2,1)} %get-tuple-element.237, bf16[1024,768]{1,0:T(8,128)(2,1)S(1)} %copy-done.16), kind=kOutput, calls=%fused_computation.34 | convolution fusion | flops 4834197504 | bytes 12582912 | tf_op jit(solution)/shard_map/dot_general | solution.py:24
  304.7 8.5 %convert_element_type.254 = bf16[768,3072]{1,0:T(8,128)(2,1)} reshape(bf16[3072,768]{1,0:T(8,128)(2,1)} %convolution_convert_fusion.1) | data formatting | bytes 9437184 | tf_op jit(solution)/shard_map/convert_element_type | solution.py:260
  313.2 8.8 %fusion.17 = bf16[768,7040]{1,0:T(8,128)(2,1)} fusion(bf16[768,8]{1,0:T(8,128)(2,1)S(1)} %reshape.835, bf16[768,768]{1,0:T(8,128)(2,1)S(1)} %convolution_convert_fusion.4, bf16[768,3072]{1,0:T(8,128)(2,1)} %convolution_convert_fusion, bf16[768,3072]{1,0:T(8,128)(2,1)} %convert_element_type.254), kind=kLoop, calls=%fused_computation.28 | loop fusion | flops 54067200 | bytes 21442560 | tf_op jit(solution)/shard_map/concatenate | solution.py:262
  326.9 67.0 %attention_backward.1 = (f32[1024,768]{1,0:T(8,128)}, f32[1024,768]{1,0:T(8,128)}, f32[1024,768]{1,0:T(8,128)}) custom-call(bf16[1024,768]{1,0:T(8,128)(2,1)} %get-tuple-element.164.q_ref, bf16[1024,768]{1,0:T(8,128)(2,1)} %get-tuple-element.160.k_ref, bf16[1024,768]{1,0:T(8,128)(2,1)} %slice.507.v_ref, bf16[1024,768]{1,0:T(8,128)(2,1)} %convolution_convert_fusion.3.d_ref, ...), custom_call_target="tpu_custom_call" | custom-call | flops 6442450944 | bytes 18874368 | tf_op jit(solution)/shard_map/attention_backward/pallas_call | solution.py:195
  393.9 13.4 %fusion.51 = f32[1024,768]{1,0:T(8,128)} fusion(f32[1024,768]{1,0:T(8,128)} %get-tuple-element.53, f32[768]{0:T(1024)S(1)} %copy-done.29, f32[1024]{0:T(1024)S(1)} %copy-done.27, f32[768]{0:T(1024)S(1)} %copy-done.31, f32[1024]{0:T(1024)S(1)} %copy-done.25, pred[768]{0:T(1024)(128)(4,1)S(1)} %copy-done.40), kind=kLoop, calls=%fused_computation.93 | loop fusion | flops 4718592 | bytes 6306560 | tf_op jit(solution)/shard_map/mul | solution.py:426
  416.1 14.7 %fusion.41 = (bf16[1024,768]{1,0:T(8,128)(2,1)}, f32[1024,768]{1,0:T(8,128)S(1)}, f32[1024,768]{1,0:T(8,128)S(1)}) fusion(f32[1024,32]{1,0:T(8,128)S(1)} %get-tuple-element.179, f32[1024,736]{1,0:T(8,128)S(1)} %get-tuple-element.181, f32[1024,736]{1,0:T(8,128)S(1)} %get-tuple-element.180, f32[1024,32]{1,0:T(8,128)S(1)} %get-tuple-element.178, ...), kind=kLoop, calls=%fused_computation.69 | loop fusion | flops 12582912 | bytes 26753792 | tf_op jit(solution)/shard_map/convert.32
  434.8 12.6 %fusion.43 = (bf16[1024,768]{1,0:T(8,128)(2,1)S(1)}, f32[1024,768]{1,0:T(8,128)S(1)}) fusion(f32[1024,32]{1,0:T(8,128)S(1)} %get-tuple-element.183, f32[1024,736]{1,0:T(8,128)S(1)} %get-tuple-element.185, f32[1024,736]{1,0:T(8,128)S(1)} %get-tuple-element.184, f32[1024,32]{1,0:T(8,128)S(1)} %get-tuple-element.182, f32[1024,768]{1,0:T(8,128)S(1)} %copy-done.13, ...), kind=kLoop, calls=%fused_computation.72 | loop fusion | flops 10223616 | bytes 20462336 | tf_op jit(solution)/shard_map/convert.33
  456.1 8.6 %fusion.104 = (bf16[768]{0:T(1024)(128)(2,1)S(1)}, f32[1024,768]{1,0:T(8,128)}) fusion(bf16[768,3200]{1,0:T(8,128)(2,1)} %all-gather.5.cloned.1.call-done, bf16[1024,768]{1,0:T(8,128)(2,1)S(1)} %convert.85, bf16[1024,768]{1,0:T(8,128)(2,1)S(1)} %get-tuple-element.176, bf16[1024,768]{1,0:T(8,128)(2,1)} %get-tuple-element.174), kind=kOutput, calls=%fused_computation.206 | convolution fusion | flops 3638820096 | bytes 11404800 | tf_op jit(solution)/shard_map/dot_general | solution.py:30
  474.9 6.4 convolution_convert_fusion.2
  492.6 88.5 %reduce-scatter.4.cloned.1.call-done = bf16[24,7040]{1,0:T(8,128)(2,1)} async-done(((bf16[768,7040]{1,0:T(8,128)(2,1)}), bf16[24,7040]{1,0:T(8,128)(2,1)}) %reduce-scatter.4.cloned.1.call-update) | async-done | bytes 337936
  581.2 10.2 %add_convert_fusion = bf16[1024,768]{0,1:T(8,128)(2,1)} fusion(f32[1024,768]{0,1:T(8,128)} %copy-done.4, bf16[1024,3072]{1,0:T(8,128)(2,1)} %get-tuple-element.237, bf16[3072,768]{1,0:T(8,128)(2,1)} %all-gather.9.cloned.1.call-done, f32[768]{0:T(1024)S(1)} %reshape.861), kind=kOutput, calls=%fused_computation.87 | convolution fusion | flops 4834197504 | bytes 15731712 | tf_op jit(solution)/shard_map/dot_general | solution.py:20
  608.6 9.2 %all_gather.18 = f32[96,2560]{1,0:T(8,128)S(1)} all-gather(f32[24,2560]{1,0:T(8,128)S(1)} %pad_maximum_fusion.1), channel_id=1, replica_groups=mesh['fsdp'=8,'dp'=4] {'dp'}, dimensions={0}, use_global_device_ids=true | all-gather | bytes 1228800 | tf_op jit(solution)/shard_map/all_gather | solution.py:305
  618.5 20.0 %all-reduce.5 = (f32[]{:T(128)}, f32[]{:T(128)}) all-reduce(f32[]{:T(128)} %bitcast.12, f32[]{:T(128)} %bitcast.13), channel_id=1, replica_groups=mesh['fsdp'=8,'dp'=4] {'fsdp'}, use_global_device_ids=true, to_apply=%region_30.31 | all-reduce | flops 2 | bytes 16 | tf_op jit(solution)/shard_map/psum | solution.py:454
  (236 shorter events, 124.2 us)
Async XLA Ops:
  7.2 75.9 %all-gather.5.cloned.1.call-start = ((), (), s32[]{:S(2)}) async-start(), calls=%async_computation.2 | async-start | bytes 5068800 | tf_op jit(solution)/shard_map/all_gather | solution.py:233
  16.0 192.3 %all-gather.7.cloned.1.call-start = ((), (), s32[]{:S(2)}) async-start(), calls=%async_computation.3 | async-start | bytes 4866048 | tf_op jit(solution)/shard_map/all_gather | solution.py:246
  16.8 230.7 %all-gather.9.cloned.1.call-start = ((), (), s32[]{:S(2)}) async-start(), calls=%async_computation.4 | async-start | bytes 4866048 | tf_op jit(solution)/shard_map/all_gather | solution.py:246
  18.4 562.8 %reduce-scatter.4.cloned.1.call-start = ((), (), s32[]{:S(2)}) async-start(), calls=%async_computation.6 | async-start | bytes 11151360
  18.5 93.5 %copy-start.39 = (pred[768]{0:T(1024)(128)(4,1)}, pred[768]{0:T(1024)(128)(4,1)S(1)}, u32[]{:S(2)}) copy-start(pred[768]{0:T(1024)(128)(4,1)S(1)} %fusion.67) | copy-start | bytes 2308
  20.2 182.5 %copy-start.2 = (bf16[1024,768]{0,1:T(8,128)(2,1)}, bf16[1024,768]{0,1:T(8,128)(2,1)S(1)}, u32[]{:S(2)}) copy-start(bf16[1024,768]{0,1:T(8,128)(2,1)S(1)} %copy.79) | copy-start | bytes 4718596
  20.5 64.7 %copy-start.32 = (f32[1024]{0:T(1024)}, f32[1024]{0:T(1024)S(1)}, u32[]{:S(2)}) copy-start(f32[1024]{0:T(1024)S(1)} %broadcast_multiply_fusion.5) | copy-start | bytes 12292
  21.0 72.9 %copy-start.34 = (f32[1024]{0:T(1024)}, f32[1024]{0:T(1024)S(1)}, u32[]{:S(2)}) copy-start(f32[1024]{0:T(1024)S(1)} %add_rsqrt_fusion.1) | copy-start | bytes 12292
  21.4 72.5 %copy-start.41 = (s32[1024]{0:T(1024)}, s32[1024]{0:T(1024)S(1)}, u32[]{:S(2)}) copy-start(s32[1024]{0:T(1024)S(1)} %get-tuple-element.217) | copy-start | bytes 12292
  21.4 90.6 %copy-start.24 = (f32[1024]{0:T(1024)}, f32[1024]{0:T(1024)S(1)}, u32[]{:S(2)}) copy-start(f32[1024]{0:T(1024)S(1)} %get-tuple-element.212) | copy-start | bytes 12292
  21.4 90.6 %copy-start.26 = (f32[1024]{0:T(1024)}, f32[1024]{0:T(1024)S(1)}, u32[]{:S(2)}) copy-start(f32[1024]{0:T(1024)S(1)} %get-tuple-element.213) | copy-start | bytes 12292
  111.7 17.6 %copy-start.28 = (f32[768]{0:T(1024)}, f32[768]{0:T(1024)S(1)}, u32[]{:S(2)}) copy-start(f32[768]{0:T(1024)S(1)} %mul.316) | copy-start | bytes 9220
  112.0 17.4 %copy-start.30 = (f32[768]{0:T(1024)}, f32[768]{0:T(1024)S(1)}, u32[]{:S(2)}) copy-start(f32[768]{0:T(1024)S(1)} %mul.311) | copy-start | bytes 9220
  208.3 39.1 %copy-start.16 = (bf16[1024,768]{1,0:T(8,128)(2,1)S(1)}, bf16[1024,768]{1,0:T(8,128)(2,1)}, u32[]{:S(2)}) copy-start(bf16[1024,768]{1,0:T(8,128)(2,1)} %param.35) | copy-start | bytes 4718596
  261.0 9.9 %copy-start.46 = (bf16[768,3072]{1,0:T(8,128)(2,1)S(1)}, bf16[768,3072]{1,0:T(8,128)(2,1)}, u32[]{:S(2)}) copy-start(bf16[768,3072]{1,0:T(8,128)(2,1)} %all-gather.7.cloned.1.call-done) | copy-start | bytes 14155780
  261.0 9.9 %copy-start.47 = (bf16[1024,3072]{1,0:T(8,128)(2,1)S(1)}, bf16[1024,3072]{1,0:T(8,128)(2,1)}, u32[]{:S(2)}) copy-start(bf16[1024,3072]{1,0:T(8,128)(2,1)} %get-tuple-element.234) | copy-start | bytes 18874372
  326.9 67.0 %copy-start.25 = (f32[1024]{0:T(1024)S(1)}, f32[1024]{0:T(1024)}, u32[]{:S(2)}) copy-start(f32[1024]{0:T(1024)} %copy-done.24) | copy-start | bytes 12292
  326.9 67.0 %copy-start.27 = (f32[1024]{0:T(1024)S(1)}, f32[1024]{0:T(1024)}, u32[]{:S(2)}) copy-start(f32[1024]{0:T(1024)} %copy-done.26) | copy-start | bytes 12292
  326.9 67.0 %copy-start.29 = (f32[768]{0:T(1024)S(1)}, f32[768]{0:T(1024)}, u32[]{:S(2)}) copy-start(f32[768]{0:T(1024)} %copy-done.28) | copy-start | bytes 9220
  326.9 67.0 %copy-start.31 = (f32[768]{0:T(1024)S(1)}, f32[768]{0:T(1024)}, u32[]{:S(2)}) copy-start(f32[768]{0:T(1024)} %copy-done.30) | copy-start | bytes 9220
  326.9 67.1 %copy-start.40 = (pred[768]{0:T(1024)(128)(4,1)S(1)}, pred[768]{0:T(1024)(128)(4,1)}, u32[]{:S(2)}) copy-start(pred[768]{0:T(1024)(128)(4,1)} %copy-done.39) | copy-start | bytes 2308
  488.2 109.7 %all-to-all-start = ((bf16[32,24,2432]{2,1,0:T(8,128)(2,1)}), bf16[32,24,2432]{2,1,0:T(8,128)(2,1)}, u32[]{:S(2)}, u32[]{:S(2)}) async-start(bf16[32,24,2432]{2,1,0:T(8,128)(2,1)} %bitcast.30), calls=%async_computation | async-start | bytes 7471104 | tf_op jit(solution)/shard_map/all_to_all | solution.py:300
  491.9 151.6 %all-gather.11.cloned.1.call-start = ((), (), s32[]{:S(2)}) async-start(), calls=%async_computation.5 | async-start | bytes 1689600 | tf_op jit(solution)/shard_map/all_gather | solution.py:294
  594.1 10.4 %copy-start.23 = (bf16[24,7040]{1,0:T(8,128)(2,1)S(1)}, bf16[24,7040]{1,0:T(8,128)(2,1)}, u32[]{:S(2)}) copy-start(bf16[24,7040]{1,0:T(8,128)(2,1)} %reduce-scatter.4.cloned.1.call-done) | copy-start | bytes 1013764
  (30 other events, 147.4 us)
Sparse Core Ops, SparseCore 0:
  16.1 66.9 all-gather.4
  86.0 61.9 all-gather.6
  150.9 61.7 all-gather.8
  407.5 173.6 reduce-scatter.3
  582.6 16.9 all-gather.10

commit v8 on v6

--- a/solution.py
+++ b/solution.py
@@ -8,7 +8,7 @@
 H = 12
 HD = 64
 BIN = 1024
-Q_BLOCK = 256
+Q_BLOCK = 1024
 
 
 norm_eps = 1e-06
@@ -124,10 +124,8 @@
             mask = seg_r_ref[pl.ds(at, Q_BLOCK), :] == seg_c
             scores = jnp.where(mask, _nt(q_h, k_h) * scale, masked_score)
             top = jnp.max(scores, axis=-1, keepdims=True)
-            shifted = jnp.exp(scores - top)
-            total = jnp.sum(shifted, axis=-1, keepdims=True)
-            log_total = top + jnp.log(total)
-            probs = (shifted * (1.0 / total)).astype(jnp.bfloat16)
+            log_total = top + jnp.log(jnp.sum(jnp.exp(scores - top), axis=-1, keepdims=True))
+            probs = jnp.exp(scores - log_total).astype(jnp.bfloat16)
             o_ref[pl.ds(at, Q_BLOCK), cols] = _nn(probs, v_h).astype(o_ref.dtype)
             lse_ref[pl.ds(at, Q_BLOCK), cols] = jnp.broadcast_to(log_total, (Q_BLOCK, HD))
             return carry

time: 587 us -> 570 us (0.971)
  Pallas kernels: 115 us -> 91.9 us
  waiting for transfers between devices: 125 us -> 133 us
    unnamed x6, waiting for transfers between devices: 0.09 us -> 24.3 us
    pallas_call x1, Pallas kernels: 66.9 us -> 47.4 us  [attention_backward(): pl.pallas_call(attention_backward_kernel, grid=(width // pair,), in_specs...]
    all_to_all x1, waiting for transfers between devices: 69.1 us -> 50.3 us  [sum_by_exchange(): received = lax.all_to_all(packed, ('fsdp', 'dp'), 0, 0, tiled=True)]
  transfers between devices with their start and end apart: 6 -> 6, of which waited for: 2 -> 4; matrix products, arithmetic and copies ran while one was open for 33% -> 33% of each run, Pallas kernels for 20% -> 16%
where the time goes in v8:
time: 570 us; the launch traced here: 561 us
  waiting for transfers between devices  133 us (23%)
  matrix products  116 us (20%)
  Pallas kernels  91.9 us (16%)
  local copies, waits for them, and re-layouts  85.4 us (15%)
  other arithmetic  80.2 us (14%)
  blocking collectives  29.6 us (5%)
  between operations  21.1 us (4%)
    dot_general x4, matrix products, matmul(): return jnp.dot(left, right, preferred_element_type=jnp.float32)  59.2 us
    all_gather x1, waiting for transfers between devices, gather_with_small(): whole = lax.all_gather(joined, ('fsdp', 'dp'), axis=0, tiled=True)  55.7 us
    all_to_all x1, waiting for transfers between devices, sum_by_exchange(): received = lax.all_to_all(packed, ('fsdp', 'dp'), 0, 0, tiled=True)  50.3 us
    pallas_call x1, Pallas kernels, attention_backward(): pl.pallas_call(attention_backward_kernel, grid=(width // pair,), in_specs...  47.4 us
    pallas_call x1, Pallas kernels, attention_forward(): pl.pallas_call(attention_forward_kernel, grid=(width // pair,), in_specs=...  44.5 us
    dot_general x4, matrix products, matmul_right_t(): lax.dot_general(left, right, (((1,), (1,)), ((), ())), preferred_element_...  31.5 us
    another operation x3, other arithmetic  26.5 us
    dot_general x4, matrix products, matmul_left_t(): lax.dot_general(left, right, (((0,), (0,)), ((), ())), preferred_element_...  24.9 us
  transfers between devices with their start and end apart: 6, of which 4 were waited for; matrix products, arithmetic and copies ran while one was open for 33% of the time, Pallas kernels for 16%

profile of v8, /device:TPU:0, one launch (start us, length us, event | category | flops | bytes accessed | tf_op | source)
XLA Modules:
  0.0 560.9 jit_solution(235507564092884984)
XLA Ops:
  9.0 6.1 %concatenate.56 = bf16[1344]{0:T(1024)(128)(2,1)S(1)} concatenate(bf16[96]{0:T(256)(128)(2,1)} %param.22, bf16[96]{0:T(256)(128)(2,1)} %param.23, bf16[288]{0:T(512)(128)(2,1)} %param.25, bf16[96]{0:T(256)(128)(2,1)} %param.27, bf16[96]{0:T(256)(128)(2,1)} %param.28, bf16[96]{0:T(256)(128)(2,1)} %param.29, bf16[384]{0:T(512)(128)(2,1)} %param.31, bf16[96]{0:T(256)(128)(2,1)} %param.33, ...), dimensions={0} | concatenate | bytes 5376 | tf_op jit(solution)/shard_map/concatenate | solution.py:227
  27.5 55.7 %all-gather.5.cloned.1.call-done = bf16[768,3200]{1,0:T(8,128)(2,1)} async-done(((bf16[24,3200]{1,0:T(8,128)(2,1)}), bf16[768,3200]{1,0:T(8,128)(2,1)}) %all-gather.5.cloned.1.call-update) | async-done | bytes 4915216 | tf_op jit(solution)/shard_map/all_gather | solution.py:232
  85.2 6.3 %convolution_add_fusion = f32[1024,2304]{1,0:T(8,128)S(1)} fusion(f32[2304]{0:T(1024)S(1)} %reshape.866, bf16[768,3200]{1,0:T(8,128)(2,1)} %all-gather.5.cloned.1.call-done, bf16[1024,768]{0,1:T(8,128)(2,1)S(1)} %copy.87, f32[768]{0:T(1024)S(1)} %reshape.865, f32[768]{0:T(1024)S(1)} %reshape.864, f32[1024]{0:T(1024)S(1)} %add_rsqrt_fusion.1, ...), kind=kOutput, calls=%fused_computation.32 | convolution fusion | flops 3630956544 | bytes 14572544 | tf_op jit(solution)/shard_map/dot_general | solution.py:20
  103.6 10.8 %fusion.60 = (bf16[1024,12,32]{0,2,1:T(8,128)(2,1)S(1)}, bf16[1024,12,32]{0,2,1:T(8,128)(2,1)S(1)}, bf16[1024,12,32]{0,2,1:T(8,128)(2,1)S(1)}, bf16[1024,12,32]{0,2,1:T(8,128)(2,1)S(1)}) fusion(f32[1024,12,64]{0,2,1:T(8,128)} %bitcast.40, f32[12,32]{1,0:T(8,128)S(1)} %mul.346, f32[1024]{0:T(1024)S(1)} %get-tuple-element.165, f32[12,32]{1,0:T(8,128)S(1)} %mul.341, ...), kind=kLoop, calls=%fused_computation.162 | loop fusion | flops 7471104 | bytes 9448448 | tf_op jit(solution)/shard_map/convert.51
  121.8 44.5 %attention_forward.1 = (bf16[1024,768]{1,0:T(8,128)(2,1)}, f32[1024,768]{1,0:T(8,128)}) custom-call(bf16[1024,768]{1,0:T(8,128)(2,1)} %copy.90.q_ref, bf16[1024,768]{1,0:T(8,128)(2,1)} %copy.91.k_ref, bf16[1024,768]{1,0:T(8,128)(2,1)} %slice.405.v_ref, s32[1024,1]{1,0:T(8,128)} %copy.92.seg_r_ref, s32[1,1024]{1,0:T(1,128)} %bitcast.51), custom_call_target="tpu_custom_call" | custom-call | flops 3221225472 | bytes 9437184 | tf_op jit(solution)/shard_map/attention_forward/pallas_call | solution.py:174
  172.1 39.0 %fusion.3 = (bf16[1024,3072]{1,0:T(8,128)(2,1)}, f32[1024,3072]{1,0:T(8,128)}) fusion(f32[3072]{0:T(1024)S(1)} %reshape.870, bf16[768,3072]{1,0:T(8,128)(2,1)} %all-gather.7.cloned.1.call-done, f32[1024,768]{0,1:T(8,128)} %copy-done.5, f32[768]{0:T(1024)S(1)} %reshape.869, f32[768]{0:T(1024)S(1)} %reshape.868, f32[1024]{0:T(1024)S(1)} %add_rsqrt_fusion, ...), kind=kOutput, calls=%fused_computation.6 | convolution fusion | flops 5043388416 | bytes 26765312 | tf_op jit(solution)/shard_map/dot_general | solution.py:20
  214.0 11.9 %fusion.72 = (bf16[3072]{0:T(1024)(128)(2,1)S(1)}, bf16[1024,3072]{1,0:T(8,128)(2,1)S(1)}) fusion(f32[1024,3072]{1,0:T(8,128)} %get-tuple-element.191, f32[3072]{0:T(1024)S(1)} %reshape.870, bf16[3072,768]{1,0:T(8,128)(2,1)} %all-gather.9.cloned.1.call-done, bf16[1024,768]{1,0:T(8,128)(2,1)S(1)} %copy-done.12), kind=kOutput, calls=%fused_computation.172 | convolution fusion | flops 4869583872 | bytes 25184256 | tf_op jit(solution)/shard_map/dot_general | solution.py:30
  225.9 7.2 %convolution_convert_fusion = bf16[768,3072]{1,0:T(8,128)(2,1)} fusion(bf16[1024,3072]{1,0:T(8,128)(2,1)S(1)} %get-tuple-element.187, f32[1024,768]{0,1:T(8,128)S(1)} %copy-done.6, f32[768]{0:T(1024)S(1)} %reshape.869, f32[768]{0:T(1024)S(1)} %reshape.868, f32[1024]{0:T(1024)S(1)} %add_rsqrt_fusion, f32[1024]{0:T(1024)S(1)} %broadcast_multiply_fusion.4), kind=kOutput, calls=%fused_computation.33 | convolution fusion | flops 4838129664 | bytes 14170112 | tf_op jit(solution)/shard_map/dot_general | solution.py:24
  233.0 6.7 %fusion.73 = (bf16[768]{0:T(1024)(128)(2,1)S(1)}, f32[1024,768]{1,0:T(8,128)}) fusion(bf16[1024,3072]{1,0:T(8,128)(2,1)S(1)} %get-tuple-element.187, bf16[768,3072]{1,0:T(8,128)(2,1)S(1)} %copy-done.38), kind=kOutput, calls=%fused_computation.173 | convolution fusion | flops 4832623616 | bytes 14157312 | tf_op jit(solution)/shard_map/dot_general | solution.py:30
  243.2 4.0 multiply_reduce_fusion
  253.3 9.8 %convolution_convert_fusion.1 = bf16[3072,768]{1,0:T(8,128)(2,1)} fusion(bf16[1024,3072]{1,0:T(8,128)(2,1)} %get-tuple-element.190, bf16[1024,768]{1,0:T(8,128)(2,1)S(1)} %copy-done.12), kind=kOutput, calls=%fused_computation.34 | convolution fusion | flops 4834197504 | bytes 12582912 | tf_op jit(solution)/shard_map/dot_general | solution.py:24
  263.0 8.5 %convert_element_type.254 = bf16[768,3072]{1,0:T(8,128)(2,1)} reshape(bf16[3072,768]{1,0:T(8,128)(2,1)} %convolution_convert_fusion.1) | data formatting | bytes 9437184 | tf_op jit(solution)/shard_map/convert_element_type | solution.py:259
  271.5 8.8 %fusion.17 = bf16[768,7040]{1,0:T(8,128)(2,1)} fusion(bf16[768,8]{1,0:T(8,128)(2,1)S(1)} %reshape.843, bf16[768,768]{1,0:T(8,128)(2,1)S(1)} %convolution_convert_fusion.4, bf16[768,3072]{1,0:T(8,128)(2,1)} %convolution_convert_fusion, bf16[768,3072]{1,0:T(8,128)(2,1)} %convert_element_type.254), kind=kLoop, calls=%fused_computation.28 | loop fusion | flops 54067200 | bytes 21442560 | tf_op jit(solution)/shard_map/concatenate | solution.py:261
  280.3 4.8 convolution_convert_fusion.3.d_ref
  285.1 47.4 %attention_backward.1 = (f32[1024,768]{1,0:T(8,128)}, f32[1024,768]{1,0:T(8,128)}, f32[1024,768]{1,0:T(8,128)}) custom-call(bf16[1024,768]{1,0:T(8,128)(2,1)} %copy.90.q_ref, bf16[1024,768]{1,0:T(8,128)(2,1)} %copy.91.k_ref, bf16[1024,768]{1,0:T(8,128)(2,1)} %slice.405.v_ref, bf16[1024,768]{1,0:T(8,128)(2,1)} %convolution_convert_fusion.3.d_ref, ...), custom_call_target="tpu_custom_call" | custom-call | flops 6442450944 | bytes 18874368 | tf_op jit(solution)/shard_map/attention_backward/pallas_call | solution.py:194
  339.8 13.4 %subtract_convert_fusion.1 = (bf16[1024,12,32]{0,2,1:T(8,128)(2,1)S(1)}, f32[1024,12,32]{0,2,1:T(8,128)S(1)}, bf16[1024,12,32]{0,2,1:T(8,128)(2,1)S(1)}, bf16[1024,12,32]{0,2,1:T(8,128)(2,1)}) fusion(f32[1024,12,64]{0,2,1:T(8,128)} %bitcast.42, f32[12,32]{1,0:T(8,128)S(1)} %copy-done.21, f32[1024]{0:T(1024)S(1)} %copy-done.27, f32[12,32]{1,0:T(8,128)S(1)} %copy-done.19, ...), kind=kLoop, calls=%fused_computation.81 | loop fusion | flops 13762560 | bytes 16526336 | tf_op jit(solution)/shard_map/convert.35
  353.3 6.4 %multiply_reduce_fusion.6 = (bf16[12,32]{1,0:T(8,128)(2,1)S(1)}, bf16[12,32]{1,0:T(8,128)(2,1)S(1)}, bf16[1024,12,32]{0,2,1:T(8,128)(2,1)S(1)}) fusion(f32[1024,12,32]{0,2,1:T(8,128)S(1)} %get-tuple-element.146, f32[1024]{0:T(1024)S(1)} %copy-done.25, f32[1024]{0:T(1024)S(1)} %copy-done.27, f32[1024,12,64]{0,2,1:T(8,128)S(1)} %bitcast.43, ...), kind=kLoop, calls=%fused_computation.76 | loop fusion | flops 4717824 | bytes 5517824 | tf_op jit(solution)/shard_map/reduce_sum | solution.py:430
  371.2 8.1 %fusion.74 = (bf16[768]{0:T(1024)(128)(2,1)S(1)}, f32[1024,768]{1,0:T(8,128)}) fusion(bf16[768,3200]{1,0:T(8,128)(2,1)} %all-gather.5.cloned.1.call-done, bf16[1024,768]{1,0:T(8,128)(2,1)S(1)} %convert.109, bf16[1024,768]{1,0:T(8,128)(2,1)S(1)} %copy-done.14, bf16[1024,768]{1,0:T(8,128)(2,1)S(1)} %copy.103), kind=kOutput, calls=%fused_computation.174 | convolution fusion | flops 3638820096 | bytes 11404800 | tf_op jit(solution)/shard_map/dot_general | solution.py:30
  389.6 6.6 %convolution_convert_fusion.2 = bf16[768,2304]{1,0:T(8,128)(2,1)S(1)} fusion(bf16[1024,768]{0,1:T(8,128)(2,1)S(1)} %copy-done.3, f32[768]{0:T(1024)S(1)} %copy-done.36, f32[768]{0:T(1024)S(1)} %copy-done.31, f32[1024]{0:T(1024)S(1)} %copy-done.29, f32[1024]{0:T(1024)S(1)} %copy-done.23, bf16[1024,768]{1,0:T(8,128)(2,1)} %copy-done.15, ...), kind=kOutput, calls=%fused_computation.35 | convolution fusion | flops 3644522496 | bytes 9844736 | tf_op jit(solution)/shard_map/dot_general | solution.py:24
  407.1 24.2 %reduce-scatter.4.cloned.1.call-done = bf16[24,7040]{1,0:T(8,128)(2,1)} async-done(((bf16[768,7040]{1,0:T(8,128)(2,1)}), bf16[24,7040]{1,0:T(8,128)(2,1)}) %reduce-scatter.4.cloned.1.call-update) | async-done | bytes 337936
  431.4 10.4 %add_convert_fusion = bf16[1024,768]{0,1:T(8,128)(2,1)} fusion(f32[1024,768]{0,1:T(8,128)} %copy-done.5, bf16[1024,3072]{1,0:T(8,128)(2,1)} %get-tuple-element.190, bf16[3072,768]{1,0:T(8,128)(2,1)} %all-gather.9.cloned.1.call-done, f32[768]{0:T(1024)S(1)} %reshape.871), kind=kOutput, calls=%fused_computation.61 | convolution fusion | flops 4834197504 | bytes 15731712 | tf_op jit(solution)/shard_map/dot_general | solution.py:20
  446.0 50.3 %all-to-all-done = bf16[32,24,2432]{2,1,0:T(8,128)(2,1)} async-done(((bf16[32,24,2432]{2,1,0:T(8,128)(2,1)}), bf16[32,24,2432]{2,1,0:T(8,128)(2,1)}, u32[]{:S(2)}, u32[]{:S(2)}) %all-to-all-start) | async-done | bytes 3735584 | tf_op jit(solution)/shard_map/all_to_all | solution.py:299
  506.9 9.7 %all_gather.18 = f32[96,2560]{1,0:T(8,128)S(1)} all-gather(f32[24,2560]{1,0:T(8,128)S(1)} %pad_maximum_fusion.5), channel_id=1, replica_groups=mesh['fsdp'=8,'dp'=4] {'dp'}, dimensions={0}, use_global_device_ids=true | all-gather | bytes 1228800 | tf_op jit(solution)/shard_map/all_gather | solution.py:304
  517.2 19.9 %all-reduce.5 = (f32[]{:T(128)}, f32[]{:T(128)}) all-reduce(f32[]{:T(128)} %bitcast.20, f32[]{:T(128)} %bitcast.21), channel_id=1, replica_groups=mesh['fsdp'=8,'dp'=4] {'fsdp'}, use_global_device_ids=true, to_apply=%region_30.31 | all-reduce | flops 2 | bytes 16 | tf_op jit(solution)/shard_map/psum | solution.py:462
  (210 shorter events, 119.3 us)
Async XLA Ops:
  7.2 8.9 %copy-start = (bf16[96,3072]{1,0:T(8,128)(2,1)S(1)}, bf16[96,3072]{1,0:T(8,128)(2,1)}, u32[]{:S(2)}) copy-start(bf16[96,3072]{1,0:T(8,128)(2,1)} %param.30) | copy-start | bytes 1769476
  7.2 75.9 %all-gather.5.cloned.1.call-start = ((), (), s32[]{:S(2)}) async-start(), calls=%async_computation.2 | async-start | bytes 5068800 | tf_op jit(solution)/shard_map/all_gather | solution.py:232
  16.0 156.0 %all-gather.7.cloned.1.call-start = ((), (), s32[]{:S(2)}) async-start(), calls=%async_computation.3 | async-start | bytes 4866048 | tf_op jit(solution)/shard_map/all_gather | solution.py:245
  16.8 197.2 %all-gather.9.cloned.1.call-start = ((), (), s32[]{:S(2)}) async-start(), calls=%async_computation.4 | async-start | bytes 4866048 | tf_op jit(solution)/shard_map/all_gather | solution.py:245
  18.5 412.9 %reduce-scatter.4.cloned.1.call-start = ((), (), s32[]{:S(2)}) async-start(), calls=%async_computation.6 | async-start | bytes 11151360
  20.2 146.1 %copy-start.2 = (bf16[1024,768]{0,1:T(8,128)(2,1)}, bf16[1024,768]{0,1:T(8,128)(2,1)S(1)}, u32[]{:S(2)}) copy-start(bf16[1024,768]{0,1:T(8,128)(2,1)S(1)} %copy.87) | copy-start | bytes 4718596
  20.5 64.7 %copy-start.22 = (f32[1024]{0:T(1024)}, f32[1024]{0:T(1024)S(1)}, u32[]{:S(2)}) copy-start(f32[1024]{0:T(1024)S(1)} %broadcast_multiply_fusion.5) | copy-start | bytes 12292
  21.0 70.6 %copy-start.28 = (f32[1024]{0:T(1024)}, f32[1024]{0:T(1024)S(1)}, u32[]{:S(2)}) copy-start(f32[1024]{0:T(1024)S(1)} %add_rsqrt_fusion.1) | copy-start | bytes 12292
  21.4 70.2 %copy-start.33 = (s32[1024]{0:T(1024)}, s32[1024]{0:T(1024)S(1)}, u32[]{:S(2)}) copy-start(s32[1024]{0:T(1024)S(1)} %get-tuple-element.170) | copy-start | bytes 12292
  21.4 82.2 %copy-start.24 = (f32[1024]{0:T(1024)}, f32[1024]{0:T(1024)S(1)}, u32[]{:S(2)}) copy-start(f32[1024]{0:T(1024)S(1)} %get-tuple-element.164) | copy-start | bytes 12292
  21.4 82.2 %copy-start.26 = (f32[1024]{0:T(1024)}, f32[1024]{0:T(1024)S(1)}, u32[]{:S(2)}) copy-start(f32[1024]{0:T(1024)S(1)} %get-tuple-element.165) | copy-start | bytes 12292
  103.5 10.9 %copy-start.18 = (f32[12,32]{1,0:T(8,128)}, f32[12,32]{1,0:T(8,128)S(1)}, u32[]{:S(2)}) copy-start(f32[12,32]{1,0:T(8,128)S(1)} %mul.341) | copy-start | bytes 4612
  103.6 10.8 %copy-start.20 = (f32[12,32]{1,0:T(8,128)}, f32[12,32]{1,0:T(8,128)S(1)}, u32[]{:S(2)}) copy-start(f32[12,32]{1,0:T(8,128)S(1)} %mul.346) | copy-start | bytes 4612
  172.0 41.9 %copy-start.12 = (bf16[1024,768]{1,0:T(8,128)(2,1)S(1)}, bf16[1024,768]{1,0:T(8,128)(2,1)}, u32[]{:S(2)}) copy-start(bf16[1024,768]{1,0:T(8,128)(2,1)} %param.35) | copy-start | bytes 4718596
  214.0 11.9 %copy-start.6 = (f32[1024,768]{0,1:T(8,128)S(1)}, f32[1024,768]{0,1:T(8,128)}, u32[]{:S(2)}) copy-start(f32[1024,768]{0,1:T(8,128)} %copy-done.5) | copy-start | bytes 9437188
  225.9 7.2 %copy-start.38 = (bf16[768,3072]{1,0:T(8,128)(2,1)S(1)}, bf16[768,3072]{1,0:T(8,128)(2,1)}, u32[]{:S(2)}) copy-start(bf16[768,3072]{1,0:T(8,128)(2,1)} %all-gather.7.cloned.1.call-done) | copy-start | bytes 14155780
  339.8 13.5 %copy-start.4 = (f32[1024,768]{0,1:T(8,128)S(1)}, f32[1024,768]{0,1:T(8,128)}, u32[]{:S(2)}) copy-start(f32[1024,768]{0,1:T(8,128)} %copy.101) | copy-start | bytes 9437188
  362.9 8.1 %copy-start.13 = (bf16[1024,768]{1,0:T(8,128)(2,1)}, bf16[1024,768]{1,0:T(8,128)(2,1)S(1)}, u32[]{:S(2)}) copy-start(bf16[1024,768]{1,0:T(8,128)(2,1)S(1)} %copy.103) | copy-start | bytes 4718596
  371.2 8.1 %copy-start.15 = (bf16[1024,768]{1,0:T(8,128)(2,1)}, bf16[1024,768]{1,0:T(8,128)(2,1)S(1)}, u32[]{:S(2)}) copy-start(bf16[1024,768]{1,0:T(8,128)(2,1)S(1)} %convert.109) | copy-start | bytes 4718596
  402.7 93.5 %all-to-all-start = ((bf16[32,24,2432]{2,1,0:T(8,128)(2,1)}), bf16[32,24,2432]{2,1,0:T(8,128)(2,1)}, u32[]{:S(2)}, u32[]{:S(2)}) async-start(bf16[32,24,2432]{2,1,0:T(8,128)(2,1)} %bitcast.44), calls=%async_computation | async-start | bytes 7471104 | tf_op jit(solution)/shard_map/all_to_all | solution.py:299
  406.4 135.7 %all-gather.11.cloned.1.call-start = ((), (), s32[]{:S(2)}) async-start(), calls=%async_computation.5 | async-start | bytes 1689600 | tf_op jit(solution)/shard_map/all_gather | solution.py:293
  431.4 10.4 %copy-start.16 = (bf16[1024,768]{0,1:T(8,128)(2,1)S(1)}, bf16[1024,768]{0,1:T(8,128)(2,1)}, u32[]{:S(2)}) copy-start(bf16[1024,768]{0,1:T(8,128)(2,1)} %fusion.33) | copy-start | bytes 4718596
  443.4 59.3 %copy-start.17 = (bf16[24,7040]{1,0:T(8,128)(2,1)S(1)}, bf16[24,7040]{1,0:T(8,128)(2,1)}, u32[]{:S(2)}) copy-start(bf16[24,7040]{1,0:T(8,128)(2,1)} %reduce-scatter.4.cloned.1.call-done) | copy-start | bytes 1013764
  543.0 8.7 %copy-start.1 = (bf16[96,3072]{1,0:T(8,128)(2,1)S(1)}, bf16[96,3072]{1,0:T(8,128)(2,1)}, u32[]{:S(2)}) copy-start(bf16[96,3072]{1,0:T(8,128)(2,1)} %param.30) | copy-start | bytes 1769476
  (22 other events, 77.5 us)
Sparse Core Ops, SparseCore 0:
  16.1 66.9 all-gather.4
  86.6 61.8 all-gather.6
  152.0 61.9 all-gather.8
  285.2 146.0 reduce-scatter.3
  432.8 30.9 all-gather.10

commit v9 on v8

--- a/solution.py
+++ b/solution.py
@@ -2,6 +2,7 @@
 import jax.numpy as jnp
 from jax import lax
 from jax.experimental import pallas as pl
+from jax.experimental.pallas import tpu as pltpu
 from jax.sharding import PartitionSpec as P
 
 
@@ -109,10 +110,16 @@
     return lax.dot_general(a, b, (((1,), (0,)), ((), ())), preferred_element_type=jnp.float32)
 
 
-def attention_forward_kernel(q_ref, k_ref, v_ref, seg_r_ref, seg_c_ref, o_ref, lse_ref):
+def build_bias(seg_r_ref, seg_c_ref, bias_ref):
+    @pl.when(pl.program_id(0) == 0)
+    def _():
+        bias_ref[...] = jnp.where(seg_r_ref[...] == seg_c_ref[...], 0.0, masked_score).astype(jnp.float32)
+
+
+def attention_forward_kernel(q_ref, k_ref, v_ref, seg_r_ref, seg_c_ref, o_ref, lse_ref, bias_ref):
     rows = q_ref.shape[0]
-    seg_c = seg_c_ref[...]
     scale = HD ** (-0.5)
+    build_bias(seg_r_ref, seg_c_ref, bias_ref)
     for half in range(q_ref.shape[1] // HD):
         cols = slice(half * HD, (half + 1) * HD)
         k_h = k_ref[:, cols]
@@ -121,8 +128,7 @@
         def block(i, carry):
             at = pl.multiple_of(i * Q_BLOCK, Q_BLOCK)
             q_h = q_ref[pl.ds(at, Q_BLOCK), cols]
-            mask = seg_r_ref[pl.ds(at, Q_BLOCK), :] == seg_c
-            scores = jnp.where(mask, _nt(q_h, k_h) * scale, masked_score)
+            scores = _nt(q_h, k_h) * scale + bias_ref[pl.ds(at, Q_BLOCK), :]
             top = jnp.max(scores, axis=-1, keepdims=True)
             log_total = top + jnp.log(jnp.sum(jnp.exp(scores - top), axis=-1, keepdims=True))
             probs = jnp.exp(scores - log_total).astype(jnp.bfloat16)
@@ -133,10 +139,10 @@
         lax.fori_loop(0, rows // Q_BLOCK, block, 0)
 
 
-def attention_backward_kernel(q_ref, k_ref, v_ref, d_ref, lse_ref, seg_r_ref, seg_c_ref, dq_ref, dk_ref, dv_ref):
+def attention_backward_kernel(q_ref, k_ref, v_ref, d_ref, lse_ref, seg_r_ref, seg_c_ref, dq_ref, dk_ref, dv_ref, bias_ref):
     rows = q_ref.shape[0]
-    seg_c = seg_c_ref[...]
     scale = HD ** (-0.5)
+    build_bias(seg_r_ref, seg_c_ref, bias_ref)
     for half in range(q_ref.shape[1] // HD):
         cols = slice(half * HD, (half + 1) * HD)
         k_h = k_ref[:, cols]
@@ -148,8 +154,7 @@
             q_h = q_ref[pl.ds(at, Q_BLOCK), cols]
             d_h = d_ref[pl.ds(at, Q_BLOCK), cols]
             log_total = lse_ref[pl.ds(at, Q_BLOCK), pl.ds(half * HD, 1)]
-            mask = seg_r_ref[pl.ds(at, Q_BLOCK), :] == seg_c
-            scores = jnp.where(mask, _nt(q_h, k_h) * scale, masked_score)
+            scores = _nt(q_h, k_h) * scale + bias_ref[pl.ds(at, Q_BLOCK), :]
             probs = jnp.exp(scores - log_total)
             d_probs = _nt(d_h, v_h)
             dv_acc = dv_acc + _tn(probs.astype(jnp.bfloat16), d_h)
@@ -177,6 +182,7 @@
         in_specs=[spec, spec, spec, pl.BlockSpec((rows, 1), lambda j: (0, 0)), pl.BlockSpec((1, rows), lambda j: (0, 0))],
         out_specs=[spec, spec],
         out_shape=[jax.ShapeDtypeStruct((rows, width), jnp.bfloat16), jax.ShapeDtypeStruct((rows, width), jnp.float32)],
+        scratch_shapes=[pltpu.VMEM((rows, rows), jnp.float32)],
         cost_estimate=pl.CostEstimate(
             flops=4 * rows * rows * width, transcendentals=2 * rows * rows * (width // HD),
             bytes_accessed=rows * width * (2 * 4 + 4)),
@@ -197,6 +203,7 @@
         in_specs=[spec, spec, spec, spec, spec, pl.BlockSpec((rows, 1), lambda j: (0, 0)), pl.BlockSpec((1, rows), lambda j: (0, 0))],
         out_specs=[spec, spec, spec],
         out_shape=[f32, f32, f32],
+        scratch_shapes=[pltpu.VMEM((rows, rows), jnp.float32)],
         cost_estimate=pl.CostEstimate(
             flops=8 * rows * rows * width, transcendentals=rows * rows * (width // HD),
             bytes_accessed=rows * width * (2 * 4 + 4 + 12)),

time: 570 us -> 570 us (level)
  waiting for transfers between devices: 133 us -> 146 us
  Pallas kernels: 91.9 us -> 79.6 us
    pallas_call x1, Pallas kernels: 44.5 us -> 33 us  [attention_forward(): pl.pallas_call(attention_forward_kernel, grid=(width // pair,), in_specs=...]
    all_gather x2, waiting for transfers between devices: 2.89 us -> 14.3 us  [gather_alone(): return lax.all_gather(quarter(shard), ('fsdp', 'dp'), axis=0, tiled=True)]
  transfers between devices with their start and end apart: 6 -> 6, of which waited for: 4 -> 4; matrix products, arithmetic and copies ran while one was open for 33% -> 33% of each run, Pallas kernels for 16% -> 14%
where the time goes in v9:
time: 570 us; the launch traced here: 561 us
  waiting for transfers between devices  146 us (26%)
  matrix products  115 us (20%)
  local copies, waits for them, and re-layouts  85.3 us (15%)
  other arithmetic  80.2 us (14%)
  Pallas kernels  79.6 us (14%)
  blocking collectives  29.7 us (5%)
  between operations  21.1 us (4%)
    dot_general x4, matrix products, matmul(): return jnp.dot(left, right, preferred_element_type=jnp.float32)  59.1 us
    all_gather x1, waiting for transfers between devices, gather_with_small(): whole = lax.all_gather(joined, ('fsdp', 'dp'), axis=0, tiled=True)  55.7 us
    all_to_all x1, waiting for transfers between devices, sum_by_exchange(): received = lax.all_to_all(packed, ('fsdp', 'dp'), 0, 0, tiled=True)  49.1 us
    pallas_call x1, Pallas kernels, attention_backward(): pl.pallas_call(attention_backward_kernel, grid=(width // pair,), in_specs...  46.6 us
    pallas_call x1, Pallas kernels, attention_forward(): pl.pallas_call(attention_forward_kernel, grid=(width // pair,), in_specs=...  33 us
    dot_general x4, matrix products, matmul_right_t(): lax.dot_general(left, right, (((1,), (1,)), ((), ())), preferred_element_...  31.5 us
    unnamed x6, waiting for transfers between devices  26.6 us
    another operation x3, other arithmetic  26.4 us
  transfers between devices with their start and end apart: 6, of which 4 were waited for; matrix products, arithmetic and copies ran while one was open for 33% of the time, Pallas kernels for 14%

profile of v9, /device:TPU:0, one launch (start us, length us, event | category | flops | bytes accessed | tf_op | source)
XLA Modules:
  0.0 560.9 jit_solution(16438364778507401067)
XLA Ops:
  9.0 6.1 %concatenate.56 = bf16[1344]{0:T(1024)(128)(2,1)S(1)} concatenate(bf16[96]{0:T(256)(128)(2,1)} %param.22, bf16[96]{0:T(256)(128)(2,1)} %param.23, bf16[288]{0:T(512)(128)(2,1)} %param.25, bf16[96]{0:T(256)(128)(2,1)} %param.27, bf16[96]{0:T(256)(128)(2,1)} %param.28, bf16[96]{0:T(256)(128)(2,1)} %param.29, bf16[384]{0:T(512)(128)(2,1)} %param.31, bf16[96]{0:T(256)(128)(2,1)} %param.33, ...), dimensions={0} | concatenate | bytes 5376 | tf_op jit(solution)/shard_map/concatenate | solution.py:234
  27.5 55.7 %all-gather.5.cloned.1.call-done = bf16[768,3200]{1,0:T(8,128)(2,1)} async-done(((bf16[24,3200]{1,0:T(8,128)(2,1)}), bf16[768,3200]{1,0:T(8,128)(2,1)}) %all-gather.5.cloned.1.call-update) | async-done | bytes 4915216 | tf_op jit(solution)/shard_map/all_gather | solution.py:239
  85.2 6.3 %convolution_add_fusion = f32[1024,2304]{1,0:T(8,128)S(1)} fusion(f32[2304]{0:T(1024)S(1)} %reshape.866, bf16[768,3200]{1,0:T(8,128)(2,1)} %all-gather.5.cloned.1.call-done, bf16[1024,768]{0,1:T(8,128)(2,1)S(1)} %copy.87, f32[768]{0:T(1024)S(1)} %reshape.865, f32[768]{0:T(1024)S(1)} %reshape.864, f32[1024]{0:T(1024)S(1)} %add_rsqrt_fusion.1, ...), kind=kOutput, calls=%fused_computation.32 | convolution fusion | flops 3630956544 | bytes 14572544 | tf_op jit(solution)/shard_map/dot_general | solution.py:21
  103.6 10.8 %fusion.60 = (bf16[1024,12,32]{0,2,1:T(8,128)(2,1)S(1)}, bf16[1024,12,32]{0,2,1:T(8,128)(2,1)S(1)}, bf16[1024,12,32]{0,2,1:T(8,128)(2,1)S(1)}, bf16[1024,12,32]{0,2,1:T(8,128)(2,1)S(1)}) fusion(f32[1024,12,64]{0,2,1:T(8,128)} %bitcast.40, f32[12,32]{1,0:T(8,128)S(1)} %mul.346, f32[1024]{0:T(1024)S(1)} %get-tuple-element.165, f32[12,32]{1,0:T(8,128)S(1)} %mul.341, ...), kind=kLoop, calls=%fused_computation.162 | loop fusion | flops 7471104 | bytes 9448448 | tf_op jit(solution)/shard_map/convert.51
  121.8 33.0 %attention_forward.1 = (bf16[1024,768]{1,0:T(8,128)(2,1)}, f32[1024,768]{1,0:T(8,128)}) custom-call(bf16[1024,768]{1,0:T(8,128)(2,1)} %copy.90.q_ref, bf16[1024,768]{1,0:T(8,128)(2,1)} %copy.91.k_ref, bf16[1024,768]{1,0:T(8,128)(2,1)} %slice.405.v_ref, s32[1024,1]{1,0:T(8,128)} %copy.92.seg_r_ref, s32[1,1024]{1,0:T(1,128)} %bitcast.51), custom_call_target="tpu_custom_call" | custom-call | flops 3221225472 | bytes 9437184 | tf_op jit(solution)/shard_map/attention_forward/pallas_call | solution.py:179
  160.5 39.0 %fusion.3 = (bf16[1024,3072]{1,0:T(8,128)(2,1)}, f32[1024,3072]{1,0:T(8,128)}) fusion(f32[3072]{0:T(1024)S(1)} %reshape.870, bf16[768,3072]{1,0:T(8,128)(2,1)} %all-gather.7.cloned.1.call-done, f32[1024,768]{0,1:T(8,128)} %copy-done.5, f32[768]{0:T(1024)S(1)} %reshape.869, f32[768]{0:T(1024)S(1)} %reshape.868, f32[1024]{0:T(1024)S(1)} %add_rsqrt_fusion, ...), kind=kOutput, calls=%fused_computation.6 | convolution fusion | flops 5043388416 | bytes 26765312 | tf_op jit(solution)/shard_map/dot_general | solution.py:21
  199.6 14.3 %all-gather.9.cloned.1.call-done = bf16[3072,768]{1,0:T(8,128)(2,1)} async-done(((bf16[96,768]{1,0:T(8,128)(2,1)}), bf16[3072,768]{1,0:T(8,128)(2,1)}) %all-gather.9.cloned.1.call-update) | async-done | bytes 4718608 | tf_op jit(solution)/shard_map/all_gather | solution.py:252
  213.9 11.9 %fusion.72 = (bf16[3072]{0:T(1024)(128)(2,1)S(1)}, bf16[1024,3072]{1,0:T(8,128)(2,1)S(1)}) fusion(f32[1024,3072]{1,0:T(8,128)} %get-tuple-element.191, f32[3072]{0:T(1024)S(1)} %reshape.870, bf16[3072,768]{1,0:T(8,128)(2,1)} %all-gather.9.cloned.1.call-done, bf16[1024,768]{1,0:T(8,128)(2,1)S(1)} %copy-done.12), kind=kOutput, calls=%fused_computation.172 | convolution fusion | flops 4869583872 | bytes 25184256 | tf_op jit(solution)/shard_map/dot_general | solution.py:31
  225.8 7.2 %convolution_convert_fusion = bf16[768,3072]{1,0:T(8,128)(2,1)} fusion(bf16[1024,3072]{1,0:T(8,128)(2,1)S(1)} %get-tuple-element.187, f32[1024,768]{0,1:T(8,128)S(1)} %copy-done.6, f32[768]{0:T(1024)S(1)} %reshape.869, f32[768]{0:T(1024)S(1)} %reshape.868, f32[1024]{0:T(1024)S(1)} %add_rsqrt_fusion, f32[1024]{0:T(1024)S(1)} %broadcast_multiply_fusion.4), kind=kOutput, calls=%fused_computation.33 | convolution fusion | flops 4838129664 | bytes 14170112 | tf_op jit(solution)/shard_map/dot_general | solution.py:25
  233.0 6.7 %fusion.73 = (bf16[768]{0:T(1024)(128)(2,1)S(1)}, f32[1024,768]{1,0:T(8,128)}) fusion(bf16[1024,3072]{1,0:T(8,128)(2,1)S(1)} %get-tuple-element.187, bf16[768,3072]{1,0:T(8,128)(2,1)S(1)} %copy-done.38), kind=kOutput, calls=%fused_computation.173 | convolution fusion | flops 4832623616 | bytes 14157312 | tf_op jit(solution)/shard_map/dot_general | solution.py:31
  253.2 9.8 %convolution_convert_fusion.1 = bf16[3072,768]{1,0:T(8,128)(2,1)} fusion(bf16[1024,3072]{1,0:T(8,128)(2,1)} %get-tuple-element.190, bf16[1024,768]{1,0:T(8,128)(2,1)S(1)} %copy-done.12), kind=kOutput, calls=%fused_computation.34 | convolution fusion | flops 4834197504 | bytes 12582912 | tf_op jit(solution)/shard_map/dot_general | solution.py:25
  262.9 8.5 %convert_element_type.254 = bf16[768,3072]{1,0:T(8,128)(2,1)} reshape(bf16[3072,768]{1,0:T(8,128)(2,1)} %convolution_convert_fusion.1) | data formatting | bytes 9437184 | tf_op jit(solution)/shard_map/convert_element_type | solution.py:266
  271.4 8.8 %fusion.17 = bf16[768,7040]{1,0:T(8,128)(2,1)} fusion(bf16[768,8]{1,0:T(8,128)(2,1)S(1)} %reshape.843, bf16[768,768]{1,0:T(8,128)(2,1)S(1)} %convolution_convert_fusion.4, bf16[768,3072]{1,0:T(8,128)(2,1)} %convolution_convert_fusion, bf16[768,3072]{1,0:T(8,128)(2,1)} %convert_element_type.254), kind=kLoop, calls=%fused_computation.28 | loop fusion | flops 54067200 | bytes 21442560 | tf_op jit(solution)/shard_map/concatenate | solution.py:268
  280.2 4.8 convolution_convert_fusion.3.d_ref
  285.1 46.6 %attention_backward.1 = (f32[1024,768]{1,0:T(8,128)}, f32[1024,768]{1,0:T(8,128)}, f32[1024,768]{1,0:T(8,128)}) custom-call(bf16[1024,768]{1,0:T(8,128)(2,1)} %copy.90.q_ref, bf16[1024,768]{1,0:T(8,128)(2,1)} %copy.91.k_ref, bf16[1024,768]{1,0:T(8,128)(2,1)} %slice.405.v_ref, bf16[1024,768]{1,0:T(8,128)(2,1)} %convolution_convert_fusion.3.d_ref, ...), custom_call_target="tpu_custom_call" | custom-call | flops 6442450944 | bytes 18874368 | tf_op jit(solution)/shard_map/attention_backward/pallas_call | solution.py:200
  338.9 13.5 %subtract_convert_fusion.1 = (bf16[1024,12,32]{0,2,1:T(8,128)(2,1)S(1)}, f32[1024,12,32]{0,2,1:T(8,128)S(1)}, bf16[1024,12,32]{0,2,1:T(8,128)(2,1)S(1)}, bf16[1024,12,32]{0,2,1:T(8,128)(2,1)}) fusion(f32[1024,12,64]{0,2,1:T(8,128)} %bitcast.42, f32[12,32]{1,0:T(8,128)S(1)} %copy-done.21, f32[1024]{0:T(1024)S(1)} %copy-done.27, f32[12,32]{1,0:T(8,128)S(1)} %copy-done.19, ...), kind=kLoop, calls=%fused_computation.81 | loop fusion | flops 13762560 | bytes 16526336 | tf_op jit(solution)/shard_map/convert.35
  352.4 6.4 %multiply_reduce_fusion.6 = (bf16[12,32]{1,0:T(8,128)(2,1)S(1)}, bf16[12,32]{1,0:T(8,128)(2,1)S(1)}, bf16[1024,12,32]{0,2,1:T(8,128)(2,1)S(1)}) fusion(f32[1024,12,32]{0,2,1:T(8,128)S(1)} %get-tuple-element.146, f32[1024]{0:T(1024)S(1)} %copy-done.25, f32[1024]{0:T(1024)S(1)} %copy-done.27, f32[1024,12,64]{0,2,1:T(8,128)S(1)} %bitcast.43, ...), kind=kLoop, calls=%fused_computation.76 | loop fusion | flops 4717824 | bytes 5517824 | tf_op jit(solution)/shard_map/reduce_sum | solution.py:437
  370.0 8.2 %fusion.74 = (bf16[768]{0:T(1024)(128)(2,1)S(1)}, f32[1024,768]{1,0:T(8,128)}) fusion(bf16[768,3200]{1,0:T(8,128)(2,1)} %all-gather.5.cloned.1.call-done, bf16[1024,768]{1,0:T(8,128)(2,1)S(1)} %convert.109, bf16[1024,768]{1,0:T(8,128)(2,1)S(1)} %copy-done.14, bf16[1024,768]{1,0:T(8,128)(2,1)S(1)} %copy.103), kind=kOutput, calls=%fused_computation.174 | convolution fusion | flops 3638820096 | bytes 11404800 | tf_op jit(solution)/shard_map/dot_general | solution.py:31
  388.5 6.4 %convolution_convert_fusion.2 = bf16[768,2304]{1,0:T(8,128)(2,1)S(1)} fusion(bf16[1024,768]{0,1:T(8,128)(2,1)S(1)} %copy-done.3, f32[768]{0:T(1024)S(1)} %copy-done.36, f32[768]{0:T(1024)S(1)} %copy-done.31, f32[1024]{0:T(1024)S(1)} %copy-done.29, f32[1024]{0:T(1024)S(1)} %copy-done.23, bf16[1024,768]{1,0:T(8,128)(2,1)} %copy-done.15, ...), kind=kOutput, calls=%fused_computation.35 | convolution fusion | flops 3644522496 | bytes 9844736 | tf_op jit(solution)/shard_map/dot_general | solution.py:25
  405.8 26.5 %reduce-scatter.4.cloned.1.call-done = bf16[24,7040]{1,0:T(8,128)(2,1)} async-done(((bf16[768,7040]{1,0:T(8,128)(2,1)}), bf16[24,7040]{1,0:T(8,128)(2,1)}) %reduce-scatter.4.cloned.1.call-update) | async-done | bytes 337936
  432.4 10.4 %add_convert_fusion = bf16[1024,768]{0,1:T(8,128)(2,1)} fusion(f32[1024,768]{0,1:T(8,128)} %copy-done.5, bf16[1024,3072]{1,0:T(8,128)(2,1)} %get-tuple-element.190, bf16[3072,768]{1,0:T(8,128)(2,1)} %all-gather.9.cloned.1.call-done, f32[768]{0:T(1024)S(1)} %reshape.871), kind=kOutput, calls=%fused_computation.61 | convolution fusion | flops 4834197504 | bytes 15731712 | tf_op jit(solution)/shard_map/dot_general | solution.py:21
  447.1 49.1 %all-to-all-done = bf16[32,24,2432]{2,1,0:T(8,128)(2,1)} async-done(((bf16[32,24,2432]{2,1,0:T(8,128)(2,1)}), bf16[32,24,2432]{2,1,0:T(8,128)(2,1)}, u32[]{:S(2)}, u32[]{:S(2)}) %all-to-all-start) | async-done | bytes 3735584 | tf_op jit(solution)/shard_map/all_to_all | solution.py:306
  506.8 9.7 %all_gather.18 = f32[96,2560]{1,0:T(8,128)S(1)} all-gather(f32[24,2560]{1,0:T(8,128)S(1)} %pad_maximum_fusion.5), channel_id=1, replica_groups=mesh['fsdp'=8,'dp'=4] {'dp'}, dimensions={0}, use_global_device_ids=true | all-gather | bytes 1228800 | tf_op jit(solution)/shard_map/all_gather | solution.py:311
  517.2 19.9 %all-reduce.5 = (f32[]{:T(128)}, f32[]{:T(128)}) all-reduce(f32[]{:T(128)} %bitcast.20, f32[]{:T(128)} %bitcast.21), channel_id=1, replica_groups=mesh['fsdp'=8,'dp'=4] {'fsdp'}, use_global_device_ids=true, to_apply=%region_30.31 | all-reduce | flops 2 | bytes 16 | tf_op jit(solution)/shard_map/psum | solution.py:469
  (210 shorter events, 120.2 us)
Async XLA Ops:
  7.2 8.9 %copy-start = (bf16[96,3072]{1,0:T(8,128)(2,1)S(1)}, bf16[96,3072]{1,0:T(8,128)(2,1)}, u32[]{:S(2)}) copy-start(bf16[96,3072]{1,0:T(8,128)(2,1)} %param.30) | copy-start | bytes 1769476
  7.2 75.9 %all-gather.5.cloned.1.call-start = ((), (), s32[]{:S(2)}) async-start(), calls=%async_computation.2 | async-start | bytes 5068800 | tf_op jit(solution)/shard_map/all_gather | solution.py:239
  16.0 144.5 %all-gather.7.cloned.1.call-start = ((), (), s32[]{:S(2)}) async-start(), calls=%async_computation.3 | async-start | bytes 4866048 | tf_op jit(solution)/shard_map/all_gather | solution.py:252
  16.8 197.1 %all-gather.9.cloned.1.call-start = ((), (), s32[]{:S(2)}) async-start(), calls=%async_computation.4 | async-start | bytes 4866048 | tf_op jit(solution)/shard_map/all_gather | solution.py:252
  18.5 413.9 %reduce-scatter.4.cloned.1.call-start = ((), (), s32[]{:S(2)}) async-start(), calls=%async_computation.6 | async-start | bytes 11151360
  20.2 134.6 %copy-start.2 = (bf16[1024,768]{0,1:T(8,128)(2,1)}, bf16[1024,768]{0,1:T(8,128)(2,1)S(1)}, u32[]{:S(2)}) copy-start(bf16[1024,768]{0,1:T(8,128)(2,1)S(1)} %copy.87) | copy-start | bytes 4718596
  20.5 64.7 %copy-start.22 = (f32[1024]{0:T(1024)}, f32[1024]{0:T(1024)S(1)}, u32[]{:S(2)}) copy-start(f32[1024]{0:T(1024)S(1)} %broadcast_multiply_fusion.5) | copy-start | bytes 12292
  21.0 70.6 %copy-start.28 = (f32[1024]{0:T(1024)}, f32[1024]{0:T(1024)S(1)}, u32[]{:S(2)}) copy-start(f32[1024]{0:T(1024)S(1)} %add_rsqrt_fusion.1) | copy-start | bytes 12292
  21.4 70.2 %copy-start.33 = (s32[1024]{0:T(1024)}, s32[1024]{0:T(1024)S(1)}, u32[]{:S(2)}) copy-start(s32[1024]{0:T(1024)S(1)} %get-tuple-element.170) | copy-start | bytes 12292
  21.4 82.2 %copy-start.24 = (f32[1024]{0:T(1024)}, f32[1024]{0:T(1024)S(1)}, u32[]{:S(2)}) copy-start(f32[1024]{0:T(1024)S(1)} %get-tuple-element.164) | copy-start | bytes 12292
  21.4 82.2 %copy-start.26 = (f32[1024]{0:T(1024)}, f32[1024]{0:T(1024)S(1)}, u32[]{:S(2)}) copy-start(f32[1024]{0:T(1024)S(1)} %get-tuple-element.165) | copy-start | bytes 12292
  103.5 10.9 %copy-start.18 = (f32[12,32]{1,0:T(8,128)}, f32[12,32]{1,0:T(8,128)S(1)}, u32[]{:S(2)}) copy-start(f32[12,32]{1,0:T(8,128)S(1)} %mul.341) | copy-start | bytes 4612
  103.6 10.8 %copy-start.20 = (f32[12,32]{1,0:T(8,128)}, f32[12,32]{1,0:T(8,128)S(1)}, u32[]{:S(2)}) copy-start(f32[12,32]{1,0:T(8,128)S(1)} %mul.346) | copy-start | bytes 4612
  160.5 53.4 %copy-start.12 = (bf16[1024,768]{1,0:T(8,128)(2,1)S(1)}, bf16[1024,768]{1,0:T(8,128)(2,1)}, u32[]{:S(2)}) copy-start(bf16[1024,768]{1,0:T(8,128)(2,1)} %param.35) | copy-start | bytes 4718596
  213.9 11.9 %copy-start.6 = (f32[1024,768]{0,1:T(8,128)S(1)}, f32[1024,768]{0,1:T(8,128)}, u32[]{:S(2)}) copy-start(f32[1024,768]{0,1:T(8,128)} %copy-done.5) | copy-start | bytes 9437188
  225.8 7.2 %copy-start.38 = (bf16[768,3072]{1,0:T(8,128)(2,1)S(1)}, bf16[768,3072]{1,0:T(8,128)(2,1)}, u32[]{:S(2)}) copy-start(bf16[768,3072]{1,0:T(8,128)(2,1)} %all-gather.7.cloned.1.call-done) | copy-start | bytes 14155780
  338.9 13.5 %copy-start.4 = (f32[1024,768]{0,1:T(8,128)S(1)}, f32[1024,768]{0,1:T(8,128)}, u32[]{:S(2)}) copy-start(f32[1024,768]{0,1:T(8,128)} %copy.101) | copy-start | bytes 9437188
  361.8 8.0 %copy-start.13 = (bf16[1024,768]{1,0:T(8,128)(2,1)}, bf16[1024,768]{1,0:T(8,128)(2,1)S(1)}, u32[]{:S(2)}) copy-start(bf16[1024,768]{1,0:T(8,128)(2,1)S(1)} %copy.103) | copy-start | bytes 4718596
  370.0 8.2 %copy-start.15 = (bf16[1024,768]{1,0:T(8,128)(2,1)}, bf16[1024,768]{1,0:T(8,128)(2,1)S(1)}, u32[]{:S(2)}) copy-start(bf16[1024,768]{1,0:T(8,128)(2,1)S(1)} %convert.109) | copy-start | bytes 4718596
  401.4 94.7 %all-to-all-start = ((bf16[32,24,2432]{2,1,0:T(8,128)(2,1)}), bf16[32,24,2432]{2,1,0:T(8,128)(2,1)}, u32[]{:S(2)}, u32[]{:S(2)}) async-start(bf16[32,24,2432]{2,1,0:T(8,128)(2,1)} %bitcast.44), calls=%async_computation | async-start | bytes 7471104 | tf_op jit(solution)/shard_map/all_to_all | solution.py:306
  405.1 137.0 %all-gather.11.cloned.1.call-start = ((), (), s32[]{:S(2)}) async-start(), calls=%async_computation.5 | async-start | bytes 1689600 | tf_op jit(solution)/shard_map/all_gather | solution.py:300
  432.4 10.4 %copy-start.16 = (bf16[1024,768]{0,1:T(8,128)(2,1)S(1)}, bf16[1024,768]{0,1:T(8,128)(2,1)}, u32[]{:S(2)}) copy-start(bf16[1024,768]{0,1:T(8,128)(2,1)} %fusion.33) | copy-start | bytes 4718596
  444.4 58.2 %copy-start.17 = (bf16[24,7040]{1,0:T(8,128)(2,1)S(1)}, bf16[24,7040]{1,0:T(8,128)(2,1)}, u32[]{:S(2)}) copy-start(bf16[24,7040]{1,0:T(8,128)(2,1)} %reduce-scatter.4.cloned.1.call-done) | copy-start | bytes 1013764
  543.0 8.7 %copy-start.1 = (bf16[96,3072]{1,0:T(8,128)(2,1)S(1)}, bf16[96,3072]{1,0:T(8,128)(2,1)}, u32[]{:S(2)}) copy-start(bf16[96,3072]{1,0:T(8,128)(2,1)} %param.30) | copy-start | bytes 1769476
  (22 other events, 77.4 us)
Sparse Core Ops, SparseCore 0:
  16.1 66.9 all-gather.4
  86.6 61.8 all-gather.6
  152.0 61.8 all-gather.8
  285.2 147.1 reduce-scatter.3
  433.8 33.0 all-gather.10

commit v10 on v9

--- a/solution.py
+++ b/solution.py
@@ -386,6 +386,8 @@
         jnp.float32
     )
     gelu_low = jax.nn.gelu(up_proj, approximate=False).astype(jnp.bfloat16)
+    fc2_weight_grad = matmul_left_t(gelu_low, cotangent)
+    fc2_recut = fc2_weight_grad.reshape(width, -1).astype(jnp.bfloat16)
     block_out = (
         residual_stream
         + matmul(gelu_low, block_parameters[10])
@@ -393,7 +395,6 @@
     ).astype(jnp.bfloat16)
     output_gradient = cotangent.astype(jnp.float32)
     fc2_bias_grad = jnp.sum(output_gradient, axis=0)
-    fc2_weight_grad = matmul_left_t(gelu_low, cotangent)
     d_up = (matmul_right_t(cotangent, block_parameters[10]) * gelu_slope(up_proj)).astype(
         jnp.bfloat16
     )
@@ -413,12 +414,12 @@
     d_att = residual_gradient.astype(jnp.bfloat16)
     out_bias_grad = jnp.sum(d_att.astype(jnp.float32), axis=0)
     out_weight_grad = matmul_left_t(mixed, d_att)
+    early_packed, early_layout = pack_columns(
+        [fc2_recut, fc1_weight_grad, out_weight_grad],
+        [fc2_bias_grad, fc1_bias_grad, out_bias_grad, second_norm_gain_gradient, ln2_bias_grad],
+    )
+    early_packed, d_att = lax.optimization_barrier((early_packed, d_att))
     d_mixed = matmul_right_t(d_att, block_parameters[4]).astype(jnp.bfloat16)
-    early_packed, early_layout = pack_columns(
-        [fc2_weight_grad.reshape(fc1_weight_grad.shape[0], -1), fc1_weight_grad, out_weight_grad],
-        [fc2_bias_grad, fc1_bias_grad, out_bias_grad, second_norm_gain_gradient, ln2_bias_grad],
-    )
-    early_packed, d_mixed = lax.optimization_barrier((early_packed, d_mixed))
     (early_mats, early_vecs), early_mine = sum_on_sparse_core(early_packed, early_layout)
     d_qrot, d_krot, d_value = attention_bins_back(q_low, k_low, v_low, d_mixed, log_total, segment)
     d_qrot = d_qrot.reshape(row_count, H, HD)

time: 570 us -> 575 us (level)
  matrix products: 115 us -> 124 us
    unnamed x6, waiting for transfers between devices: 26.6 us -> 7.13 us
    all_to_all x1, waiting for transfers between devices: 49.1 us -> 63.6 us  [sum_by_exchange(): received = lax.all_to_all(packed, ('fsdp', 'dp'), 0, 0, tiled=True)]
    dot_general x4, matrix products: 24.8 us -> 31.4 us  [matmul_left_t(): lax.dot_general(left, right, (((0,), (0,)), ((), ())), preferred_element_...]
    all_gather x2, waiting for transfers between devices: 14.3 us -> 20.6 us  [gather_alone(): return lax.all_gather(quarter(shard), ('fsdp', 'dp'), axis=0, tiled=True)]
where the time goes in v10:
time: 575 us; the launch traced here: 566 us
  waiting for transfers between devices  149 us (26%)
  matrix products  124 us (22%)
  local copies, waits for them, and re-layouts  81.1 us (14%)
  Pallas kernels  80 us (14%)
  other arithmetic  77.3 us (13%)
  blocking collectives  29.7 us (5%)
  between operations  21.1 us (4%)
    all_to_all x1, waiting for transfers between devices, sum_by_exchange(): received = lax.all_to_all(packed, ('fsdp', 'dp'), 0, 0, tiled=True)  63.6 us
    all_gather x1, waiting for transfers between devices, gather_with_small(): whole = lax.all_gather(joined, ('fsdp', 'dp'), axis=0, tiled=True)  58 us
    dot_general x4, matrix products, matmul(): return jnp.dot(left, right, preferred_element_type=jnp.float32)  57.8 us
    pallas_call x1, Pallas kernels, attention_backward(): pl.pallas_call(attention_backward_kernel, grid=(width // pair,), in_specs...  47 us
    dot_general x4, matrix products, matmul_right_t(): lax.dot_general(left, right, (((1,), (1,)), ((), ())), preferred_element_...  34.6 us
    pallas_call x1, Pallas kernels, attention_forward(): pl.pallas_call(attention_forward_kernel, grid=(width // pair,), in_specs=...  33 us
    dot_general x4, matrix products, matmul_left_t(): lax.dot_general(left, right, (((0,), (0,)), ((), ())), preferred_element_...  31.4 us
    another operation x3, other arithmetic  23.9 us
  transfers between devices with their start and end apart: 6, of which 4 were waited for; matrix products, arithmetic and copies ran while one was open for 33% of the time, Pallas kernels for 14%

profile of v10, /device:TPU:0, one launch (start us, length us, event | category | flops | bytes accessed | tf_op | source)
XLA Modules:
  0.0 566.3 jit_solution(8406545719727400716)
XLA Ops:
  7.3 6.2 %concatenate.56 = bf16[1344]{0:T(1024)(128)(2,1)S(1)} concatenate(bf16[96]{0:T(256)(128)(2,1)} %param.22, bf16[96]{0:T(256)(128)(2,1)} %param.23, bf16[288]{0:T(512)(128)(2,1)} %param.25, bf16[96]{0:T(256)(128)(2,1)} %param.27, bf16[96]{0:T(256)(128)(2,1)} %param.28, bf16[96]{0:T(256)(128)(2,1)} %param.29, bf16[384]{0:T(512)(128)(2,1)} %param.31, bf16[96]{0:T(256)(128)(2,1)} %param.33, ...), dimensions={0} | concatenate | bytes 5376 | tf_op jit(solution)/shard_map/concatenate | solution.py:234
  25.1 58.0 %all-gather.5.cloned.1.call-done = bf16[768,3200]{1,0:T(8,128)(2,1)} async-done(((bf16[24,3200]{1,0:T(8,128)(2,1)}), bf16[768,3200]{1,0:T(8,128)(2,1)}) %all-gather.5.cloned.1.call-update) | async-done | bytes 4915216 | tf_op jit(solution)/shard_map/all_gather | solution.py:239
  85.3 6.3 %convolution_add_fusion = f32[1024,2304]{1,0:T(8,128)S(1)} fusion(f32[2304]{0:T(1024)S(1)} %reshape.866, bf16[768,3200]{1,0:T(8,128)(2,1)} %all-gather.5.cloned.1.call-done, bf16[1024,768]{0,1:T(8,128)(2,1)S(1)} %copy.87, f32[768]{0:T(1024)S(1)} %reshape.865, f32[768]{0:T(1024)S(1)} %reshape.864, f32[1024]{0:T(1024)S(1)} %add_rsqrt_fusion.1, ...), kind=kOutput, calls=%fused_computation.32 | convolution fusion | flops 3630956544 | bytes 14572544 | tf_op jit(solution)/shard_map/dot_general | solution.py:21
  98.6 4.5 copy.88
  103.2 8.6 %fusion.58 = (bf16[1024,12,32]{0,2,1:T(8,128)(2,1)S(1)}, bf16[1024,12,32]{0,2,1:T(8,128)(2,1)S(1)}, bf16[1024,12,32]{0,2,1:T(8,128)(2,1)S(1)}, bf16[1024,12,32]{0,2,1:T(8,128)(2,1)S(1)}) fusion(f32[1024,12,64]{0,2,1:T(8,128)S(1)} %bitcast.40, f32[12,32]{1,0:T(8,128)S(1)} %mul.346, f32[1024]{0:T(1024)S(1)} %get-tuple-element.165, f32[12,32]{1,0:T(8,128)S(1)} %mul.341, ...), kind=kLoop, calls=%fused_computation.159 | loop fusion | flops 7471104 | bytes 9448448 | tf_op jit(solution)/shard_map/convert.51
  118.3 33.0 %attention_forward.1 = (bf16[1024,768]{1,0:T(8,128)(2,1)}, f32[1024,768]{1,0:T(8,128)}) custom-call(bf16[1024,768]{1,0:T(8,128)(2,1)} %copy.90.q_ref, bf16[1024,768]{1,0:T(8,128)(2,1)} %copy.91.k_ref, bf16[1024,768]{1,0:T(8,128)(2,1)} %slice.405.v_ref, s32[1024,1]{1,0:T(8,128)} %copy.92.seg_r_ref, s32[1,1024]{1,0:T(1,128)} %bitcast.53), custom_call_target="tpu_custom_call" | custom-call | flops 3221225472 | bytes 9437184 | tf_op jit(solution)/shard_map/attention_forward/pallas_call | solution.py:179
  155.6 37.9 %fusion.3 = (bf16[1024,3072]{1,0:T(8,128)(2,1)}, f32[1024,3072]{1,0:T(8,128)}) fusion(f32[3072]{0:T(1024)S(1)} %reshape.870, bf16[768,3072]{1,0:T(8,128)(2,1)} %all-gather.7.cloned.1.call-done, f32[1024,768]{0,1:T(8,128)S(1)} %get-tuple-element.185, f32[768]{0:T(1024)S(1)} %reshape.869, f32[768]{0:T(1024)S(1)} %reshape.868, f32[1024]{0:T(1024)S(1)} %add_rsqrt_fusion, ...), kind=kOutput, calls=%fused_computation.6 | convolution fusion | flops 5043388416 | bytes 26765312 | tf_op jit(solution)/shard_map/dot_general | solution.py:21
  193.5 20.5 %all-gather.9.cloned.1.call-done = bf16[3072,768]{1,0:T(8,128)(2,1)} async-done(((bf16[96,768]{1,0:T(8,128)(2,1)}), bf16[3072,768]{1,0:T(8,128)(2,1)}) %all-gather.9.cloned.1.call-update) | async-done | bytes 4718608 | tf_op jit(solution)/shard_map/all_gather | solution.py:252
  214.0 13.9 %fusion.73 = (bf16[3072]{0:T(1024)(128)(2,1)S(1)}, bf16[1024,3072]{1,0:T(8,128)(2,1)}) fusion(f32[1024,3072]{1,0:T(8,128)} %get-tuple-element.191, f32[3072]{0:T(1024)S(1)} %reshape.870, bf16[3072,768]{1,0:T(8,128)(2,1)} %all-gather.9.cloned.1.call-done, bf16[1024,768]{1,0:T(8,128)(2,1)} %param.35), kind=kOutput, calls=%fused_computation.171 | convolution fusion | flops 4869583872 | bytes 25184256 | tf_op jit(solution)/shard_map/dot_general | solution.py:31
  228.0 9.9 %convolution_convert_fusion = bf16[768,3072]{1,0:T(8,128)(2,1)} fusion(bf16[1024,3072]{1,0:T(8,128)(2,1)} %get-tuple-element.187, f32[1024,768]{0,1:T(8,128)S(1)} %get-tuple-element.185, f32[768]{0:T(1024)S(1)} %reshape.869, f32[768]{0:T(1024)S(1)} %reshape.868, f32[1024]{0:T(1024)S(1)} %add_rsqrt_fusion, f32[1024]{0:T(1024)S(1)} %broadcast_multiply_fusion.4), kind=kOutput, calls=%fused_computation.33 | convolution fusion | flops 4838129664 | bytes 14170112 | tf_op jit(solution)/shard_map/dot_general | solution.py:25
  238.0 6.8 %fusion.74 = (bf16[768]{0:T(1024)(128)(2,1)S(1)}, f32[1024,768]{1,0:T(8,128)}) fusion(bf16[1024,3072]{1,0:T(8,128)(2,1)S(1)} %copy-done.39, bf16[768,3072]{1,0:T(8,128)(2,1)S(1)} %copy-done.38), kind=kOutput, calls=%fused_computation.172 | convolution fusion | flops 4832623616 | bytes 14157312 | tf_op jit(solution)/shard_map/dot_general | solution.py:31
  259.2 9.8 %convolution_convert_fusion.1 = bf16[3072,768]{1,0:T(8,128)(2,1)} fusion(bf16[1024,3072]{1,0:T(8,128)(2,1)} %get-tuple-element.190, bf16[1024,768]{1,0:T(8,128)(2,1)S(1)} %copy-done.12), kind=kOutput, calls=%fused_computation.34 | convolution fusion | flops 4834197504 | bytes 12582912 | tf_op jit(solution)/shard_map/dot_general | solution.py:25
  269.0 8.5 %convert_element_type.254 = bf16[768,3072]{1,0:T(8,128)(2,1)} reshape(bf16[3072,768]{1,0:T(8,128)(2,1)} %convolution_convert_fusion.1) | data formatting | bytes 9437184 | tf_op jit(solution)/shard_map/convert_element_type | solution.py:390
  277.5 9.3 %fusion.17 = bf16[768,7040]{1,0:T(8,128)(2,1)} fusion(bf16[768,8]{1,0:T(8,128)(2,1)S(1)} %reshape.843, bf16[768,768]{1,0:T(8,128)(2,1)} %convolution_convert_fusion.4, bf16[768,3072]{1,0:T(8,128)(2,1)} %convolution_convert_fusion, bf16[768,3072]{1,0:T(8,128)(2,1)} %convert_element_type.254), kind=kLoop, calls=%fused_computation.28 | loop fusion | flops 54067200 | bytes 21442560 | tf_op jit(solution)/shard_map/concatenate | solution.py:268
  291.2 47.0 %attention_backward.1 = (f32[1024,768]{1,0:T(8,128)}, f32[1024,768]{1,0:T(8,128)}, f32[1024,768]{1,0:T(8,128)}) custom-call(bf16[1024,768]{1,0:T(8,128)(2,1)} %copy.90.q_ref, bf16[1024,768]{1,0:T(8,128)(2,1)} %copy.91.k_ref, bf16[1024,768]{1,0:T(8,128)(2,1)} %slice.405.v_ref, bf16[1024,768]{1,0:T(8,128)(2,1)} %convolution_convert_fusion.3.d_ref, ...), custom_call_target="tpu_custom_call" | custom-call | flops 6442450944 | bytes 18874368 | tf_op jit(solution)/shard_map/attention_backward/pallas_call | solution.py:200
  345.3 12.0 %subtract_convert_fusion.1 = (bf16[1024,12,32]{0,2,1:T(8,128)(2,1)}, f32[1024,12,32]{0,2,1:T(8,128)S(1)}, bf16[1024,12,32]{0,2,1:T(8,128)(2,1)}, bf16[1024,12,32]{0,2,1:T(8,128)(2,1)}) fusion(f32[1024,12,64]{0,2,1:T(8,128)} %bitcast.44, f32[12,32]{1,0:T(8,128)S(1)} %copy-done.19, f32[1024]{0:T(1024)S(1)} %copy-done.27, f32[12,32]{1,0:T(8,128)S(1)} %copy-done.21, ...), kind=kLoop, calls=%fused_computation.81 | loop fusion | flops 13762560 | bytes 16526336 | tf_op jit(solution)/shard_map/convert.35
  357.3 7.1 %multiply_reduce_fusion.6 = (bf16[12,32]{1,0:T(8,128)(2,1)S(1)}, bf16[12,32]{1,0:T(8,128)(2,1)S(1)}, bf16[1024,12,32]{0,2,1:T(8,128)(2,1)}) fusion(f32[1024,12,32]{0,2,1:T(8,128)S(1)} %get-tuple-element.146, f32[1024]{0:T(1024)S(1)} %copy-done.25, f32[1024]{0:T(1024)S(1)} %copy-done.27, f32[1024,12,64]{0,2,1:T(8,128)S(1)} %bitcast.45, ...), kind=kLoop, calls=%fused_computation.76 | loop fusion | flops 4717824 | bytes 5517824 | tf_op jit(solution)/shard_map/reduce_sum | solution.py:438
  377.3 9.6 %fusion.75 = (bf16[768]{0:T(1024)(128)(2,1)S(1)}, f32[1024,768]{1,0:T(8,128)}) fusion(bf16[768,3200]{1,0:T(8,128)(2,1)} %all-gather.5.cloned.1.call-done, bf16[1024,768]{1,0:T(8,128)(2,1)} %convert.109, bf16[1024,768]{1,0:T(8,128)(2,1)} %copy.104, bf16[1024,768]{1,0:T(8,128)(2,1)} %copy.103), kind=kOutput, calls=%fused_computation.173 | convolution fusion | flops 3638820096 | bytes 11404800 | tf_op jit(solution)/shard_map/dot_general | solution.py:31
  397.4 7.2 %convolution_convert_fusion.2 = bf16[768,2304]{1,0:T(8,128)(2,1)S(1)} fusion(bf16[1024,768]{0,1:T(8,128)(2,1)} %copy-done.4, f32[768]{0:T(1024)S(1)} %copy-done.36, f32[768]{0:T(1024)S(1)} %copy-done.31, f32[1024]{0:T(1024)S(1)} %copy-done.29, f32[1024]{0:T(1024)S(1)} %copy-done.23, bf16[1024,768]{1,0:T(8,128)(2,1)} %convert.109, ...), kind=kOutput, calls=%fused_computation.35 | convolution fusion | flops 3644522496 | bytes 9844736 | tf_op jit(solution)/shard_map/dot_general | solution.py:25
  416.7 7.1 %reduce-scatter.4.cloned.1.call-done = bf16[24,7040]{1,0:T(8,128)(2,1)} async-done(((bf16[768,7040]{1,0:T(8,128)(2,1)}), bf16[24,7040]{1,0:T(8,128)(2,1)}) %reduce-scatter.4.cloned.1.call-update) | async-done | bytes 337936
  423.8 9.8 %add_convert_fusion = bf16[1024,768]{0,1:T(8,128)(2,1)} fusion(f32[1024,768]{0,1:T(8,128)S(1)} %get-tuple-element.185, bf16[1024,3072]{1,0:T(8,128)(2,1)} %get-tuple-element.190, bf16[3072,768]{1,0:T(8,128)(2,1)} %all-gather.9.cloned.1.call-done, f32[768]{0:T(1024)S(1)} %reshape.871), kind=kOutput, calls=%fused_computation.61 | convolution fusion | flops 4834197504 | bytes 15731712 | tf_op jit(solution)/shard_map/dot_general | solution.py:21
  437.9 63.6 %all-to-all-done = bf16[32,24,2432]{2,1,0:T(8,128)(2,1)} async-done(((bf16[32,24,2432]{2,1,0:T(8,128)(2,1)}), bf16[32,24,2432]{2,1,0:T(8,128)(2,1)}, u32[]{:S(2)}, u32[]{:S(2)}) %all-to-all-start) | async-done | bytes 3735584 | tf_op jit(solution)/shard_map/all_to_all | solution.py:306
  512.2 9.5 %all_gather.18 = f32[96,2560]{1,0:T(8,128)S(1)} all-gather(f32[24,2560]{1,0:T(8,128)S(1)} %pad_maximum_fusion.5), channel_id=1, replica_groups=mesh['fsdp'=8,'dp'=4] {'dp'}, dimensions={0}, use_global_device_ids=true | all-gather | bytes 1228800 | tf_op jit(solution)/shard_map/all_gather | solution.py:311
  522.3 20.2 %all-reduce.5 = (f32[]{:T(128)}, f32[]{:T(128)}) all-reduce(f32[]{:T(128)} %bitcast.20, f32[]{:T(128)} %bitcast.21), channel_id=1, replica_groups=mesh['fsdp'=8,'dp'=4] {'fsdp'}, use_global_device_ids=true, to_apply=%region_30.31 | all-reduce | flops 2 | bytes 16 | tf_op jit(solution)/shard_map/psum | solution.py:470
  (210 shorter events, 118.9 us)
Async XLA Ops:
  7.2 8.9 %copy-start = (bf16[96,3072]{1,0:T(8,128)(2,1)S(1)}, bf16[96,3072]{1,0:T(8,128)(2,1)}, u32[]{:S(2)}) copy-start(bf16[96,3072]{1,0:T(8,128)(2,1)} %param.30) | copy-start | bytes 1769476
  7.2 76.0 %all-gather.5.cloned.1.call-start = ((), (), s32[]{:S(2)}) async-start(), calls=%async_computation.2 | async-start | bytes 5068800 | tf_op jit(solution)/shard_map/all_gather | solution.py:239
  16.0 139.6 %all-gather.7.cloned.1.call-start = ((), (), s32[]{:S(2)}) async-start(), calls=%async_computation.3 | async-start | bytes 4866048 | tf_op jit(solution)/shard_map/all_gather | solution.py:252
  16.8 197.3 %all-gather.9.cloned.1.call-start = ((), (), s32[]{:S(2)}) async-start(), calls=%async_computation.4 | async-start | bytes 4866048 | tf_op jit(solution)/shard_map/all_gather | solution.py:252
  18.5 405.3 %reduce-scatter.4.cloned.1.call-start = ((), (), s32[]{:S(2)}) async-start(), calls=%async_computation.6 | async-start | bytes 11151360
  20.3 71.2 %copy-start.4 = (bf16[1024,768]{0,1:T(8,128)(2,1)}, bf16[1024,768]{0,1:T(8,128)(2,1)S(1)}, u32[]{:S(2)}) copy-start(bf16[1024,768]{0,1:T(8,128)(2,1)S(1)} %copy.87) | copy-start | bytes 4718596
  20.6 64.6 %copy-start.22 = (f32[1024]{0:T(1024)}, f32[1024]{0:T(1024)S(1)}, u32[]{:S(2)}) copy-start(f32[1024]{0:T(1024)S(1)} %broadcast_multiply_fusion.5) | copy-start | bytes 12292
  21.1 70.5 %copy-start.28 = (f32[1024]{0:T(1024)}, f32[1024]{0:T(1024)S(1)}, u32[]{:S(2)}) copy-start(f32[1024]{0:T(1024)S(1)} %add_rsqrt_fusion.1) | copy-start | bytes 12292
  21.5 70.1 %copy-start.33 = (s32[1024]{0:T(1024)}, s32[1024]{0:T(1024)S(1)}, u32[]{:S(2)}) copy-start(s32[1024]{0:T(1024)S(1)} %get-tuple-element.170) | copy-start | bytes 12292
  21.5 81.7 %copy-start.24 = (f32[1024]{0:T(1024)}, f32[1024]{0:T(1024)S(1)}, u32[]{:S(2)}) copy-start(f32[1024]{0:T(1024)S(1)} %get-tuple-element.164) | copy-start | bytes 12292
  21.5 81.6 %copy-start.26 = (f32[1024]{0:T(1024)}, f32[1024]{0:T(1024)S(1)}, u32[]{:S(2)}) copy-start(f32[1024]{0:T(1024)S(1)} %get-tuple-element.165) | copy-start | bytes 12292
  85.2 6.4 %copy-start.35 = (f32[768]{0:T(1024)}, f32[768]{0:T(1024)S(1)}, u32[]{:S(2)}) copy-start(f32[768]{0:T(1024)S(1)} %reshape.865) | copy-start | bytes 9220
  85.3 6.3 %copy-start.30 = (f32[768]{0:T(1024)}, f32[768]{0:T(1024)S(1)}, u32[]{:S(2)}) copy-start(f32[768]{0:T(1024)S(1)} %reshape.864) | copy-start | bytes 9220
  98.5 15.4 %copy-start.6 = (f32[1024,768]{0,1:T(8,128)}, f32[1024,768]{0,1:T(8,128)S(1)}, u32[]{:S(2)}) copy-start(f32[1024,768]{0,1:T(8,128)S(1)} %copy.89) | copy-start | bytes 9437188
  98.6 4.6 copy-start.18
  98.6 4.5 copy-start.20
  228.0 9.9 %copy-start.38 = (bf16[768,3072]{1,0:T(8,128)(2,1)S(1)}, bf16[768,3072]{1,0:T(8,128)(2,1)}, u32[]{:S(2)}) copy-start(bf16[768,3072]{1,0:T(8,128)(2,1)} %all-gather.7.cloned.1.call-done) | copy-start | bytes 14155780
  228.0 9.9 %copy-start.39 = (bf16[1024,3072]{1,0:T(8,128)(2,1)S(1)}, bf16[1024,3072]{1,0:T(8,128)(2,1)}, u32[]{:S(2)}) copy-start(bf16[1024,3072]{1,0:T(8,128)(2,1)} %get-tuple-element.187) | copy-start | bytes 18874372
  345.3 12.1 %copy-start.7 = (f32[1024,768]{0,1:T(8,128)S(1)}, f32[1024,768]{0,1:T(8,128)}, u32[]{:S(2)}) copy-start(f32[1024,768]{0,1:T(8,128)} %copy.101) | copy-start | bytes 9437188
  397.4 9.4 %copy-start.8 = (f32[1024,768]{0,1:T(8,128)S(1)}, f32[1024,768]{0,1:T(8,128)}, u32[]{:S(2)}) copy-start(f32[1024,768]{0,1:T(8,128)} %copy.105) | copy-start | bytes 9437188
  412.3 89.2 %all-to-all-start = ((bf16[32,24,2432]{2,1,0:T(8,128)(2,1)}), bf16[32,24,2432]{2,1,0:T(8,128)(2,1)}, u32[]{:S(2)}, u32[]{:S(2)}) async-start(bf16[32,24,2432]{2,1,0:T(8,128)(2,1)} %bitcast.46), calls=%async_computation | async-start | bytes 7471104 | tf_op jit(solution)/shard_map/all_to_all | solution.py:306
  416.0 131.5 %all-gather.11.cloned.1.call-start = ((), (), s32[]{:S(2)}) async-start(), calls=%async_computation.5 | async-start | bytes 1689600 | tf_op jit(solution)/shard_map/all_gather | solution.py:300
  436.3 71.7 %copy-start.17 = (bf16[24,7040]{1,0:T(8,128)(2,1)S(1)}, bf16[24,7040]{1,0:T(8,128)(2,1)}, u32[]{:S(2)}) copy-start(bf16[24,7040]{1,0:T(8,128)(2,1)} %reduce-scatter.4.cloned.1.call-done) | copy-start | bytes 1013764
  550.3 6.8 %copy-start.1 = (bf16[96,3072]{1,0:T(8,128)(2,1)S(1)}, bf16[96,3072]{1,0:T(8,128)(2,1)}, u32[]{:S(2)}) copy-start(bf16[96,3072]{1,0:T(8,128)(2,1)} %param.30) | copy-start | bytes 1769476
  (22 other events, 76.6 us)
Sparse Core Ops, SparseCore 0:
  16.1 66.9 all-gather.4
  86.6 61.9 all-gather.6
  152.1 61.9 all-gather.8
  287.0 136.7 reduce-scatter.3
  425.2 26.1 all-gather.10

commit v11 on v10

--- a/solution.py
+++ b/solution.py
@@ -307,9 +307,15 @@
     mine = jnp.sum(received.reshape(blocks, -1, packed.shape[1]).astype(jnp.float32), axis=0)
     freq_part, rest_part = square_sums_of_block(mine, layout, 1)
     rest_part = rest_part + carried
-    extra = jnp.zeros((mine.shape[0], 128), jnp.float32).at[0, 0].set(freq_part).at[0, 1].set(rest_part)
-    owned = lax.all_gather(jnp.concatenate([mine, extra], axis=1), "dp", axis=0, tiled=True)
-    partials = jnp.sum(owned[:: mine.shape[0], packed.shape[1] : packed.shape[1] + 2], axis=0)
+    pair = jnp.stack([freq_part, rest_part])
+    high = pair.astype(jnp.bfloat16)
+    low = (pair - high.astype(jnp.float32)).astype(jnp.bfloat16)
+    extra = jnp.zeros((mine.shape[0], 128), jnp.bfloat16).at[0, 0:2].set(high).at[0, 2:4].set(low)
+    owned = lax.all_gather(
+        jnp.concatenate([mine.astype(jnp.bfloat16), extra], axis=1), "dp", axis=0, tiled=True
+    )
+    tile = owned[:: mine.shape[0], packed.shape[1] : packed.shape[1] + 4].astype(jnp.float32)
+    partials = jnp.sum(tile[:, 0:2] + tile[:, 2:4], axis=0)
     return unpack_columns(owned[:, : packed.shape[1]], layout), partials
 
 
@@ -414,12 +420,12 @@
     d_att = residual_gradient.astype(jnp.bfloat16)
     out_bias_grad = jnp.sum(d_att.astype(jnp.float32), axis=0)
     out_weight_grad = matmul_left_t(mixed, d_att)
+    d_mixed = matmul_right_t(d_att, block_parameters[4]).astype(jnp.bfloat16)
     early_packed, early_layout = pack_columns(
         [fc2_recut, fc1_weight_grad, out_weight_grad],
         [fc2_bias_grad, fc1_bias_grad, out_bias_grad, second_norm_gain_gradient, ln2_bias_grad],
     )
-    early_packed, d_att = lax.optimization_barrier((early_packed, d_att))
-    d_mixed = matmul_right_t(d_att, block_parameters[4]).astype(jnp.bfloat16)
+    early_packed, d_mixed = lax.optimization_barrier((early_packed, d_mixed))
     (early_mats, early_vecs), early_mine = sum_on_sparse_core(early_packed, early_layout)
     d_qrot, d_krot, d_value = attention_bins_back(q_low, k_low, v_low, d_mixed, log_total, segment)
     d_qrot = d_qrot.reshape(row_count, H, HD)

time: 575 us -> 573 us (level)
  matrix products: 124 us -> 114 us
  other arithmetic: 77.3 us -> 86.4 us
    all_to_all x1, waiting for transfers between devices: 63.6 us -> 77.3 us  [sum_by_exchange(): received = lax.all_to_all(packed, ('fsdp', 'dp'), 0, 0, tiled=True)]
    unnamed x6, waiting for transfers between devices: 7.13 us -> 0.08 us
    dot_general x4, matrix products: 31.4 us -> 24.8 us  [matmul_left_t(): lax.dot_general(left, right, (((0,), (0,)), ((), ())), preferred_element_...]
    another operation x3 -> x6, other arithmetic: 23.9 us -> 29.7 us
  transfers between devices with their start and end apart: 6 -> 6, of which waited for: 4 -> 3; matrix products, arithmetic and copies ran while one was open for 33% -> 33% of each run, Pallas kernels for 14% -> 14%
where the time goes in v11:
time: 573 us; the launch traced here: 564 us
  waiting for transfers between devices  148 us (26%)
  matrix products  114 us (20%)
  other arithmetic  86.4 us (15%)
  local copies, waits for them, and re-layouts  82.4 us (14%)
  Pallas kernels  79.6 us (14%)
  blocking collectives  28.4 us (5%)
  between operations  21.1 us (4%)
    all_to_all x1, waiting for transfers between devices, sum_by_exchange(): received = lax.all_to_all(packed, ('fsdp', 'dp'), 0, 0, tiled=True)  77.3 us
    dot_general x4, matrix products, matmul(): return jnp.dot(left, right, preferred_element_type=jnp.float32)  57.8 us
    all_gather x1, waiting for transfers between devices, gather_with_small(): whole = lax.all_gather(joined, ('fsdp', 'dp'), axis=0, tiled=True)  55.8 us
    pallas_call x1, Pallas kernels, attention_backward(): pl.pallas_call(attention_backward_kernel, grid=(width // pair,), in_specs...  46.6 us
    pallas_call x1, Pallas kernels, attention_forward(): pl.pallas_call(attention_forward_kernel, grid=(width // pair,), in_specs=...  33 us
    dot_general x4, matrix products, matmul_right_t(): lax.dot_general(left, right, (((1,), (1,)), ((), ())), preferred_element_...  31.5 us
    another operation x6, other arithmetic  29.7 us
    dot_general x4, matrix products, matmul_left_t(): lax.dot_general(left, right, (((0,), (0,)), ((), ())), preferred_element_...  24.8 us
  transfers between devices with their start and end apart: 6, of which 3 were waited for; matrix products, arithmetic and copies ran while one was open for 33% of the time, Pallas kernels for 14%

profile of v11, /device:TPU:0, one launch (start us, length us, event | category | flops | bytes accessed | tf_op | source)
XLA Modules:
  0.0 564.0 jit_solution(9902030876638287686)
XLA Ops:
  9.0 6.1 %concatenate.68 = bf16[1344]{0:T(1024)(128)(2,1)S(1)} concatenate(bf16[96]{0:T(256)(128)(2,1)} %param.22, bf16[96]{0:T(256)(128)(2,1)} %param.23, bf16[288]{0:T(512)(128)(2,1)} %param.25, bf16[96]{0:T(256)(128)(2,1)} %param.27, bf16[96]{0:T(256)(128)(2,1)} %param.28, bf16[96]{0:T(256)(128)(2,1)} %param.29, bf16[384]{0:T(512)(128)(2,1)} %param.31, bf16[96]{0:T(256)(128)(2,1)} %param.33, ...), dimensions={0} | concatenate | bytes 5376 | tf_op jit(solution)/shard_map/concatenate | solution.py:234
  27.4 55.8 %all-gather.5.cloned.1.call-done = bf16[768,3200]{1,0:T(8,128)(2,1)} async-done(((bf16[24,3200]{1,0:T(8,128)(2,1)}), bf16[768,3200]{1,0:T(8,128)(2,1)}) %all-gather.5.cloned.1.call-update) | async-done | bytes 4915216 | tf_op jit(solution)/shard_map/all_gather | solution.py:239
  85.2 6.3 %convolution_add_fusion = f32[1024,2304]{1,0:T(8,128)S(1)} fusion(f32[2304]{0:T(1024)S(1)} %reshape.913, bf16[768,3200]{1,0:T(8,128)(2,1)} %all-gather.5.cloned.1.call-done, bf16[1024,768]{0,1:T(8,128)(2,1)S(1)} %copy.87, f32[768]{0:T(1024)S(1)} %reshape.912, f32[768]{0:T(1024)S(1)} %reshape.911, f32[1024]{0:T(1024)S(1)} %add_rsqrt_fusion.1, ...), kind=kOutput, calls=%fused_computation.32 | convolution fusion | flops 3630956544 | bytes 14572544 | tf_op jit(solution)/shard_map/dot_general | solution.py:21
  103.2 10.8 %fusion.61 = (bf16[1024,12,32]{0,2,1:T(8,128)(2,1)S(1)}, bf16[1024,12,32]{0,2,1:T(8,128)(2,1)S(1)}, bf16[1024,12,32]{0,2,1:T(8,128)(2,1)S(1)}, bf16[1024,12,32]{0,2,1:T(8,128)(2,1)S(1)}) fusion(f32[1024,12,64]{0,2,1:T(8,128)} %bitcast.40, f32[12,32]{1,0:T(8,128)S(1)} %mul.346, f32[1024]{0:T(1024)S(1)} %get-tuple-element.165, f32[12,32]{1,0:T(8,128)S(1)} %mul.341, ...), kind=kLoop, calls=%fused_computation.174 | loop fusion | flops 7471104 | bytes 9448448 | tf_op jit(solution)/shard_map/convert.55
  121.4 33.0 %attention_forward.1 = (bf16[1024,768]{1,0:T(8,128)(2,1)}, f32[1024,768]{1,0:T(8,128)}) custom-call(bf16[1024,768]{1,0:T(8,128)(2,1)} %copy.90.q_ref, bf16[1024,768]{1,0:T(8,128)(2,1)} %copy.91.k_ref, bf16[1024,768]{1,0:T(8,128)(2,1)} %slice.421.v_ref, s32[1024,1]{1,0:T(8,128)} %copy.92.seg_r_ref, s32[1,1024]{1,0:T(1,128)} %bitcast.51), custom_call_target="tpu_custom_call" | custom-call | flops 3221225472 | bytes 9437184 | tf_op jit(solution)/shard_map/attention_forward/pallas_call | solution.py:179
  160.2 39.0 %fusion.3 = (bf16[1024,3072]{1,0:T(8,128)(2,1)}, f32[1024,3072]{1,0:T(8,128)}) fusion(f32[3072]{0:T(1024)S(1)} %reshape.917, bf16[768,3072]{1,0:T(8,128)(2,1)} %all-gather.7.cloned.1.call-done, f32[1024,768]{0,1:T(8,128)} %copy-done.5, f32[768]{0:T(1024)S(1)} %reshape.916, f32[768]{0:T(1024)S(1)} %reshape.915, f32[1024]{0:T(1024)S(1)} %add_rsqrt_fusion, ...), kind=kOutput, calls=%fused_computation.6 | convolution fusion | flops 5043388416 | bytes 26765312 | tf_op jit(solution)/shard_map/dot_general | solution.py:21
  199.2 14.9 %all-gather.9.cloned.1.call-done = bf16[3072,768]{1,0:T(8,128)(2,1)} async-done(((bf16[96,768]{1,0:T(8,128)(2,1)}), bf16[3072,768]{1,0:T(8,128)(2,1)}) %all-gather.9.cloned.1.call-update) | async-done | bytes 4718608 | tf_op jit(solution)/shard_map/all_gather | solution.py:252
  214.1 11.9 %fusion.72 = (bf16[3072]{0:T(1024)(128)(2,1)S(1)}, bf16[1024,3072]{1,0:T(8,128)(2,1)S(1)}) fusion(f32[1024,3072]{1,0:T(8,128)} %get-tuple-element.191, f32[3072]{0:T(1024)S(1)} %reshape.917, bf16[3072,768]{1,0:T(8,128)(2,1)} %all-gather.9.cloned.1.call-done, bf16[1024,768]{1,0:T(8,128)(2,1)S(1)} %copy-done.12), kind=kOutput, calls=%fused_computation.183 | convolution fusion | flops 4869583872 | bytes 25184256 | tf_op jit(solution)/shard_map/dot_general | solution.py:31
  226.0 7.2 %convolution_convert_fusion = bf16[768,3072]{1,0:T(8,128)(2,1)} fusion(bf16[1024,3072]{1,0:T(8,128)(2,1)S(1)} %get-tuple-element.187, f32[1024,768]{0,1:T(8,128)S(1)} %copy-done.6, f32[768]{0:T(1024)S(1)} %reshape.916, f32[768]{0:T(1024)S(1)} %reshape.915, f32[1024]{0:T(1024)S(1)} %add_rsqrt_fusion, f32[1024]{0:T(1024)S(1)} %broadcast_multiply_fusion.4), kind=kOutput, calls=%fused_computation.33 | convolution fusion | flops 4838129664 | bytes 14170112 | tf_op jit(solution)/shard_map/dot_general | solution.py:25
  233.1 6.7 %fusion.73 = (bf16[768]{0:T(1024)(128)(2,1)S(1)}, f32[1024,768]{1,0:T(8,128)}) fusion(bf16[1024,3072]{1,0:T(8,128)(2,1)S(1)} %get-tuple-element.187, bf16[768,3072]{1,0:T(8,128)(2,1)S(1)} %copy-done.37), kind=kOutput, calls=%fused_computation.184 | convolution fusion | flops 4832623616 | bytes 14157312 | tf_op jit(solution)/shard_map/dot_general | solution.py:31
  243.5 4.0 multiply_reduce_fusion
  253.5 9.8 %convolution_convert_fusion.1 = bf16[3072,768]{1,0:T(8,128)(2,1)} fusion(bf16[1024,3072]{1,0:T(8,128)(2,1)} %get-tuple-element.190, bf16[1024,768]{1,0:T(8,128)(2,1)S(1)} %copy-done.12), kind=kOutput, calls=%fused_computation.34 | convolution fusion | flops 4834197504 | bytes 12582912 | tf_op jit(solution)/shard_map/dot_general | solution.py:25
  263.2 8.5 %convert_element_type.314 = bf16[768,3072]{1,0:T(8,128)(2,1)} reshape(bf16[3072,768]{1,0:T(8,128)(2,1)} %convolution_convert_fusion.1) | data formatting | bytes 9437184 | tf_op jit(solution)/shard_map/convert_element_type | solution.py:396
  271.7 8.9 %fusion.17 = bf16[768,7040]{1,0:T(8,128)(2,1)} fusion(bf16[768,8]{1,0:T(8,128)(2,1)S(1)} %reshape.896, bf16[768,768]{1,0:T(8,128)(2,1)S(1)} %convolution_convert_fusion.4, bf16[768,3072]{1,0:T(8,128)(2,1)} %convolution_convert_fusion, bf16[768,3072]{1,0:T(8,128)(2,1)} %convert_element_type.314), kind=kLoop, calls=%fused_computation.28 | loop fusion | flops 54067200 | bytes 21442560 | tf_op jit(solution)/shard_map/concatenate | solution.py:268
  280.6 4.8 convolution_convert_fusion.3.d_ref
  285.5 46.6 %attention_backward.1 = (f32[1024,768]{1,0:T(8,128)}, f32[1024,768]{1,0:T(8,128)}, f32[1024,768]{1,0:T(8,128)}) custom-call(bf16[1024,768]{1,0:T(8,128)(2,1)} %copy.90.q_ref, bf16[1024,768]{1,0:T(8,128)(2,1)} %copy.91.k_ref, bf16[1024,768]{1,0:T(8,128)(2,1)} %slice.421.v_ref, bf16[1024,768]{1,0:T(8,128)(2,1)} %convolution_convert_fusion.3.d_ref, ...), custom_call_target="tpu_custom_call" | custom-call | flops 6442450944 | bytes 18874368 | tf_op jit(solution)/shard_map/attention_backward/pallas_call | solution.py:200
  339.3 13.5 %subtract_convert_fusion.1 = (bf16[1024,12,32]{0,2,1:T(8,128)(2,1)S(1)}, f32[1024,12,32]{0,2,1:T(8,128)S(1)}, bf16[1024,12,32]{0,2,1:T(8,128)(2,1)S(1)}, bf16[1024,12,32]{0,2,1:T(8,128)(2,1)}) fusion(f32[1024,12,64]{0,2,1:T(8,128)} %bitcast.42, f32[12,32]{1,0:T(8,128)S(1)} %copy-done.20, f32[1024]{0:T(1024)S(1)} %copy-done.26, f32[12,32]{1,0:T(8,128)S(1)} %copy-done.18, ...), kind=kLoop, calls=%fused_computation.81 | loop fusion | flops 13762560 | bytes 16526336 | tf_op jit(solution)/shard_map/convert.39
  352.8 6.4 %multiply_reduce_fusion.6 = (bf16[12,32]{1,0:T(8,128)(2,1)S(1)}, bf16[12,32]{1,0:T(8,128)(2,1)S(1)}, bf16[1024,12,32]{0,2,1:T(8,128)(2,1)S(1)}) fusion(f32[1024,12,32]{0,2,1:T(8,128)S(1)} %get-tuple-element.146, f32[1024]{0:T(1024)S(1)} %copy-done.24, f32[1024]{0:T(1024)S(1)} %copy-done.26, f32[1024,12,64]{0,2,1:T(8,128)S(1)} %bitcast.43, ...), kind=kLoop, calls=%fused_computation.76 | loop fusion | flops 4717824 | bytes 5517824 | tf_op jit(solution)/shard_map/reduce_sum | solution.py:444
  370.4 8.1 %fusion.74 = (bf16[768]{0:T(1024)(128)(2,1)S(1)}, f32[1024,768]{1,0:T(8,128)}) fusion(bf16[768,3200]{1,0:T(8,128)(2,1)} %all-gather.5.cloned.1.call-done, bf16[1024,768]{1,0:T(8,128)(2,1)S(1)} %convert.113, bf16[1024,768]{1,0:T(8,128)(2,1)S(1)} %copy-done.14, bf16[1024,768]{1,0:T(8,128)(2,1)S(1)} %copy.103), kind=kOutput, calls=%fused_computation.185 | convolution fusion | flops 3638820096 | bytes 11404800 | tf_op jit(solution)/shard_map/dot_general | solution.py:31
  388.7 6.4 %convolution_convert_fusion.2 = bf16[768,2304]{1,0:T(8,128)(2,1)S(1)} fusion(bf16[1024,768]{0,1:T(8,128)(2,1)S(1)} %copy-done.3, f32[768]{0:T(1024)S(1)} %copy-done.35, f32[768]{0:T(1024)S(1)} %copy-done.30, f32[1024]{0:T(1024)S(1)} %copy-done.28, f32[1024]{0:T(1024)S(1)} %copy-done.22, bf16[1024,768]{1,0:T(8,128)(2,1)} %copy-done.15, ...), kind=kOutput, calls=%fused_computation.35 | convolution fusion | flops 3644522496 | bytes 9844736 | tf_op jit(solution)/shard_map/dot_general | solution.py:25
  408.6 9.1 %add_convert_fusion = bf16[1024,768]{0,1:T(8,128)(2,1)S(1)} fusion(f32[1024,768]{0,1:T(8,128)} %copy-done.5, bf16[1024,3072]{1,0:T(8,128)(2,1)} %get-tuple-element.190, bf16[3072,768]{1,0:T(8,128)(2,1)} %all-gather.9.cloned.1.call-done, f32[768]{0:T(1024)S(1)} %reshape.918), kind=kOutput, calls=%fused_computation.61 | convolution fusion | flops 4834197504 | bytes 15731712 | tf_op jit(solution)/shard_map/dot_general | solution.py:21
  419.2 77.3 %all-to-all-done = bf16[32,24,2432]{2,1,0:T(8,128)(2,1)} async-done(((bf16[32,24,2432]{2,1,0:T(8,128)(2,1)}), bf16[32,24,2432]{2,1,0:T(8,128)(2,1)}, u32[]{:S(2)}, u32[]{:S(2)}) %all-to-all-start) | async-done | bytes 3735584 | tf_op jit(solution)/shard_map/all_to_all | solution.py:306
  511.1 9.3 %all_gather.18 = bf16[96,2560]{1,0:T(8,128)(2,1)S(1)} all-gather(bf16[24,2560]{1,0:T(8,128)(2,1)S(1)} %pad_maximum_fusion.5), channel_id=1, replica_groups=mesh['fsdp'=8,'dp'=4] {'dp'}, dimensions={0}, use_global_device_ids=true | all-gather | bytes 614400 | tf_op jit(solution)/shard_map/all_gather | solution.py:314
  521.1 19.0 %all-reduce.5 = (f32[]{:T(128)}, f32[]{:T(128)}) all-reduce(f32[]{:T(128)} %bitcast.20, f32[]{:T(128)} %bitcast.21), channel_id=1, replica_groups=mesh['fsdp'=8,'dp'=4] {'fsdp'}, use_global_device_ids=true, to_apply=%region_31.32 | all-reduce | flops 2 | bytes 16 | tf_op jit(solution)/shard_map/psum | solution.py:476
  (215 shorter events, 119.5 us)
Async XLA Ops:
  7.2 8.9 %copy-start = (bf16[96,3072]{1,0:T(8,128)(2,1)S(1)}, bf16[96,3072]{1,0:T(8,128)(2,1)}, u32[]{:S(2)}) copy-start(bf16[96,3072]{1,0:T(8,128)(2,1)} %param.30) | copy-start | bytes 1769476
  7.2 75.9 %all-gather.5.cloned.1.call-start = ((), (), s32[]{:S(2)}) async-start(), calls=%async_computation.2 | async-start | bytes 5068800 | tf_op jit(solution)/shard_map/all_gather | solution.py:239
  16.0 144.2 %all-gather.7.cloned.1.call-start = ((), (), s32[]{:S(2)}) async-start(), calls=%async_computation.3 | async-start | bytes 4866048 | tf_op jit(solution)/shard_map/all_gather | solution.py:252
  16.8 197.3 %all-gather.9.cloned.1.call-start = ((), (), s32[]{:S(2)}) async-start(), calls=%async_computation.4 | async-start | bytes 4866048 | tf_op jit(solution)/shard_map/all_gather | solution.py:252
  18.5 483.9 %reduce-scatter.4.cloned.1.call-start = ((), (), s32[]{:S(2)}) async-start(), calls=%async_computation.6 | async-start | bytes 11151360
  20.2 134.2 %copy-start.2 = (bf16[1024,768]{0,1:T(8,128)(2,1)}, bf16[1024,768]{0,1:T(8,128)(2,1)S(1)}, u32[]{:S(2)}) copy-start(bf16[1024,768]{0,1:T(8,128)(2,1)S(1)} %copy.87) | copy-start | bytes 4718596
  20.5 64.7 %copy-start.21 = (f32[1024]{0:T(1024)}, f32[1024]{0:T(1024)S(1)}, u32[]{:S(2)}) copy-start(f32[1024]{0:T(1024)S(1)} %broadcast_multiply_fusion.5) | copy-start | bytes 12292
  21.0 70.5 %copy-start.27 = (f32[1024]{0:T(1024)}, f32[1024]{0:T(1024)S(1)}, u32[]{:S(2)}) copy-start(f32[1024]{0:T(1024)S(1)} %add_rsqrt_fusion.1) | copy-start | bytes 12292
  21.4 70.2 %copy-start.32 = (s32[1024]{0:T(1024)}, s32[1024]{0:T(1024)S(1)}, u32[]{:S(2)}) copy-start(s32[1024]{0:T(1024)S(1)} %get-tuple-element.167) | copy-start | bytes 12292
  21.4 81.8 %copy-start.23 = (f32[1024]{0:T(1024)}, f32[1024]{0:T(1024)S(1)}, u32[]{:S(2)}) copy-start(f32[1024]{0:T(1024)S(1)} %get-tuple-element.164) | copy-start | bytes 12292
  21.4 81.8 %copy-start.25 = (f32[1024]{0:T(1024)}, f32[1024]{0:T(1024)S(1)}, u32[]{:S(2)}) copy-start(f32[1024]{0:T(1024)S(1)} %get-tuple-element.165) | copy-start | bytes 12292
  85.1 6.5 %copy-start.29 = (f32[768]{0:T(1024)}, f32[768]{0:T(1024)S(1)}, u32[]{:S(2)}) copy-start(f32[768]{0:T(1024)S(1)} %reshape.911) | copy-start | bytes 9220
  85.2 6.4 %copy-start.34 = (f32[768]{0:T(1024)}, f32[768]{0:T(1024)S(1)}, u32[]{:S(2)}) copy-start(f32[768]{0:T(1024)S(1)} %reshape.912) | copy-start | bytes 9220
  103.1 10.9 %copy-start.17 = (f32[12,32]{1,0:T(8,128)}, f32[12,32]{1,0:T(8,128)S(1)}, u32[]{:S(2)}) copy-start(f32[12,32]{1,0:T(8,128)S(1)} %mul.341) | copy-start | bytes 4612
  103.2 10.8 %copy-start.19 = (f32[12,32]{1,0:T(8,128)}, f32[12,32]{1,0:T(8,128)S(1)}, u32[]{:S(2)}) copy-start(f32[12,32]{1,0:T(8,128)S(1)} %mul.346) | copy-start | bytes 4612
  160.1 53.9 %copy-start.12 = (bf16[1024,768]{1,0:T(8,128)(2,1)S(1)}, bf16[1024,768]{1,0:T(8,128)(2,1)}, u32[]{:S(2)}) copy-start(bf16[1024,768]{1,0:T(8,128)(2,1)} %param.35) | copy-start | bytes 4718596
  214.1 11.9 %copy-start.6 = (f32[1024,768]{0,1:T(8,128)S(1)}, f32[1024,768]{0,1:T(8,128)}, u32[]{:S(2)}) copy-start(f32[1024,768]{0,1:T(8,128)} %copy-done.5) | copy-start | bytes 9437188
  225.9 7.2 %copy-start.37 = (bf16[768,3072]{1,0:T(8,128)(2,1)S(1)}, bf16[768,3072]{1,0:T(8,128)(2,1)}, u32[]{:S(2)}) copy-start(bf16[768,3072]{1,0:T(8,128)(2,1)} %all-gather.7.cloned.1.call-done) | copy-start | bytes 14155780
  339.3 13.5 %copy-start.4 = (f32[1024,768]{0,1:T(8,128)S(1)}, f32[1024,768]{0,1:T(8,128)}, u32[]{:S(2)}) copy-start(f32[1024,768]{0,1:T(8,128)} %copy.101) | copy-start | bytes 9437188
  362.2 8.0 %copy-start.13 = (bf16[1024,768]{1,0:T(8,128)(2,1)}, bf16[1024,768]{1,0:T(8,128)(2,1)S(1)}, u32[]{:S(2)}) copy-start(bf16[1024,768]{1,0:T(8,128)(2,1)S(1)} %copy.103) | copy-start | bytes 4718596
  370.4 8.1 %copy-start.15 = (bf16[1024,768]{1,0:T(8,128)(2,1)}, bf16[1024,768]{1,0:T(8,128)(2,1)S(1)}, u32[]{:S(2)}) copy-start(bf16[1024,768]{1,0:T(8,128)(2,1)S(1)} %convert.113) | copy-start | bytes 4718596
  401.7 94.8 %all-to-all-start = ((bf16[32,24,2432]{2,1,0:T(8,128)(2,1)}), bf16[32,24,2432]{2,1,0:T(8,128)(2,1)}, u32[]{:S(2)}, u32[]{:S(2)}) async-start(bf16[32,24,2432]{2,1,0:T(8,128)(2,1)} %bitcast.44), calls=%async_computation | async-start | bytes 7471104 | tf_op jit(solution)/shard_map/all_to_all | solution.py:306
  405.4 139.8 %all-gather.11.cloned.1.call-start = ((), (), s32[]{:S(2)}) async-start(), calls=%async_computation.5 | async-start | bytes 1689600 | tf_op jit(solution)/shard_map/all_gather | solution.py:300
  546.1 8.7 %copy-start.1 = (bf16[96,3072]{1,0:T(8,128)(2,1)S(1)}, bf16[96,3072]{1,0:T(8,128)(2,1)}, u32[]{:S(2)}) copy-start(bf16[96,3072]{1,0:T(8,128)(2,1)} %param.30) | copy-start | bytes 1769476
  (22 other events, 72.6 us)
Sparse Core Ops, SparseCore 0:
  16.1 66.9 all-gather.4
  86.6 61.9 all-gather.6
  152.1 61.9 all-gather.8
  285.6 147.0 reduce-scatter.3
  507.0 18.9 all-gather.10
